TPU v7x, 32 devices: a whole 2x2x4 slice. The times are simulated.
32 devices in a mesh: groups: 2 (over y), seq: 4 (over z), head: 2 (over x), sub: 2 (over core).
Axes of the slice: x: 2, y: 2, z: 4, core: 2. Of those that a mesh axis runs over, the one named last changes fastest.
Arguments:
- activations: bfloat16 [16384, 1024], P(('groups', 'seq', 'sub')), parts along dimension 0, may hold values from -21 to 21
- w_query: bfloat16 [1024, 1024], P(None, 'head'), may hold values from -0.1875 to 0.1875
- w_key: bfloat16 [1024, 1024], P(None, 'head'), may hold values from -0.1875 to 0.1875
- w_value: bfloat16 [1024, 1024], P(None, 'head'), may hold values from -0.1875 to 0.1875
- w_out: bfloat16 [1024, 1024], P('head'), may hold values from -0.1875 to 0.1875
- tile_lists: int32 [128, 8], P('groups'), parts along dimension 0, may hold values from 0 to 63, as said below
- query_block_counts: int32 [128], P('groups'), parts along dimension 0, may hold values from 4 to 8, as said below
Outputs:
- mixed: bfloat16 [16384, 1024], P(('groups', 'seq', 'sub'), 'head'), parts along dimension 0
There are 2 independent parts, one for each index of `groups`. A program takes and returns all parts, laid end to end along the dimension named above; an argument that names none is the same for every part. Nothing has to cross between parts.
Inputs may be any that keep to these rules, and one draw needn't show every extreme that they name: `tile_lists`: each row lists 8 different key tiles; only its first query_block_counts entries are used. Take the aligned blocks of 8 rows (one device's query blocks) and of 8 tiles (one device's key tiles): the used entries of one block of rows name exactly 4 different tiles of every block of tiles. `query_block_counts`: the last row of each aligned block of 8 rows is 8.
All inputs are finite; a program needn't handle non-finite values.
Results may differ from a plain program's by a relative error of at most 0.019.
The roundings to bfloat16 on the way count: a program that leaves them out, or rounds other values in their place, can miss the bound.
Values may be sent and summed in bfloat16 or wider, within the bound.
No kernel may reach another device: no remote copies, remote signals or barrier semaphores. Data moves between devices by JAX's collectives and lax.ppermute only.
A program may use at most 128 MiB of HBM per device.

v0:
```python
import jax
import jax.numpy as jnp
from jax import lax
from jax.sharding import PartitionSpec as P

HS = 128
TILE = 128
BALANCING_ROUNDS = 3


COLUMN_FLOOR = 0.1


def body(activations, w_query, w_key, w_value, w_out, tile_lists, query_block_counts):
    seq_devices = lax.axis_size(("seq", "sub"))
    device_index = lax.axis_index(("seq", "sub"))
    block_total = tile_lists.shape[0]
    maximum_tiles = tile_lists.shape[1]
    row_count = activations.shape[0]
    local_blocks = row_count // TILE
    heads_here = w_query.shape[1] // HS
    capacity = local_blocks * (maximum_tiles // 2) // seq_devices
    query_rows = jnp.dot(activations, w_query, preferred_element_type=jnp.float32).astype(
        jnp.bfloat16
    )
    key_proj = jnp.dot(activations, w_key, preferred_element_type=jnp.float32).astype(jnp.bfloat16)
    values = jnp.dot(activations, w_value, preferred_element_type=jnp.float32).astype(jnp.bfloat16)
    payload = jnp.concatenate([key_proj, values], axis=1).reshape(
        local_blocks, TILE, 2 * heads_here * HS
    )
    all_valid = jnp.arange(maximum_tiles, dtype=jnp.int32)[None, :] < query_block_counts[:, None]
    owned_ids = device_index * local_blocks + jnp.arange(local_blocks, dtype=jnp.int32)
    wanted = jnp.any(
        (tile_lists[:, :, None] == owned_ids[None, None, :]) & all_valid[:, :, None], axis=1
    )
    wanted = jnp.any(wanted.reshape(seq_devices, local_blocks, local_blocks), axis=1).astype(
        jnp.int32
    )
    slot_ranks = jnp.cumsum(wanted, axis=1) - wanted
    selector = (slot_ranks[:, None, :] == jnp.arange(capacity, dtype=jnp.int32)[None, :, None]) & (
        wanted[:, None, :] > 0
    )
    outgoing = jnp.einsum(
        "dcj,jrf->dcrf", selector.astype(jnp.bfloat16), payload, preferred_element_type=jnp.float32
    ).astype(jnp.bfloat16)
    my_lists = lax.dynamic_slice_in_dim(tile_lists, device_index * local_blocks, local_blocks, 0)
    my_valid = lax.dynamic_slice_in_dim(all_valid, device_index * local_blocks, local_blocks, 0)
    tile_ids = jnp.arange(block_total, dtype=jnp.int32)
    matches = (my_lists[:, :, None] == tile_ids[None, None, :]) & my_valid[:, :, None]
    requested = jnp.any(matches, axis=(0, 1)).astype(jnp.int32).reshape(seq_devices, local_blocks)
    own_ranks = jnp.cumsum(requested, axis=1) - requested
    slot_table = (jnp.arange(seq_devices, dtype=jnp.int32)[:, None] * capacity + own_ranks).reshape(
        -1
    )
    slot_index = jnp.sum(jnp.where(matches, slot_table[None, None, :], 0), axis=2)
    arrived = lax.all_to_all(outgoing, ("seq", "sub"), split_axis=0, concat_axis=0, tiled=True)
    arrived = arrived.reshape(seq_devices * capacity, TILE, 2 * heads_here * HS)
    slot_tiles = jnp.take(arrived, slot_index.reshape(-1), axis=0)
    slot_tiles = slot_tiles.reshape(local_blocks, maximum_tiles, TILE, 2, heads_here, HS)
    key_slots = slot_tiles[:, :, :, 0]
    value_slots = slot_tiles[:, :, :, 1]
    query_blocks = query_rows.reshape(local_blocks, TILE, heads_here, HS)
    scores = jnp.einsum(
        "bihd,bmjhd->hbimj", query_blocks, key_slots, preferred_element_type=jnp.float32
    ) * HS ** (-0.5)
    valid_mask = my_valid[None, :, None, :, None]
    row_max = jnp.max(jnp.where(valid_mask, scores, -1e30), axis=(3, 4), keepdims=True)
    weights = jnp.where(valid_mask, jnp.exp(scores - row_max), 0.0)
    onehot = matches.astype(jnp.float32)
    selector_float = selector.astype(jnp.float32)
    for round_number in range(BALANCING_ROUNDS):
        weights = weights / jnp.sum(weights, axis=(3, 4), keepdims=True)
        partial_cols = jnp.sum(weights, axis=2)
        column_complete = jnp.einsum(
            "bmt,hbmj->htj", onehot, partial_cols, precision=lax.Precision.HIGHEST
        )
        owned_sums = lax.psum_scatter(
            column_complete.astype(jnp.bfloat16), ("seq", "sub"), scatter_dimension=1, tiled=True
        ).astype(jnp.float32)
        going_back = jnp.einsum(
            "dcj,hjr->dchr", selector_float, owned_sums, precision=lax.Precision.HIGHEST
        )
        returned = lax.all_to_all(
            going_back, ("seq", "sub"), split_axis=0, concat_axis=0, tiled=True
        )
        returned = returned.reshape(seq_devices * capacity, heads_here, TILE)
        per_slot = jnp.take(returned, slot_index.reshape(-1), axis=0)
        per_slot = per_slot.reshape(local_blocks, maximum_tiles, heads_here, TILE).transpose(
            2, 0, 1, 3
        )
        per_slot = jnp.where(my_valid[None, :, :, None], per_slot, 0.0)
        weights = weights / jnp.maximum(per_slot[:, :, None, :, :], COLUMN_FLOOR)
    probabilities = weights.astype(jnp.bfloat16)
    attended = jnp.einsum(
        "hbimj,bmjhd->bihd", probabilities, value_slots, preferred_element_type=jnp.float32
    )
    attended = attended.astype(jnp.bfloat16).reshape(row_count, heads_here * HS)
    partial_out = jnp.dot(attended, w_out, preferred_element_type=jnp.float32)
    return lax.psum_scatter(
        partial_out.astype(jnp.bfloat16), "head", scatter_dimension=1, tiled=True
    )


def solution(mesh):
    placed = (
        P(("groups", "seq", "sub"), None),
        P(None, "head"),
        P(None, "head"),
        P(None, "head"),
        P("head", None),
        P("groups", None),
        P("groups"),
    )
    return jax.shard_map(
        body,
        mesh=mesh,
        in_specs=placed,
        out_specs=P(("groups", "seq", "sub"), "head"),
        check_vma=False,
    )
```

profile of v0, /device:TPU:0, one launch (start us, length us, event | category | flops | bytes accessed | tf_op | source)
XLA Modules:
  0.0 545.1 jit_solution(10447828296143462744)
XLA Ops:
  6.5 0.9 iota_compare_fusion
  7.5 0.8 and_reduce_fusion
  8.6 2.5 convolution_convert_fusion.4
  11.1 2.5 convolution_convert_fusion.3
  13.8 2.0 copy.100
  15.8 4.6 copy.58
  20.4 7.1 %convolution_convert_fusion = bf16[8,4,128,1024]{3,0,2,1:T(8,128)(2,1)} fusion(bf16[8,128,1024]{2,0,1:T(8,128)(2,1)} %copy.58, s32[8,8]{1,0:T(8,128)S(1)} %convert_subtract_fusion, pred[8,8]{1,0:T(8,128)(4,1)S(1)} %get-tuple-element.6), kind=kOutput, calls=%fused_computation.28 | convolution fusion | flops 71303680 | bytes 10486080 | tf_op jit(solution)/shard_map/dcj,jrf->dcrf/dot_general | solution.py:43
  27.5 11.3 %copy.59 = bf16[8,4,128,1024]{3,2,1,0:T(8,128)(2,1)} copy(bf16[8,4,128,1024]{3,0,2,1:T(8,128)(2,1)} %convolution_convert_fusion) | data formatting | bytes 16777216 | tf_op jit(solution)/shard_map/convert_element_type | solution.py:45
  38.8 6.3 %all-to-all-start = ((bf16[8,4,128,1024]{3,2,1,0:T(8,128)(2,1)}), bf16[8,4,128,1024]{3,2,1,0:T(8,128)(2,1)}, u32[]{:S(2)}, u32[]{:S(2)}) async-start(bf16[8,4,128,1024]{3,2,1,0:T(8,128)(2,1)} %copy.59), calls=%async_computation | async-start | bytes 16777216 | tf_op jit(solution)/shard_map/all_to_all | solution.py:56
  46.1 0.3 select_reduce_fusion.1
  46.6 2.5 convolution_convert_fusion.2
  49.4 179.7 %all-to-all-done = bf16[8,4,128,1024]{3,2,1,0:T(8,128)(2,1)} async-done(((bf16[8,4,128,1024]{3,2,1,0:T(8,128)(2,1)}), bf16[8,4,128,1024]{3,2,1,0:T(8,128)(2,1)}, u32[]{:S(2)}, u32[]{:S(2)}) %all-to-all-start) | async-done | bytes 8388640 | tf_op jit(solution)/shard_map/all_to_all | solution.py:56
  229.1 10.8 %gather_fusion = bf16[64,128,1024]{2,1,0:T(8,128)(2,1)} fusion(bf16[32,128,1024]{2,1,0:T(8,128)(2,1)} %bitcast.4, s32[1024]{0:T(1024)S(1)} %pad_clamp_fusion.1), kind=kCustom, calls=%fused_computation.3 | custom fusion | bytes 33554688 | tf_op jit(solution)/shard_map/jit(_take)/gather | solution.py:58
  240.0 22.4 %copy.60 = bf16[64,128,1024]{1,2,0:T(8,128)(2,1)} copy(bf16[64,128,1024]{2,1,0:T(8,128)(2,1)} %gather_fusion) | data formatting | bytes 33554432 | tf_op jit(solution)/shard_map/jit(_take)/gather | solution.py:58
  262.4 21.6 %copy.61 = bf16[8,8,128,2,4,128]{5,2,1,0,4,3:T(8,128)(2,1)} copy(bf16[8,8,128,2,4,128]{2,5,4,3,1,0:T(8,128)(2,1)} %bitcast.134) | data formatting | bytes 33554432 | tf_op jit(solution)/shard_map/jit(_take)/gather | solution.py:58
  284.0 14.2 %broadcast_select_fusion = bf16[8,8,128,2,4,128]{5,2,1,0,4,3:T(8,128)(2,1)} fusion(bf16[8,8,128,2,4,128]{5,2,1,0,4,3:T(8,128)(2,1)} %copy.61, pred[8,8]{1,0:T(8,128)(4,1)S(1)} %compare_and_fusion), kind=kLoop, calls=%fused_computation.21 | loop fusion | flops 8388608 | bytes 33554496 | tf_op jit(solution)/shard_map/jit(_take)/select_n | solution.py:58
  298.2 5.1 select_reduce_fusion
  303.3 3.5 fusion.63
  306.8 4.9 divide_reduce_fusion
  311.7 0.3 fusion.31
  312.1 0.6 copy.157
  312.8 29.7 %reduce-scatter.13.cloned.1.call-done = bf16[8,512]{1,0:T(8,128)(2,1)} async-done(((bf16[64,512]{1,0:T(8,128)(2,1)}), bf16[8,512]{1,0:T(8,128)(2,1)}) %reduce-scatter.13.cloned.1.call-update) | async-done | bytes 8208
  342.5 0.7 reshape.229
  343.3 0.6 copy.63
  343.9 3.4 all-to-all-start.1
  347.4 5.8 %all-to-all-done.1 = f32[8,4,4,128]{3,2,1,0:T(4,128)S(1)} async-done(((f32[8,4,4,128]{3,2,1,0:T(4,128)}), f32[8,4,4,128]{3,2,1,0:T(4,128)S(1)}, u32[]{:S(2)}, u32[]{:S(2)}) %all-to-all-start.1) | async-done | bytes 65568 | tf_op jit(solution)/shard_map/all_to_all | solution.py:83
  353.2 0.7 gather_fusion.1
  354.0 8.6 %fusion.8 = f32[4,8,128]{2,1,0:T(8,128)S(1)} fusion(f32[4,8,8,128]{3,2,1,0:T(8,128)S(1)} %fusion.40, f32[4,8,128]{2,1,0:T(8,128)S(1)} %fusion.63, f32[4,8,128]{2,1,0:T(8,128)S(1)} %get-tuple-element.8, f32[4,8,128,8,128]{2,4,3,1,0:T(8,128)} %copy-done.2, pred[8,8]{1,0:T(8,128)(4,1)S(1)} %constant_dynamic-slice_fusion), kind=kLoop, calls=%fused_computation.17 | loop fusion | flops 25161728 | bytes 16957504 | tf_op jit(solution)/shard_map/reduce_sum | solution.py:72
  362.7 1.9 copy-done.3
  364.5 11.3 %fusion.9 = f32[4,8,8,128]{3,2,1,0:T(8,128)S(1)} fusion(f32[4,8,128]{2,1,0:T(8,128)S(1)} %fusion.8, f32[4,8,8,128]{3,2,1,0:T(8,128)S(1)} %fusion.40, f32[4,8,128]{2,1,0:T(8,128)S(1)} %fusion.63, f32[4,8,128]{2,1,0:T(8,128)S(1)} %get-tuple-element.8, f32[4,8,128,8,128]{2,4,3,1,0:T(8,128)S(1)} %copy-done.3, pred[8,8]{1,0:T(8,128)(4,1)S(1)} %constant_dynamic-slice_fusion), kind=kLoop, calls=%fused_computation.18 | loop fusion | flops 29327360 | bytes 17088576 | tf_op jit(solution)/shard_map/reduce_sum | solution.py:73
  375.9 0.3 fusion.30
  376.3 0.6 copy.156
  377.0 28.9 %reduce-scatter.15.cloned.1.call-done = bf16[8,512]{1,0:T(8,128)(2,1)} async-done(((bf16[64,512]{1,0:T(8,128)(2,1)}), bf16[8,512]{1,0:T(8,128)(2,1)}) %reduce-scatter.15.cloned.1.call-update) | async-done | bytes 8208
  405.9 0.7 reshape.231
  406.7 8.3 %all_to_all.20 = f32[8,4,4,128]{3,2,1,0:T(4,128)S(1)} all-to-all(f32[8,4,4,128]{3,2,1,0:T(4,128)S(1)} %copy.67), channel_id=1, replica_groups=mesh['groups'=2,'seq'=4,'head'=2,'sub'=2] {'seq','sub'}, dimensions={0} | all-to-all | bytes 131072 | tf_op jit(solution)/shard_map/all_to_all | solution.py:83
  415.0 0.7 gather_fusion.2
  415.9 11.8 %fusion.10 = f32[4,8,128]{2,1,0:T(8,128)S(1)} fusion(f32[4,8,8,128]{3,2,1,0:T(8,128)S(1)} %fusion.38, f32[4,8,128]{2,1,0:T(8,128)S(1)} %fusion.8, f32[4,8,8,128]{3,2,1,0:T(8,128)S(1)} %fusion.40, f32[4,8,128]{2,1,0:T(8,128)S(1)} %fusion.63, f32[4,8,128]{2,1,0:T(8,128)S(1)} %get-tuple-element.8, f32[4,8,128,8,128]{2,4,3,1,0:T(8,128)} %copy-done.2, ...), kind=kLoop, calls=%fused_computation.19 | loop fusion | flops 33550336 | bytes 17104960 | tf_op jit(solution)/shard_map/reduce_sum | solution.py:72
  427.8 16.3 %fusion.11 = f32[4,8,8,128]{3,2,1,0:T(8,128)S(1)} fusion(f32[4,8,128]{2,1,0:T(8,128)S(1)} %fusion.10, f32[4,8,8,128]{3,2,1,0:T(8,128)S(1)} %fusion.38, f32[4,8,128]{2,1,0:T(8,128)S(1)} %fusion.8, f32[4,8,8,128]{3,2,1,0:T(8,128)S(1)} %fusion.40, f32[4,8,128]{2,1,0:T(8,128)S(1)} %fusion.63, f32[4,8,128]{2,1,0:T(8,128)S(1)} %get-tuple-element.8, ...), kind=kLoop, calls=%fused_computation.20 | loop fusion | flops 37715968 | bytes 17236032 | tf_op jit(solution)/shard_map/reduce_sum | solution.py:73
  444.1 0.3 fusion.29
  444.5 0.6 copy.155
  445.2 29.0 %reduce-scatter.17.cloned.1.call-done = bf16[8,512]{1,0:T(8,128)(2,1)} async-done(((bf16[64,512]{1,0:T(8,128)(2,1)}), bf16[8,512]{1,0:T(8,128)(2,1)}) %reduce-scatter.17.cloned.1.call-update) | async-done | bytes 8208
  474.2 0.7 reshape.233
  475.0 8.3 %all_to_all.21 = f32[8,4,4,128]{3,2,1,0:T(4,128)S(1)} all-to-all(f32[8,4,4,128]{3,2,1,0:T(4,128)S(1)} %copy.71), channel_id=1, replica_groups=mesh['groups'=2,'seq'=4,'head'=2,'sub'=2] {'seq','sub'}, dimensions={0} | all-to-all | bytes 131072 | tf_op jit(solution)/shard_map/all_to_all | solution.py:83
  483.3 0.7 gather_fusion.3
  484.3 20.4 %fusion.21 = bf16[8,128,4,128]{1,3,2,0:T(8,128)(2,1)S(1)} fusion(bf16[8,8,128,2,4,128]{5,2,1,0,4,3:T(8,128)(2,1)} %broadcast_select_fusion, f32[4,8,8,128]{3,2,1,0:T(8,128)S(1)} %fusion.36, f32[4,8,128]{2,1,0:T(8,128)S(1)} %fusion.10, f32[4,8,8,128]{3,2,1,0:T(8,128)S(1)} %fusion.38, f32[4,8,128]{2,1,0:T(8,128)S(1)} %fusion.8, ...), kind=kOutput, calls=%fused_computation.36 | convolution fusion | flops 1116209152 | bytes 26673216 | tf_op jit(solution)/shard_map/hbimj,bmjhd->bihd/dot_general | solution.py:94
  504.7 0.7 copy.77
  505.4 2.6 convolution_convert_fusion.1
  508.1 30.5 %reduce-scatter.11.cloned.1.call-done = bf16[1024,512]{1,0:T(8,128)(2,1)} async-done(((bf16[1024,1024]{1,0:T(8,128)(2,1)}), bf16[1024,512]{1,0:T(8,128)(2,1)}) %reduce-scatter.11.cloned.1.call-update) | async-done | bytes 1048592 | tf_op jit(solution)/shard_map/reduce_scatter | solution.py:99
  (62 shorter events, 3.4 us)
Async XLA Ops:
  6.5 2.1 copy-start
  27.5 18.0 %copy-start.4 = (s32[64,8]{0,1:T(8,128)S(1)}, s32[64,8]{0,1:T(8,128)}, u32[]{:S(2)}) copy-start(s32[64,8]{0,1:T(8,128)} %param.14) | copy-start | bytes 6148
  38.8 190.3 %all-to-all-start = ((bf16[8,4,128,1024]{3,2,1,0:T(8,128)(2,1)}), bf16[8,4,128,1024]{3,2,1,0:T(8,128)(2,1)}, u32[]{:S(2)}, u32[]{:S(2)}) async-start(bf16[8,4,128,1024]{3,2,1,0:T(8,128)(2,1)} %copy.59), calls=%async_computation | async-start | bytes 16777216 | tf_op jit(solution)/shard_map/all_to_all | solution.py:56
  45.2 297.3 %reduce-scatter.13.cloned.1.call-start = ((), (), s32[]{:S(2)}) async-start(), calls=%async_computation.9 | async-start | bytes 73728
  303.3 8.4 %copy-start.2 = (f32[4,8,128,8,128]{2,4,3,1,0:T(8,128)}, f32[4,8,128,8,128]{2,4,3,1,0:T(8,128)S(1)}, u32[]{:S(2)}) copy-start(f32[4,8,128,8,128]{2,4,3,1,0:T(8,128)S(1)} %get-tuple-element.9) | copy-start | bytes 50331652
  343.9 9.2 %all-to-all-start.1 = ((f32[8,4,4,128]{3,2,1,0:T(4,128)}), f32[8,4,4,128]{3,2,1,0:T(4,128)S(1)}, u32[]{:S(2)}, u32[]{:S(2)}) async-start(f32[8,4,4,128]{3,2,1,0:T(4,128)} %copy.63), calls=%async_computation.1 | async-start | bytes 131072 | tf_op jit(solution)/shard_map/all_to_all | solution.py:83
  347.3 58.6 %reduce-scatter.15.cloned.1.call-start = ((), (), s32[]{:S(2)}) async-start(), calls=%async_computation.10 | async-start | bytes 73728
  353.8 10.7 %copy-start.3 = (f32[4,8,128,8,128]{2,4,3,1,0:T(8,128)S(1)}, f32[4,8,128,8,128]{2,4,3,1,0:T(8,128)}, u32[]{:S(2)}) copy-start(f32[4,8,128,8,128]{2,4,3,1,0:T(8,128)} %copy-done.2) | copy-start | bytes 50331652
  376.9 97.3 %reduce-scatter.17.cloned.1.call-start = ((), (), s32[]{:S(2)}) async-start(), calls=%async_computation.11 | async-start | bytes 73728
  445.1 93.4 %reduce-scatter.11.cloned.1.call-start = ((), (), s32[]{:S(2)}) async-start(), calls=%async_computation.8 | async-start | bytes 3145728 | tf_op jit(solution)/shard_map/reduce_scatter | solution.py:99
  484.2 21.1 %copy-start.5 = (bf16[512,1024]{1,0:T(8,128)(2,1)S(1)}, bf16[512,1024]{1,0:T(8,128)(2,1)}, u32[]{:S(2)}) copy-start(bf16[512,1024]{1,0:T(8,128)(2,1)} %param.13) | copy-start | bytes 3145732
  484.2 54.3 %copy-start.1 = (bf16[1024,1024]{1,0:T(8,128)(2,1)S(1)}, bf16[1024,1024]{1,0:T(8,128)(2,1)}, u32[]{:S(2)}) copy-start(bf16[1024,1024]{1,0:T(8,128)(2,1)} %param.9) | copy-start | bytes 6291460
Sparse Core Ops, SparseCore 0:
  312.9 29.5 reduce-scatter.12
  377.0 28.8 reduce-scatter.14
  445.3 28.8 reduce-scatter.16
  508.2 30.3 reduce-scatter.10
where the time goes:
time: 547 us; the launch traced here: 545 us
  waiting for transfers between devices  304 us (56%)
  local copies, waits for them, and re-layouts  83.3 us (15%)
  other arithmetic  73.9 us (14%)
  matrix products  44.2 us (8%)
  blocking collectives  16.6 us (3%)
  between operations  13.5 us (2%)
  starting transfers between devices  10 us (2%)
    all_to_all x1, waiting for transfers between devices, body(): lax.all_to_all(outgoing, ('seq', 'sub'), split_axis=0, concat_axis=0, til...  180 us
    unnamed x7, waiting for transfers between devices  87.6 us
    gather x3, local copies, waits for them, and re-layouts, body(): slot_tiles = jnp.take(arrived, slot_index.reshape(-1), axis=0)  54.9 us
    reduce_sum x3, other arithmetic, body(): partial_cols = jnp.sum(weights, axis=2)  32.5 us
    reduce_scatter x1, waiting for transfers between devices, body(): lax.psum_scatter(partial_out.astype(jnp.bfloat16), 'head', scatter_dimens...  30.5 us
    reduce_sum x3, other arithmetic, body(): weights = weights / jnp.sum(weights, axis=(3, 4), keepdims=True)  23.9 us
    dot_general x1, matrix products, body(): jnp.einsum('hbimj,bmjhd->bihd', probabilities, value_slots, preferred_ele...  20.4 us
    all_to_all x2, blocking collectives, body(): lax.all_to_all(going_back, ('seq', 'sub'), split_axis=0, concat_axis=0, t...  16.6 us
  transfers between devices with their start and end apart: 6, of which 6 were waited for; matrix products, arithmetic and copies ran while one was open for 1% of the time, Pallas kernels for 0%

commit v1 on v0

--- a/solution.py
+++ b/solution.py
@@ -67,38 +67,41 @@
     row_max = jnp.max(jnp.where(valid_mask, scores, -1e30), axis=(3, 4), keepdims=True)
     weights = jnp.where(valid_mask, jnp.exp(scores - row_max), 0.0)
     onehot = matches.astype(jnp.float32)
-    selector_float = selector.astype(jnp.float32)
     for round_number in range(BALANCING_ROUNDS):
         weights = weights / jnp.sum(weights, axis=(3, 4), keepdims=True)
         partial_cols = jnp.sum(weights, axis=2)
         column_complete = jnp.einsum(
-            "bmt,hbmj->htj", onehot, partial_cols, precision=lax.Precision.HIGHEST
+            "bmt,hbmj->thj", onehot, partial_cols, precision=lax.Precision.HIGHEST
+        ).reshape(seq_devices, local_blocks, heads_here, TILE)
+        from_all = lax.all_to_all(
+            column_complete, ("seq", "sub"), split_axis=0, concat_axis=0, tiled=True
         )
-        owned_sums = lax.psum_scatter(
-            column_complete.astype(jnp.bfloat16), ("seq", "sub"), scatter_dimension=1, tiled=True
-        ).astype(jnp.float32)
-        going_back = jnp.einsum(
-            "dcj,hjr->dchr", selector_float, owned_sums, precision=lax.Precision.HIGHEST
-        )
-        returned = lax.all_to_all(
-            going_back, ("seq", "sub"), split_axis=0, concat_axis=0, tiled=True
-        )
-        returned = returned.reshape(seq_devices * capacity, heads_here, TILE)
-        per_slot = jnp.take(returned, slot_index.reshape(-1), axis=0)
-        per_slot = per_slot.reshape(local_blocks, maximum_tiles, heads_here, TILE).transpose(
-            2, 0, 1, 3
-        )
-        per_slot = jnp.where(my_valid[None, :, :, None], per_slot, 0.0)
+        owned_sums = jnp.sum(from_all, axis=0)
+        spread = jnp.broadcast_to(owned_sums[None], (seq_devices,) + owned_sums.shape)
+        totals = lax.all_to_all(
+            spread, ("seq", "sub"), split_axis=0, concat_axis=0, tiled=True
+        ).reshape(block_total, heads_here, TILE)
+        per_slot = jnp.einsum("bmt,thj->hbmj", onehot, totals, precision=lax.Precision.HIGHEST)
         weights = weights / jnp.maximum(per_slot[:, :, None, :, :], COLUMN_FLOOR)
     probabilities = weights.astype(jnp.bfloat16)
     attended = jnp.einsum(
         "hbimj,bmjhd->bihd", probabilities, value_slots, preferred_element_type=jnp.float32
     )
     attended = attended.astype(jnp.bfloat16).reshape(row_count, heads_here * HS)
-    partial_out = jnp.dot(attended, w_out, preferred_element_type=jnp.float32)
-    return lax.psum_scatter(
-        partial_out.astype(jnp.bfloat16), "head", scatter_dimension=1, tiled=True
-    )
+    head_count = lax.axis_size("head")
+    if head_count != 2:
+        partial_out = jnp.dot(attended, w_out, preferred_element_type=jnp.float32)
+        return lax.psum_scatter(
+            partial_out.astype(jnp.bfloat16), "head", scatter_dimension=1, tiled=True
+        )
+    head_index = lax.axis_index("head")
+    width = w_out.shape[1] // 2
+    other_cols = lax.dynamic_slice_in_dim(w_out, (1 - head_index) * width, width, 1)
+    my_cols = lax.dynamic_slice_in_dim(w_out, head_index * width, width, 1)
+    other_part = jnp.dot(attended, other_cols, preferred_element_type=jnp.float32)
+    received = lax.ppermute(other_part.astype(jnp.bfloat16), "head", perm=[(0, 1), (1, 0)])
+    my_part = jnp.dot(attended, my_cols, preferred_element_type=jnp.float32)
+    return (my_part + received.astype(jnp.float32)).astype(jnp.bfloat16)
 
 
 def solution(mesh):

time: 547 us -> 465 us (0.85)
  waiting for transfers between devices: 304 us -> 210 us
  blocking collectives: 16.6 us -> 46.6 us
  between operations: 13.5 us -> 0.33 us
  local copies, waits for them, and re-layouts: 83.3 us -> 75.3 us
    unnamed x7 -> x0, waiting for transfers between devices: 87.6 us -> none
    reduce_scatter x1 -> x0, waiting for transfers between devices: 30.5 us -> none  [body(): lax.psum_scatter(partial_out.astype(jnp.bfloat16), 'head', scatter_dimens...]
    all_to_all x2 -> x5, blocking collectives: 16.6 us -> 46.6 us  [the longest x3 27.7 us: body(): lax.all_to_all(column_complete, ('seq', 'sub'), split_axis=0, concat_axis...]
    ppermute x0 -> x1, waiting for transfers between devices: none -> 23.4 us  [body(): lax.ppermute(other_part.astype(jnp.bfloat16), 'head', perm=[(0, 1), (1, 0)])]
    unnamed x22 -> x13, local copies, waits for them, and re-layouts: 8.11 us -> 2.01 us
  transfers between devices with their start and end apart: 6 -> 3, of which waited for: 6 -> 3; matrix products, arithmetic and copies ran while one was open for 1% -> 1% of each run, Pallas kernels for 0% -> 0%
where the time goes in v1:
time: 465 us; the launch traced here: 463 us
  waiting for transfers between devices  210 us (45%)
  local copies, waits for them, and re-layouts  75.3 us (16%)
  other arithmetic  72.8 us (16%)
  matrix products  46.9 us (10%)
  blocking collectives  46.6 us (10%)
  starting transfers between devices  11.4 us (2%)
    all_to_all x1, waiting for transfers between devices, body(): lax.all_to_all(outgoing, ('seq', 'sub'), split_axis=0, concat_axis=0, til...  180 us
    gather x3, local copies, waits for them, and re-layouts, body(): slot_tiles = jnp.take(arrived, slot_index.reshape(-1), axis=0)  55 us
    reduce_sum x3, other arithmetic, body(): partial_cols = jnp.sum(weights, axis=2)  32.5 us
    all_to_all x3, blocking collectives, body(): lax.all_to_all(column_complete, ('seq', 'sub'), split_axis=0, concat_axis...  27.7 us
    ppermute x1, waiting for transfers between devices, body(): lax.ppermute(other_part.astype(jnp.bfloat16), 'head', perm=[(0, 1), (1, 0)])  23.4 us
    reduce_sum x3, other arithmetic, body(): weights = weights / jnp.sum(weights, axis=(3, 4), keepdims=True)  23.4 us
    dot_general x1, matrix products, body(): jnp.einsum('hbimj,bmjhd->bihd', probabilities, value_slots, preferred_ele...  20.4 us
    all_to_all x2, blocking collectives, body(): lax.all_to_all(spread, ('seq', 'sub'), split_axis=0, concat_axis=0, tiled...  18.9 us
  transfers between devices with their start and end apart: 3, of which 3 were waited for; matrix products, arithmetic and copies ran while one was open for 1% of the time, Pallas kernels for 0%

profile of v1, /device:TPU:0, one launch (start us, length us, event | category | flops | bytes accessed | tf_op | source)
XLA Modules:
  0.0 463.3 jit_solution(11576679925666854136)
XLA Ops:
  0.0 0.9 iota_compare_fusion
  1.0 0.8 and_reduce_fusion
  1.8 0.1 copy.80
  1.9 0.2 reduce_window_sum.21
  2.1 2.5 convolution_convert_fusion.2
  4.6 2.5 convolution_convert_fusion.3
  7.1 0.2 maximum_bitcast_fusion
  7.3 2.0 copy.85
  9.3 4.6 copy.56
  13.9 7.1 %convolution_convert_fusion = bf16[8,4,128,1024]{3,0,2,1:T(8,128)(2,1)} fusion(bf16[8,128,1024]{2,0,1:T(8,128)(2,1)} %copy.56, s32[8,8]{1,0:T(8,128)S(1)} %convert_subtract_fusion, pred[8,8]{1,0:T(8,128)(4,1)S(1)} %get-tuple-element.5), kind=kOutput, calls=%fused_computation.25 | convolution fusion | flops 71303680 | bytes 10486080 | tf_op jit(solution)/shard_map/dcj,jrf->dcrf/dot_general | solution.py:43
  21.0 11.3 %copy.57 = bf16[8,4,128,1024]{3,2,1,0:T(8,128)(2,1)} copy(bf16[8,4,128,1024]{3,0,2,1:T(8,128)(2,1)} %convolution_convert_fusion) | data formatting | bytes 16777216 | tf_op jit(solution)/shard_map/convert_element_type | solution.py:45
  32.3 6.4 %all-to-all-start = ((bf16[8,4,128,1024]{3,2,1,0:T(8,128)(2,1)}), bf16[8,4,128,1024]{3,2,1,0:T(8,128)(2,1)}, u32[]{:S(2)}, u32[]{:S(2)}) async-start(bf16[8,4,128,1024]{3,2,1,0:T(8,128)(2,1)} %copy.57), calls=%async_computation | async-start | bytes 16777216 | tf_op jit(solution)/shard_map/all_to_all | solution.py:56
  39.0 0.2 reduce_window_sum.19
  39.4 0.3 select_reduce_fusion.1
  39.8 2.5 convolution_convert_fusion.1
  42.3 0.3 reshape.156
  42.6 180.0 %all-to-all-done = bf16[8,4,128,1024]{3,2,1,0:T(8,128)(2,1)} async-done(((bf16[8,4,128,1024]{3,2,1,0:T(8,128)(2,1)}), bf16[8,4,128,1024]{3,2,1,0:T(8,128)(2,1)}, u32[]{:S(2)}, u32[]{:S(2)}) %all-to-all-start) | async-done | bytes 8388640 | tf_op jit(solution)/shard_map/all_to_all | solution.py:56
  222.6 10.9 %gather_fusion = bf16[64,128,1024]{2,1,0:T(8,128)(2,1)} fusion(bf16[32,128,1024]{2,1,0:T(8,128)(2,1)} %bitcast.4, s32[1024]{0:T(1024)S(1)} %pad_clamp_fusion), kind=kCustom, calls=%fused_computation | custom fusion | bytes 33554688 | tf_op jit(solution)/shard_map/jit(_take)/gather | solution.py:58
  233.6 22.4 %copy.58 = bf16[64,128,1024]{1,2,0:T(8,128)(2,1)} copy(bf16[64,128,1024]{2,1,0:T(8,128)(2,1)} %gather_fusion) | data formatting | bytes 33554432 | tf_op jit(solution)/shard_map/jit(_take)/gather | solution.py:58
  256.0 21.6 %copy.59 = bf16[8,8,128,2,4,128]{5,2,1,0,4,3:T(8,128)(2,1)} copy(bf16[8,8,128,2,4,128]{2,5,4,3,1,0:T(8,128)(2,1)} %bitcast.119) | data formatting | bytes 33554432 | tf_op jit(solution)/shard_map/jit(_take)/gather | solution.py:58
  277.6 14.2 %broadcast_select_fusion = bf16[8,8,128,2,4,128]{5,2,1,0,4,3:T(8,128)(2,1)} fusion(bf16[8,8,128,2,4,128]{5,2,1,0,4,3:T(8,128)(2,1)} %copy.59, pred[8,8]{1,0:T(8,128)(4,1)S(1)} %compare_and_fusion.4), kind=kLoop, calls=%fused_computation.18 | loop fusion | flops 8388608 | bytes 33554496 | tf_op jit(solution)/shard_map/jit(_take)/select_n | solution.py:58
  291.8 5.1 %select_reduce_fusion = (f32[4,8,128]{2,1,0:T(8,128)S(1)}, f32[4,8,128,8,128]{2,4,3,1,0:T(8,128)S(1)}) fusion(pred[8,8]{1,0:T(8,128)(4,1)S(1)} %constant_dynamic-slice_fusion, bf16[8,8,128,2,4,128]{5,2,1,0,4,3:T(8,128)(2,1)} %broadcast_select_fusion, bf16[8,128,4,128,1]{3,2,1,0,4:T(4,128)(2,1)S(1)} %bitcast.121), kind=kOutput, calls=%fused_computation.11 | convolution fusion | flops 1086320640 | bytes 26230848 | tf_op jit(solution)/shard_map/bihd,bmjhd->hbimj/dot_general | solution.py:63
  296.9 3.5 fusion.80
  300.4 4.9 %divide_reduce_fusion = f32[4,8,8,128]{3,2,1,0:T(8,128)S(1)} fusion(f32[4,8,128]{2,1,0:T(8,128)S(1)} %fusion.80, f32[4,8,128]{2,1,0:T(8,128)S(1)} %get-tuple-element.7, f32[4,8,128,8,128]{2,4,3,1,0:T(8,128)S(1)} %get-tuple-element.8, pred[8,8]{1,0:T(8,128)(4,1)S(1)} %constant_dynamic-slice_fusion), kind=kLoop, calls=%fused_computation.12 | loop fusion | flops 20938752 | bytes 16941120 | tf_op jit(solution)/shard_map/reduce_sum | solution.py:72
  305.3 0.4 convolution_bitcast_fusion.2
  305.7 9.1 %all_to_all.35 = f32[8,8,4,128]{3,1,2,0:T(8,128)S(1)} all-to-all(f32[8,8,4,128]{3,1,2,0:T(8,128)S(1)} %convolution_bitcast_fusion.2), channel_id=1, replica_groups=mesh['groups'=2,'seq'=4,'head'=2,'sub'=2] {'seq','sub'}, dimensions={0} | all-to-all | bytes 262144 | tf_op jit(solution)/shard_map/all_to_all | solution.py:76
  314.9 9.7 %all_to_all.36 = f32[8,8,4,128]{3,1,2,0:T(8,128)S(1)} all-to-all(f32[8,8,4,128]{3,1,2,0:T(8,128)S(1)} %broadcast_in_dim.53), channel_id=1, replica_groups=mesh['groups'=2,'seq'=4,'head'=2,'sub'=2] {'seq','sub'}, dimensions={0} | all-to-all | bytes 262144 | tf_op jit(solution)/shard_map/all_to_all | solution.py:81
  324.6 0.3 fusion.28
  324.8 8.2 %fusion.8 = f32[4,8,128]{2,1,0:T(8,128)S(1)} fusion(f32[4,8,8,128]{3,2,1,0:T(8,128)S(1)} %fusion.28, f32[4,8,128]{2,1,0:T(8,128)S(1)} %fusion.80, f32[4,8,128]{2,1,0:T(8,128)S(1)} %get-tuple-element.7, f32[4,8,128,8,128]{2,4,3,1,0:T(8,128)} %copy-done.2, pred[8,8]{1,0:T(8,128)(4,1)S(1)} %constant_dynamic-slice_fusion), kind=kLoop, calls=%fused_computation.14 | loop fusion | flops 25161728 | bytes 16957504 | tf_op jit(solution)/shard_map/reduce_sum | solution.py:71
  333.0 11.3 %fusion.9 = f32[4,8,8,128]{3,2,1,0:T(8,128)S(1)} fusion(f32[4,8,128]{2,1,0:T(8,128)S(1)} %fusion.8, f32[4,8,8,128]{3,2,1,0:T(8,128)S(1)} %fusion.28, f32[4,8,128]{2,1,0:T(8,128)S(1)} %fusion.80, f32[4,8,128]{2,1,0:T(8,128)S(1)} %get-tuple-element.7, f32[4,8,128,8,128]{2,4,3,1,0:T(8,128)S(1)} %copy-done.3, pred[8,8]{1,0:T(8,128)(4,1)S(1)} %constant_dynamic-slice_fusion), kind=kLoop, calls=%fused_computation.15 | loop fusion | flops 29327360 | bytes 17088576 | tf_op jit(solution)/shard_map/reduce_sum | solution.py:72
  344.3 0.4 convolution_bitcast_fusion.1
  344.7 9.3 %all_to_all.37 = f32[8,8,4,128]{3,1,2,0:T(8,128)S(1)} all-to-all(f32[8,8,4,128]{3,1,2,0:T(8,128)S(1)} %convolution_bitcast_fusion.1), channel_id=1, replica_groups=mesh['groups'=2,'seq'=4,'head'=2,'sub'=2] {'seq','sub'}, dimensions={0} | all-to-all | bytes 262144 | tf_op jit(solution)/shard_map/all_to_all | solution.py:76
  354.0 9.3 %all_to_all.38 = f32[8,8,4,128]{3,1,2,0:T(8,128)S(1)} all-to-all(f32[8,8,4,128]{3,1,2,0:T(8,128)S(1)} %broadcast_in_dim.86), channel_id=1, replica_groups=mesh['groups'=2,'seq'=4,'head'=2,'sub'=2] {'seq','sub'}, dimensions={0} | all-to-all | bytes 262144 | tf_op jit(solution)/shard_map/all_to_all | solution.py:81
  363.3 0.2 fusion.27
  363.6 11.8 %fusion.10 = f32[4,8,128]{2,1,0:T(8,128)S(1)} fusion(f32[4,8,8,128]{3,2,1,0:T(8,128)S(1)} %fusion.27, f32[4,8,128]{2,1,0:T(8,128)S(1)} %fusion.8, f32[4,8,8,128]{3,2,1,0:T(8,128)S(1)} %fusion.28, f32[4,8,128]{2,1,0:T(8,128)S(1)} %fusion.80, f32[4,8,128]{2,1,0:T(8,128)S(1)} %get-tuple-element.7, f32[4,8,128,8,128]{2,4,3,1,0:T(8,128)} %copy-done.2, ...), kind=kLoop, calls=%fused_computation.16 | loop fusion | flops 33550336 | bytes 17104960 | tf_op jit(solution)/shard_map/reduce_sum | solution.py:71
  375.4 16.3 %fusion.11 = f32[4,8,8,128]{3,2,1,0:T(8,128)S(1)} fusion(f32[4,8,128]{2,1,0:T(8,128)S(1)} %fusion.10, f32[4,8,8,128]{3,2,1,0:T(8,128)S(1)} %fusion.27, f32[4,8,128]{2,1,0:T(8,128)S(1)} %fusion.8, f32[4,8,8,128]{3,2,1,0:T(8,128)S(1)} %fusion.28, f32[4,8,128]{2,1,0:T(8,128)S(1)} %fusion.80, f32[4,8,128]{2,1,0:T(8,128)S(1)} %get-tuple-element.7, ...), kind=kLoop, calls=%fused_computation.17 | loop fusion | flops 37715968 | bytes 17236032 | tf_op jit(solution)/shard_map/reduce_sum | solution.py:72
  391.7 0.4 convolution_bitcast_fusion
  392.1 9.3 %all_to_all.39 = f32[8,8,4,128]{3,1,2,0:T(8,128)S(1)} all-to-all(f32[8,8,4,128]{3,1,2,0:T(8,128)S(1)} %convolution_bitcast_fusion), channel_id=1, replica_groups=mesh['groups'=2,'seq'=4,'head'=2,'sub'=2] {'seq','sub'}, dimensions={0} | all-to-all | bytes 262144 | tf_op jit(solution)/shard_map/all_to_all | solution.py:76
  401.4 0.7 broadcast_in_dim.87
  402.1 3.6 all-to-all-start.6
  405.7 6.5 %all-to-all-done.6 = f32[8,8,4,128]{3,1,2,0:T(8,128)S(1)} async-done(((f32[8,8,4,128]{3,1,2,0:T(8,128)}), f32[8,8,4,128]{3,1,2,0:T(8,128)S(1)}, u32[]{:S(2)}, u32[]{:S(2)}) %all-to-all-start.6) | async-done | bytes 131104 | tf_op jit(solution)/shard_map/all_to_all | solution.py:81
  412.1 0.3 fusion.26
  412.4 20.4 %fusion.21 = bf16[8,128,4,128]{1,3,2,0:T(8,128)(2,1)S(1)} fusion(bf16[8,8,128,2,4,128]{5,2,1,0,4,3:T(8,128)(2,1)} %broadcast_select_fusion, f32[4,8,8,128]{3,2,1,0:T(8,128)S(1)} %fusion.26, f32[4,8,128]{2,1,0:T(8,128)S(1)} %fusion.10, f32[4,8,8,128]{3,2,1,0:T(8,128)S(1)} %fusion.27, f32[4,8,128]{2,1,0:T(8,128)S(1)} %fusion.8, ...), kind=kOutput, calls=%fused_computation.34 | convolution fusion | flops 1116209152 | bytes 26673216 | tf_op jit(solution)/shard_map/hbimj,bmjhd->bihd/dot_general | solution.py:87
  432.8 0.7 copy.67
  433.5 1.7 convolution_convert_fusion.4
  435.3 1.5 collective-permute-start
  436.7 23.4 %collective-permute-done = bf16[1024,512]{1,0:T(8,128)(2,1)} collective-permute-done((bf16[1024,512]{1,0:T(8,128)(2,1)}, bf16[1024,512]{1,0:T(8,128)(2,1)}, u32[]{:S(2)}, u32[]{:S(2)}) %collective-permute-start) | collective-permute-done | bytes 1048608 | tf_op jit(solution)/shard_map/ppermute | solution.py:102
  460.2 3.1 add_convert_fusion
  (38 shorter events, 0.9 us)
Async XLA Ops:
  0.0 2.1 copy-start
  21.0 17.7 %copy-start.4 = (s32[64,8]{0,1:T(8,128)S(1)}, s32[64,8]{0,1:T(8,128)}, u32[]{:S(2)}) copy-start(s32[64,8]{0,1:T(8,128)} %param.12) | copy-start | bytes 6148
  32.3 190.3 %all-to-all-start = ((bf16[8,4,128,1024]{3,2,1,0:T(8,128)(2,1)}), bf16[8,4,128,1024]{3,2,1,0:T(8,128)(2,1)}, u32[]{:S(2)}, u32[]{:S(2)}) async-start(bf16[8,4,128,1024]{3,2,1,0:T(8,128)(2,1)} %copy.57), calls=%async_computation | async-start | bytes 16777216 | tf_op jit(solution)/shard_map/all_to_all | solution.py:56
  296.9 8.4 %copy-start.2 = (f32[4,8,128,8,128]{2,4,3,1,0:T(8,128)}, f32[4,8,128,8,128]{2,4,3,1,0:T(8,128)S(1)}, u32[]{:S(2)}) copy-start(f32[4,8,128,8,128]{2,4,3,1,0:T(8,128)S(1)} %get-tuple-element.8) | copy-start | bytes 50331652
  314.9 18.1 %copy-start.3 = (f32[4,8,128,8,128]{2,4,3,1,0:T(8,128)S(1)}, f32[4,8,128,8,128]{2,4,3,1,0:T(8,128)}, u32[]{:S(2)}) copy-start(f32[4,8,128,8,128]{2,4,3,1,0:T(8,128)} %copy-done.2) | copy-start | bytes 50331652
  402.1 10.1 %all-to-all-start.6 = ((f32[8,8,4,128]{3,1,2,0:T(8,128)}), f32[8,8,4,128]{3,1,2,0:T(8,128)S(1)}, u32[]{:S(2)}, u32[]{:S(2)}) async-start(f32[8,8,4,128]{3,1,2,0:T(8,128)} %broadcast_in_dim.87), calls=%async_computation.6 | async-start | bytes 262144 | tf_op jit(solution)/shard_map/all_to_all | solution.py:81
  412.4 21.1 %copy-start.5 = (bf16[512,1024]{1,0:T(8,128)(2,1)S(1)}, bf16[512,1024]{1,0:T(8,128)(2,1)}, u32[]{:S(2)}) copy-start(bf16[512,1024]{1,0:T(8,128)(2,1)} %param.11) | copy-start | bytes 3145732
  412.4 50.9 %copy-start.1 = (bf16[1024,1024]{1,0:T(8,128)(2,1)S(1)}, bf16[1024,1024]{1,0:T(8,128)(2,1)}, u32[]{:S(2)}) copy-start(bf16[1024,1024]{1,0:T(8,128)(2,1)} %param.7) | copy-start | bytes 6291460
  435.3 24.9 %collective-permute-start = (bf16[1024,512]{1,0:T(8,128)(2,1)}, bf16[1024,512]{1,0:T(8,128)(2,1)}, u32[]{:S(2)}, u32[]{:S(2)}) collective-permute-start(bf16[1024,512]{1,0:T(8,128)(2,1)} %convolution_convert_fusion.4), channel_id=1, source_target_pairs={{0,2},{2,0},{1,3},{3,1},{4,6},{6,4},{5,7},{7,5},{8,10},{10,8},{9,1... | collective-permute-start | bytes 3145736 | tf_op jit(solution)/shard_map/ppermute | solution.py:102

commit v2 on v1

--- a/solution.py
+++ b/solution.py
@@ -20,14 +20,14 @@
     local_blocks = row_count // TILE
     heads_here = w_query.shape[1] // HS
     capacity = local_blocks * (maximum_tiles // 2) // seq_devices
+    head_count = lax.axis_size("head")
+    head_index = lax.axis_index("head")
+    rows_part = TILE // head_count
     query_rows = jnp.dot(activations, w_query, preferred_element_type=jnp.float32).astype(
         jnp.bfloat16
     )
-    key_proj = jnp.dot(activations, w_key, preferred_element_type=jnp.float32).astype(jnp.bfloat16)
-    values = jnp.dot(activations, w_value, preferred_element_type=jnp.float32).astype(jnp.bfloat16)
-    payload = jnp.concatenate([key_proj, values], axis=1).reshape(
-        local_blocks, TILE, 2 * heads_here * HS
-    )
+    act_tiles = activations.reshape(local_blocks, TILE, activations.shape[1])
+    my_rows = lax.dynamic_slice_in_dim(act_tiles, head_index * rows_part, rows_part, 1)
     all_valid = jnp.arange(maximum_tiles, dtype=jnp.int32)[None, :] < query_block_counts[:, None]
     owned_ids = device_index * local_blocks + jnp.arange(local_blocks, dtype=jnp.int32)
     wanted = jnp.any(
@@ -41,7 +41,7 @@
         wanted[:, None, :] > 0
     )
     outgoing = jnp.einsum(
-        "dcj,jrf->dcrf", selector.astype(jnp.bfloat16), payload, preferred_element_type=jnp.float32
+        "dcj,jrf->cdrf", selector.astype(jnp.bfloat16), my_rows, preferred_element_type=jnp.float32
     ).astype(jnp.bfloat16)
     my_lists = lax.dynamic_slice_in_dim(tile_lists, device_index * local_blocks, local_blocks, 0)
     my_valid = lax.dynamic_slice_in_dim(all_valid, device_index * local_blocks, local_blocks, 0)
@@ -49,19 +49,67 @@
     matches = (my_lists[:, :, None] == tile_ids[None, None, :]) & my_valid[:, :, None]
     requested = jnp.any(matches, axis=(0, 1)).astype(jnp.int32).reshape(seq_devices, local_blocks)
     own_ranks = jnp.cumsum(requested, axis=1) - requested
-    slot_table = (jnp.arange(seq_devices, dtype=jnp.int32)[:, None] * capacity + own_ranks).reshape(
-        -1
+    sources = jnp.arange(seq_devices, dtype=jnp.int32)
+    if seq_devices & (seq_devices - 1) == 0:
+        source_steps = jnp.bitwise_xor(sources, device_index)
+    else:
+        source_steps = (device_index - sources) % seq_devices
+    slot_table = (source_steps[:, None] * capacity + own_ranks).reshape(-1)
+    slot_index = jnp.sum(jnp.where(matches, slot_table[None, None, :], 0), axis=2)
+    key_weights = w_key.reshape(w_key.shape[0], heads_here, HS)
+    value_weights = w_value.reshape(w_value.shape[0], heads_here, HS)
+    power_of_two = seq_devices & (seq_devices - 1) == 0
+    own_selector = selector[device_index].astype(jnp.bfloat16)
+    key_parts = []
+    value_parts = []
+    for step in range(seq_devices):
+        if step == 0:
+            if head_count == 2:
+                other_rows = lax.dynamic_slice_in_dim(
+                    act_tiles, (1 - head_index) * rows_part, rows_part, 1
+                )
+                full = jnp.concatenate([my_rows, other_rows], axis=1)
+            else:
+                full = act_tiles
+            full = jnp.einsum(
+                "cj,jrf->crf", own_selector, full, preferred_element_type=jnp.float32
+            ).astype(jnp.bfloat16)
+        else:
+            if power_of_two:
+                target = jnp.bitwise_xor(device_index, step)
+                pairs = [(i, i ^ step) for i in range(seq_devices)]
+            else:
+                target = (device_index + step) % seq_devices
+                pairs = [(i, (i + step) % seq_devices) for i in range(seq_devices)]
+            piece = lax.dynamic_index_in_dim(outgoing, target, axis=1, keepdims=False)
+            got = lax.ppermute(piece, ("seq", "sub"), perm=pairs)
+            if head_count == 2:
+                partner = lax.ppermute(got, "head", perm=[(0, 1), (1, 0)])
+                full = jnp.concatenate([got, partner], axis=1)
+            else:
+                full = lax.all_gather(got, "head", axis=1, tiled=True)
+        key_parts.append(
+            jnp.einsum(
+                "cjf,fhd->chjd", full, key_weights, preferred_element_type=jnp.float32
+            ).astype(jnp.bfloat16)
+        )
+        value_parts.append(
+            jnp.einsum(
+                "cjf,fhd->chjd", full, value_weights, preferred_element_type=jnp.float32
+            ).astype(jnp.bfloat16)
+        )
+    key_all = jnp.concatenate(key_parts, axis=0)
+    value_all = jnp.concatenate(value_parts, axis=0)
+    flat_index = slot_index.reshape(-1)
+    key_slots = jnp.take(key_all, flat_index, axis=0, mode="clip").reshape(
+        local_blocks, maximum_tiles, heads_here, TILE, HS
     )
-    slot_index = jnp.sum(jnp.where(matches, slot_table[None, None, :], 0), axis=2)
-    arrived = lax.all_to_all(outgoing, ("seq", "sub"), split_axis=0, concat_axis=0, tiled=True)
-    arrived = arrived.reshape(seq_devices * capacity, TILE, 2 * heads_here * HS)
-    slot_tiles = jnp.take(arrived, slot_index.reshape(-1), axis=0)
-    slot_tiles = slot_tiles.reshape(local_blocks, maximum_tiles, TILE, 2, heads_here, HS)
-    key_slots = slot_tiles[:, :, :, 0]
-    value_slots = slot_tiles[:, :, :, 1]
+    value_slots = jnp.take(value_all, flat_index, axis=0, mode="clip").reshape(
+        local_blocks, maximum_tiles, heads_here, TILE, HS
+    )
     query_blocks = query_rows.reshape(local_blocks, TILE, heads_here, HS)
     scores = jnp.einsum(
-        "bihd,bmjhd->hbimj", query_blocks, key_slots, preferred_element_type=jnp.float32
+        "bihd,bmhjd->hbimj", query_blocks, key_slots, preferred_element_type=jnp.float32
     ) * HS ** (-0.5)
     valid_mask = my_valid[None, :, None, :, None]
     row_max = jnp.max(jnp.where(valid_mask, scores, -1e30), axis=(3, 4), keepdims=True)
@@ -85,7 +133,7 @@
         weights = weights / jnp.maximum(per_slot[:, :, None, :, :], COLUMN_FLOOR)
     probabilities = weights.astype(jnp.bfloat16)
     attended = jnp.einsum(
-        "hbimj,bmjhd->bihd", probabilities, value_slots, preferred_element_type=jnp.float32
+        "hbimj,bmhjd->bihd", probabilities, value_slots, preferred_element_type=jnp.float32
     )
     attended = attended.astype(jnp.bfloat16).reshape(row_count, heads_here * HS)
     head_count = lax.axis_size("head")

time: 465 us -> 359 us (0.77)
  waiting for transfers between devices: 210 us -> 110 us
  blocking collectives: 46.6 us -> 0 us
  matrix products: 46.9 us -> 84.9 us
  starting transfers between devices: 11.4 us -> 40.5 us
  local copies, waits for them, and re-layouts: 75.3 us -> 57.9 us
  other arithmetic: 72.8 us -> 58.8 us
    all_to_all x1 -> x3, waiting for transfers between devices: 180 us -> 9.34 us  [body(): lax.all_to_all(column_complete, ('seq', 'sub'), split_axis=0, concat_axis...]
    ppermute x0 -> x14, waiting for transfers between devices: none -> 68.7 us  [the longest x7 36.4 us: body(): got = lax.ppermute(piece, ('seq', 'sub'), perm=pairs)]
    all_to_all x5 -> x0, blocking collectives: 46.6 us -> none  [the longest x3 27.7 us: body(): lax.all_to_all(column_complete, ('seq', 'sub'), split_axis=0, concat_axis...]
    gather x3 -> x2, local copies, waits for them, and re-layouts: 55 us -> 15.4 us  [the longest x1 7.71 us: body(): jnp.take(key_all, flat_index, axis=0, mode='clip')]
    dot_general x5 -> x20, matrix products: 37.7 us -> 72.4 us  [the longest x8 21.5 us: body(): jnp.einsum('cjf,fhd->chjd', full, value_weights, preferred_element_type=j...]
    dynamic_slice x0 -> x9, local copies, waits for them, and re-layouts: none -> 33.1 us  [the longest x8 31.3 us: body(): piece = lax.dynamic_index_in_dim(outgoing, target, axis=1, keepdims=False)]
    ppermute x0 -> x14, starting transfers between devices: none -> 16.7 us  [the longest x7 9.05 us: body(): got = lax.ppermute(piece, ('seq', 'sub'), perm=pairs)]
    select_n x2 -> x0, other arithmetic: 14.2 us -> none  [body(): slot_tiles = jnp.take(arrived, slot_index.reshape(-1), axis=0)]
  transfers between devices with their start and end apart: 3 -> 21, of which waited for: 3 -> 13; matrix products, arithmetic and copies ran while one was open for 1% -> 19% of each run, Pallas kernels for 0% -> 0%
where the time goes in v2:
time: 359 us; the launch traced here: 353 us
  waiting for transfers between devices  110 us (31%)
  matrix products  84.9 us (24%)
  other arithmetic  58.8 us (16%)
  local copies, waits for them, and re-layouts  57.9 us (16%)
  starting transfers between devices  40.5 us (11%)
    ppermute x7, waiting for transfers between devices, body(): got = lax.ppermute(piece, ('seq', 'sub'), perm=pairs)  36.4 us
    reduce_sum x3, other arithmetic, body(): partial_cols = jnp.sum(weights, axis=2)  33 us
    ppermute x7, waiting for transfers between devices, body(): partner = lax.ppermute(got, 'head', perm=[(0, 1), (1, 0)])  32.3 us
    dynamic_slice x8, local copies, waits for them, and re-layouts, body(): piece = lax.dynamic_index_in_dim(outgoing, target, axis=1, keepdims=False)  31.3 us
    ppermute x1, waiting for transfers between devices, body(): lax.ppermute(other_part.astype(jnp.bfloat16), 'head', perm=[(0, 1), (1, 0)])  24.2 us
    reduce_sum x3, other arithmetic, body(): weights = weights / jnp.sum(weights, axis=(3, 4), keepdims=True)  23.4 us
    dot_general x8, matrix products, body(): jnp.einsum('cjf,fhd->chjd', full, value_weights, preferred_element_type=j...  21.5 us
    dot_general x1, matrix products, body(): jnp.einsum('hbimj,bmhjd->bihd', probabilities, value_slots, preferred_ele...  20.4 us
  transfers between devices with their start and end apart: 21, of which 13 were waited for; matrix products, arithmetic and copies ran while one was open for 19% of the time, Pallas kernels for 0%

profile of v2, /device:TPU:0, one launch (start us, length us, event | category | flops | bytes accessed | tf_op | source)
XLA Modules:
  0.0 353.3 jit_solution(12958517226348950676)
XLA Ops:
  3.8 3.3 convolution_convert_fusion
  7.1 20.9 %dynamic-slice_bitcast_fusion = (bf16[4,1,64,1024]{3,1,0,2:T(2,128)(2,1)}, bf16[4,1,64,1024]{3,1,0,2:T(2,128)(2,1)}, bf16[4,1,64,1024]{3,1,0,2:T(2,128)(2,1)S(1)...) fusion(bf16[64,1024,8,4]{1,2,3,0:T(8,128)(2,1)} %convolution_co, ...), kind=kLoop, calls=%fused_computation.107 | loop fusion | bytes 7340060 | tf_op jit(solution)/shard_map/jit(dynamic_index_in_dim)/dynamic_slice | solution.py:84
  31.3 2.6 collective-permute-start.2
  36.7 2.8 collective-permute-start.6
  41.5 4.1 %convolution_convert_fusion.1 = bf16[1024,512]{1,0:T(8,128)(2,1)} fusion(bf16[1024,1024]{1,0:T(8,128)(2,1)} %param.7, bf16[1024,512]{1,0:T(8,128)(2,1)} %param.8), kind=kOutput, calls=%fused_computation.32 | convolution fusion | flops 1074266112 | bytes 4194304 | tf_op jit(solution)/shard_map/dot_general | solution.py:26
  48.0 2.9 fusion.28
  57.7 3.1 fusion.37
  60.9 5.4 %collective-permute-done.2 = bf16[4,64,1024]{2,1,0:T(8,128)(2,1)} collective-permute-done((bf16[4,64,1024]{2,1,0:T(8,128)(2,1)}, bf16[4,64,1024]{2,1,0:T(8,128)(2,1)}, u32[]{:S(2)}, u32[]{:S(2)}) %collective-permute-start.2) | collective-permute-done | bytes 524320 | tf_op jit(solution)/shard_map/ppermute | solution.py:85
  68.0 9.1 %collective-permute-done.4 = bf16[4,64,1024]{2,1,0:T(8,128)(2,1)} collective-permute-done((bf16[4,64,1024]{2,1,0:T(8,128)(2,1)}, bf16[4,64,1024]{2,1,0:T(8,128)(2,1)}, u32[]{:S(2)}, u32[]{:S(2)}) %collective-permute-start.4) | collective-permute-done | bytes 524320 | tf_op jit(solution)/shard_map/ppermute | solution.py:85
  80.0 2.8 fusion.53
  83.4 2.6 fusion.55
  86.0 21.8 %collective-permute-done.8 = bf16[4,64,1024]{2,1,0:T(8,128)(2,1)} collective-permute-done((bf16[4,64,1024]{2,1,0:T(8,128)(2,1)}, bf16[4,64,1024]{2,1,0:T(8,128)(2,1)}, u32[]{:S(2)}, u32[]{:S(2)}) %collective-permute-start.8) | collective-permute-done | bytes 524320 | tf_op jit(solution)/shard_map/ppermute | solution.py:85
  111.9 2.5 fusion.57
  114.4 2.7 fusion.59
  117.2 5.6 %collective-permute-done.7 = bf16[4,64,1024]{2,1,0:T(8,128)(2,1)S(1)} collective-permute-done((bf16[4,64,1024]{2,1,0:T(8,128)(2,1)}, bf16[4,64,1024]{2,1,0:T(8,128)(2,1)S(1)}, u32[]{:S(2)}, u32[]{:S(2)}) %collective-permute-start.7) | collective-permute-done | bytes 524320 | tf_op jit(solution)/shard_map/ppermute | solution.py:87
  122.8 2.8 fusion.61
  125.5 8.5 %collective-permute-done.9 = bf16[4,64,1024]{2,1,0:T(8,128)(2,1)S(1)} collective-permute-done((bf16[4,64,1024]{2,1,0:T(8,128)(2,1)}, bf16[4,64,1024]{2,1,0:T(8,128)(2,1)S(1)}, u32[]{:S(2)}, u32[]{:S(2)}) %collective-permute-start.9) | collective-permute-done | bytes 524320 | tf_op jit(solution)/shard_map/ppermute | solution.py:87
  134.0 2.7 fusion.63
  136.8 8.5 %collective-permute-done.11 = bf16[4,64,1024]{2,1,0:T(8,128)(2,1)S(1)} collective-permute-done((bf16[4,64,1024]{2,1,0:T(8,128)(2,1)S(1)}, bf16[4,64,1024]{2,1,0:T(8,128)(2,1)S(1)}, u32[]{:S(2)}, u32[]{:S(2)}) %collective-permute-start.11) | collective-permute-done | bytes 524320 | tf_op jit(solution)/shard_map/ppermute | solution.py:87
  146.7 9.7 %collective-permute-done.13 = bf16[4,64,1024]{2,1,0:T(8,128)(2,1)S(1)} collective-permute-done((bf16[4,64,1024]{2,1,0:T(8,128)(2,1)S(1)}, bf16[4,64,1024]{2,1,0:T(8,128)(2,1)S(1)}, u32[]{:S(2)}, u32[]{:S(2)}) %collective-permute-start.13) | collective-permute-done | bytes 524320 | tf_op jit(solution)/shard_map/ppermute | solution.py:87
  158.0 7.7 %gather_fusion.1 = bf16[64,4,128,128]{3,2,1,0:T(8,128)(2,1)} fusion(bf16[32,4,128,128]{3,2,1,0:T(8,128)(2,1)} %fusion.67, s32[1024]{0:T(1024)S(1)} %pad_clamp_fusion), kind=kCustom, calls=%fused_computation.1 | custom fusion | bytes 16777472 | tf_op jit(solution)/shard_map/jit(_take)/gather | solution.py:104
  165.7 5.2 %select_reduce_fusion = (f32[4,8,128]{2,1,0:T(8,128)S(1)}, f32[4,8,128,8,128]{2,4,3,1,0:T(8,128)S(1)}) fusion(pred[8,8]{1,0:T(8,128)(4,1)S(1)} %constant_dynamic-slice_fusion, bf16[8,8,4,128,128]{4,3,2,1,0:T(8,128)(2,1)} %bitcast.348, bf16[8,128,4,128,1]{3,2,1,0,4:T(4,128)(2,1)S(1)} %bitcast.350), kind=kOutput, calls=%fused_computation.12 | convolution fusion | flops 1086320640 | bytes 26230848 | tf_op jit(solution)/shard_map/bihd,bmhjd->hbimj/dot_general | solution.py:111
  170.9 3.5 fusion.156
  176.6 4.9 %divide_reduce_fusion = f32[4,8,8,128]{3,2,1,0:T(8,128)S(1)} fusion(f32[4,8,128]{2,1,0:T(8,128)S(1)} %fusion.156, f32[4,8,128]{2,1,0:T(8,128)S(1)} %get-tuple-element.16, f32[4,8,128,8,128]{2,4,3,1,0:T(8,128)S(1)} %get-tuple-element.17, pred[8,8]{1,0:T(8,128)(4,1)S(1)} %constant_dynamic-slice_fusion), kind=kLoop, calls=%fused_computation.13 | loop fusion | flops 20938752 | bytes 16941120 | tf_op jit(solution)/shard_map/reduce_sum | solution.py:120
  182.6 4.6 %all-to-all-start = ((f32[8,8,4,128]{3,1,2,0:T(8,128)}), f32[8,8,4,128]{3,1,2,0:T(8,128)S(1)}, u32[]{:S(2)}, u32[]{:S(2)}) async-start(f32[8,8,4,128]{3,1,2,0:T(8,128)} %convolution_bitcast_fusion.2), calls=%async_computation | async-start | bytes 262144 | tf_op jit(solution)/shard_map/all_to_all | solution.py:124
  187.2 2.6 fusion.39
  189.9 2.7 fusion.41
  194.7 3.9 %all-to-all-start.1 = ((f32[8,8,4,128]{3,1,2,0:T(8,128)}), f32[8,8,4,128]{3,1,2,0:T(8,128)S(1)}, u32[]{:S(2)}, u32[]{:S(2)}) async-start(f32[8,8,4,128]{3,1,2,0:T(8,128)} %broadcast_in_dim.47), calls=%async_computation.1 | async-start | bytes 262144 | tf_op jit(solution)/shard_map/all_to_all | solution.py:129
  201.1 4.2 %all-to-all-done.1 = f32[8,8,4,128]{3,1,2,0:T(8,128)S(1)} async-done(((f32[8,8,4,128]{3,1,2,0:T(8,128)}), f32[8,8,4,128]{3,1,2,0:T(8,128)S(1)}, u32[]{:S(2)}, u32[]{:S(2)}) %all-to-all-start.1) | async-done | bytes 131104 | tf_op jit(solution)/shard_map/all_to_all | solution.py:129
  205.5 8.2 %fusion.8 = f32[4,8,128]{2,1,0:T(8,128)S(1)} fusion(f32[4,8,8,128]{3,2,1,0:T(8,128)S(1)} %fusion.70, f32[4,8,128]{2,1,0:T(8,128)S(1)} %fusion.156, f32[4,8,128]{2,1,0:T(8,128)S(1)} %get-tuple-element.16, f32[4,8,128,8,128]{2,4,3,1,0:T(8,128)} %copy-done.2, pred[8,8]{1,0:T(8,128)(4,1)S(1)} %constant_dynamic-slice_fusion), kind=kLoop, calls=%fused_computation.15 | loop fusion | flops 25161728 | bytes 16957504 | tf_op jit(solution)/shard_map/reduce_sum | solution.py:119
  213.7 11.7 %fusion.9 = f32[4,8,8,128]{3,2,1,0:T(8,128)S(1)} fusion(f32[4,8,128]{2,1,0:T(8,128)S(1)} %fusion.8, f32[4,8,8,128]{3,2,1,0:T(8,128)S(1)} %fusion.70, f32[4,8,128]{2,1,0:T(8,128)S(1)} %fusion.156, f32[4,8,128]{2,1,0:T(8,128)S(1)} %get-tuple-element.16, f32[4,8,128,8,128]{2,4,3,1,0:T(8,128)} %copy-done.2, pred[8,8]{1,0:T(8,128)(4,1)S(1)} %constant_dynamic-slice_fusion), kind=kLoop, calls=%fused_computation.16 | loop fusion | flops 29327360 | bytes 17088576 | tf_op jit(solution)/shard_map/reduce_sum | solution.py:120
  226.5 3.4 all-to-all-start.2
  229.9 2.7 fusion.45
  232.6 3.9 %all-to-all-done.2 = f32[8,8,4,128]{3,1,2,0:T(8,128)S(1)} async-done(((f32[8,8,4,128]{3,1,2,0:T(8,128)}), f32[8,8,4,128]{3,1,2,0:T(8,128)S(1)}, u32[]{:S(2)}, u32[]{:S(2)}) %all-to-all-start.2) | async-done | bytes 131104 | tf_op jit(solution)/shard_map/all_to_all | solution.py:124
  237.2 3.4 all-to-all-start.3
  240.6 2.6 fusion.47
  243.2 4.1 %all-to-all-done.3 = f32[8,8,4,128]{3,1,2,0:T(8,128)S(1)} async-done(((f32[8,8,4,128]{3,1,2,0:T(8,128)}), f32[8,8,4,128]{3,1,2,0:T(8,128)S(1)}, u32[]{:S(2)}, u32[]{:S(2)}) %all-to-all-start.3) | async-done | bytes 131104 | tf_op jit(solution)/shard_map/all_to_all | solution.py:129
  247.6 11.8 %fusion.10 = f32[4,8,128]{2,1,0:T(8,128)S(1)} fusion(f32[4,8,8,128]{3,2,1,0:T(8,128)S(1)} %fusion.69, f32[4,8,128]{2,1,0:T(8,128)S(1)} %fusion.8, f32[4,8,8,128]{3,2,1,0:T(8,128)S(1)} %fusion.70, f32[4,8,128]{2,1,0:T(8,128)S(1)} %fusion.156, f32[4,8,128]{2,1,0:T(8,128)S(1)} %get-tuple-element.16, f32[4,8,128,8,128]{2,4,3,1,0:T(8,128)} %copy-done.2, ...), kind=kLoop, calls=%fused_computation.17 | loop fusion | flops 33550336 | bytes 17104960 | tf_op jit(solution)/shard_map/reduce_sum | solution.py:119
  259.4 16.3 %fusion.11 = f32[4,8,8,128]{3,2,1,0:T(8,128)S(1)} fusion(f32[4,8,128]{2,1,0:T(8,128)S(1)} %fusion.10, f32[4,8,8,128]{3,2,1,0:T(8,128)S(1)} %fusion.69, f32[4,8,128]{2,1,0:T(8,128)S(1)} %fusion.8, f32[4,8,8,128]{3,2,1,0:T(8,128)S(1)} %fusion.70, f32[4,8,128]{2,1,0:T(8,128)S(1)} %fusion.156, f32[4,8,128]{2,1,0:T(8,128)S(1)} %get-tuple-element.16, ...), kind=kLoop, calls=%fused_computation.18 | loop fusion | flops 37715968 | bytes 17236032 | tf_op jit(solution)/shard_map/reduce_sum | solution.py:120
  276.8 3.4 all-to-all-start.4
  280.2 2.7 fusion.49
  282.9 4.0 %all-to-all-done.4 = f32[8,8,4,128]{3,1,2,0:T(8,128)S(1)} async-done(((f32[8,8,4,128]{3,1,2,0:T(8,128)}), f32[8,8,4,128]{3,1,2,0:T(8,128)S(1)}, u32[]{:S(2)}, u32[]{:S(2)}) %all-to-all-start.4) | async-done | bytes 131104 | tf_op jit(solution)/shard_map/all_to_all | solution.py:124
  287.6 3.6 %all-to-all-start.5 = ((f32[8,8,4,128]{3,1,2,0:T(8,128)}), f32[8,8,4,128]{3,1,2,0:T(8,128)S(1)}, u32[]{:S(2)}, u32[]{:S(2)}) async-start(f32[8,8,4,128]{3,1,2,0:T(8,128)} %broadcast_in_dim.49), calls=%async_computation.5 | async-start | bytes 262144 | tf_op jit(solution)/shard_map/all_to_all | solution.py:129
  291.2 2.6 fusion.51
  293.8 7.7 %gather_fusion = bf16[64,4,128,128]{3,2,1,0:T(8,128)(2,1)} fusion(bf16[32,4,128,128]{3,2,1,0:T(8,128)(2,1)} %fusion.51, s32[1024]{0:T(1024)S(1)} %pad_clamp_fusion), kind=kCustom, calls=%fused_computation | custom fusion | bytes 16777472 | tf_op jit(solution)/shard_map/jit(_take)/gather | solution.py:107
  301.7 20.4 %fusion.31 = bf16[8,128,4,128]{1,3,2,0:T(8,128)(2,1)S(1)} fusion(bf16[8,8,4,128,128]{4,3,2,1,0:T(8,128)(2,1)} %bitcast.347, f32[4,8,8,128]{3,2,1,0:T(8,128)S(1)} %fusion.68, f32[4,8,128]{2,1,0:T(8,128)S(1)} %fusion.10, f32[4,8,8,128]{3,2,1,0:T(8,128)S(1)} %fusion.69, f32[4,8,128]{2,1,0:T(8,128)S(1)} %fusion.8, f32[4,8,8,128]{3,2,1,0:T(8,128)S(1)} %fusion.70, ...), kind=kOutput, calls=%fused_computation.35 | convolution fusion | flops 1116209152 | bytes 26673216 | tf_op jit(solution)/shard_map/hbimj,bmhjd->bihd/dot_general | solution.py:135
  326.0 24.2 %collective-permute-done.14 = bf16[1024,512]{1,0:T(8,128)(2,1)S(1)} collective-permute-done((bf16[1024,512]{1,0:T(8,128)(2,1)}, bf16[1024,512]{1,0:T(8,128)(2,1)S(1)}, u32[]{:S(2)}, u32[]{:S(2)}) %collective-permute-start.14) | collective-permute-done | bytes 1048608 | tf_op jit(solution)/shard_map/ppermute | solution.py:150
  350.2 2.8 add_convert_fusion
  (114 shorter events, 49.5 us)
Async XLA Ops:
  0.0 80.0 %copy-start = (bf16[1024,512]{1,0:T(8,128)(2,1)S(1)}, bf16[1024,512]{1,0:T(8,128)(2,1)}, u32[]{:S(2)}) copy-start(bf16[1024,512]{1,0:T(8,128)(2,1)} %param.9) | copy-start | bytes 3145732
  7.1 33.7 %copy-start.3 = (s32[64,8]{0,1:T(8,128)S(1)}, s32[64,8]{0,1:T(8,128)}, u32[]{:S(2)}) copy-start(s32[64,8]{0,1:T(8,128)} %param.12) | copy-start | bytes 6148
  29.4 26.8 %collective-permute-start = (bf16[4,64,1024]{2,1,0:T(8,128)(2,1)}, bf16[4,64,1024]{2,1,0:T(8,128)(2,1)}, u32[]{:S(2)}, u32[]{:S(2)}) collective-permute-start(bf16[4,64,1024]{2,1,0:T(8,128)(2,1)} %bitcast.346), channel_id=1, source_target_pairs={{0,1},{1,0},{4,5},{5,4},{8,9},{9,8},{12,13},{13,12},{2,3},{3,2},{6... | collective-permute-start | bytes 1572872 | tf_op jit(solution)/shard_map/ppermute | solution.py:85
  31.3 35.0 %collective-permute-start.2 = (bf16[4,64,1024]{2,1,0:T(8,128)(2,1)}, bf16[4,64,1024]{2,1,0:T(8,128)(2,1)}, u32[]{:S(2)}, u32[]{:S(2)}) collective-permute-start(bf16[4,64,1024]{2,1,0:T(8,128)(2,1)} %bitcast.345), channel_id=1, source_target_pairs={{0,4},{1,5},{4,0},{5,1},{8,12},{9,13},{12,8},{13,9},{2,6},{3,7},{6... | collective-permute-start | bytes 1572872 | tf_op jit(solution)/shard_map/ppermute | solution.py:85
  35.2 42.0 %collective-permute-start.4 = (bf16[4,64,1024]{2,1,0:T(8,128)(2,1)}, bf16[4,64,1024]{2,1,0:T(8,128)(2,1)}, u32[]{:S(2)}, u32[]{:S(2)}) collective-permute-start(bf16[4,64,1024]{2,1,0:T(8,128)(2,1)} %bitcast.344), channel_id=1, source_target_pairs={{0,5},{1,4},{4,1},{5,0},{8,13},{9,12},{12,9},{13,8},{2,7},{3,6},{6... | collective-permute-start | bytes 1572872 | tf_op jit(solution)/shard_map/ppermute | solution.py:85
  36.7 41.9 %collective-permute-start.6 = (bf16[4,64,1024]{2,1,0:T(8,128)(2,1)}, bf16[4,64,1024]{2,1,0:T(8,128)(2,1)}, u32[]{:S(2)}, u32[]{:S(2)}) collective-permute-start(bf16[4,64,1024]{2,1,0:T(8,128)(2,1)} %bitcast.343), channel_id=1, source_target_pairs={{0,8},{1,9},{4,12},{5,13},{8,0},{9,1},{12,4},{13,5},{2,10},{3,11},... | collective-permute-start | bytes 1572872 | tf_op jit(solution)/shard_map/ppermute | solution.py:85
  40.8 67.0 %collective-permute-start.8 = (bf16[4,64,1024]{2,1,0:T(8,128)(2,1)}, bf16[4,64,1024]{2,1,0:T(8,128)(2,1)}, u32[]{:S(2)}, u32[]{:S(2)}) collective-permute-start(bf16[4,64,1024]{2,1,0:T(8,128)(2,1)} %bitcast.342), channel_id=1, source_target_pairs={{0,9},{1,8},{4,13},{5,12},{8,1},{9,0},{12,5},{13,4},{2,11},{3,10},... | collective-permute-start | bytes 1572872 | tf_op jit(solution)/shard_map/ppermute | solution.py:85
  56.2 26.6 %collective-permute-start.1 = (bf16[4,64,1024]{2,1,0:T(8,128)(2,1)}, bf16[4,64,1024]{2,1,0:T(8,128)(2,1)S(1)}, u32[]{:S(2)}, u32[]{:S(2)}) collective-permute-start(bf16[4,64,1024]{2,1,0:T(8,128)(2,1)} %collective-permute-done), channel_id=1, source_target_pairs={{0,2},{2,0},{1,3},{3,1},{4,6},{6,4},{5,7},{7,5},{8,10},{10,8},{9,1... | collective-permute-start | bytes 1572872 | tf_op jit(solution)/shard_map/ppermute | solution.py:87
  66.3 42.9 %collective-permute-start.10 = (bf16[4,64,1024]{2,1,0:T(8,128)(2,1)S(1)}, bf16[4,64,1024]{2,1,0:T(8,128)(2,1)S(1)}, u32[]{:S(2)}, u32[]{:S(2)}) collective-permute-start(bf16[4,64,1024]{2,1,0:T(8,128)(2,1)S(1)} %bitcast.354), channel_id=1, source_target_pairs={{0,12},{1,13},{4,8},{5,9},{8,4},{9,5},{12,0},{13,1},{2,14},{3,15},... | collective-permute-start | bytes 1572872 | tf_op jit(solution)/shard_map/ppermute | solution.py:85
  77.2 32.6 %collective-permute-start.12 = (bf16[4,64,1024]{2,1,0:T(8,128)(2,1)S(1)}, bf16[4,64,1024]{2,1,0:T(8,128)(2,1)S(1)}, u32[]{:S(2)}, u32[]{:S(2)}) collective-permute-start(bf16[4,64,1024]{2,1,0:T(8,128)(2,1)S(1)} %bitcast.353), channel_id=1, source_target_pairs={{0,13},{1,12},{4,9},{5,8},{8,5},{9,4},{12,1},{13,0},{2,15},{3,14},... | collective-permute-start | bytes 1572872 | tf_op jit(solution)/shard_map/ppermute | solution.py:85
  78.5 32.8 %collective-permute-start.3 = (bf16[4,64,1024]{2,1,0:T(8,128)(2,1)}, bf16[4,64,1024]{2,1,0:T(8,128)(2,1)S(1)}, u32[]{:S(2)}, u32[]{:S(2)}) collective-permute-start(bf16[4,64,1024]{2,1,0:T(8,128)(2,1)} %collective-permute-done.2), channel_id=1, source_target_pairs={{0,2},{2,0},{1,3},{3,1},{4,6},{6,4},{5,7},{7,5},{8,10},{10,8},{9,1... | collective-permute-start | bytes 1572872 | tf_op jit(solution)/shard_map/ppermute | solution.py:87
  82.8 27.0 %copy-start.13 = (bf16[4,64,1024]{2,1,0:T(8,128)(2,1)}, bf16[4,64,1024]{2,1,0:T(8,128)(2,1)S(1)}, u32[]{:S(2)}) copy-start(bf16[4,64,1024]{2,1,0:T(8,128)(2,1)S(1)} %collective-permute-done.1) | copy-start | bytes 1572868
  82.8 31.6 %collective-permute-start.5 = (bf16[4,64,1024]{2,1,0:T(8,128)(2,1)}, bf16[4,64,1024]{2,1,0:T(8,128)(2,1)S(1)}, u32[]{:S(2)}, u32[]{:S(2)}) collective-permute-start(bf16[4,64,1024]{2,1,0:T(8,128)(2,1)} %collective-permute-done.4), channel_id=1, source_target_pairs={{0,2},{2,0},{1,3},{3,1},{4,6},{6,4},{5,7},{7,5},{8,10},{10,8},{9,1... | collective-permute-start | bytes 1572872 | tf_op jit(solution)/shard_map/ppermute | solution.py:87
  107.8 15.0 %collective-permute-start.7 = (bf16[4,64,1024]{2,1,0:T(8,128)(2,1)}, bf16[4,64,1024]{2,1,0:T(8,128)(2,1)S(1)}, u32[]{:S(2)}, u32[]{:S(2)}) collective-permute-start(bf16[4,64,1024]{2,1,0:T(8,128)(2,1)} %collective-permute-done.6), channel_id=1, source_target_pairs={{0,2},{2,0},{1,3},{3,1},{4,6},{6,4},{5,7},{7,5},{8,10},{10,8},{9,1... | collective-permute-start | bytes 1572872 | tf_op jit(solution)/shard_map/ppermute | solution.py:87
  109.2 36.0 %copy-start.8 = (bf16[4,64,1024]{2,1,0:T(8,128)(2,1)}, bf16[4,64,1024]{2,1,0:T(8,128)(2,1)S(1)}, u32[]{:S(2)}) copy-start(bf16[4,64,1024]{2,1,0:T(8,128)(2,1)S(1)} %collective-permute-done.10) | copy-start | bytes 1572868
  109.2 24.8 %collective-permute-start.9 = (bf16[4,64,1024]{2,1,0:T(8,128)(2,1)}, bf16[4,64,1024]{2,1,0:T(8,128)(2,1)S(1)}, u32[]{:S(2)}, u32[]{:S(2)}) collective-permute-start(bf16[4,64,1024]{2,1,0:T(8,128)(2,1)} %collective-permute-done.8), channel_id=1, source_target_pairs={{0,2},{2,0},{1,3},{3,1},{4,6},{6,4},{5,7},{7,5},{8,10},{10,8},{9,1... | collective-permute-start | bytes 1572872 | tf_op jit(solution)/shard_map/ppermute | solution.py:87
  109.8 46.7 %copy-start.6 = (bf16[4,64,1024]{2,1,0:T(8,128)(2,1)}, bf16[4,64,1024]{2,1,0:T(8,128)(2,1)S(1)}, u32[]{:S(2)}) copy-start(bf16[4,64,1024]{2,1,0:T(8,128)(2,1)S(1)} %collective-permute-done.12) | copy-start | bytes 1572868
  109.8 35.4 %collective-permute-start.11 = (bf16[4,64,1024]{2,1,0:T(8,128)(2,1)S(1)}, bf16[4,64,1024]{2,1,0:T(8,128)(2,1)S(1)}, u32[]{:S(2)}, u32[]{:S(2)}) collective-permute-start(bf16[4,64,1024]{2,1,0:T(8,128)(2,1)S(1)} %collective-permute-done.10), channel_id=1, source_target_pairs={{0,2},{2,0},{1,3},{3,1},{4,6},{6,4},{5,7},{7,5},{8,10},{10,8},{9,1... | collective-permute-start | bytes 1572872 | tf_op jit(solution)/shard_map/ppermute | solution.py:87
  111.3 25.5 %copy-start.18 = (bf16[4,64,1024]{2,1,0:T(8,128)(2,1)}, bf16[4,64,1024]{2,1,0:T(8,128)(2,1)S(1)}, u32[]{:S(2)}) copy-start(bf16[4,64,1024]{2,1,0:T(8,128)(2,1)S(1)} %collective-permute-done.3) | copy-start | bytes 1572868
  111.3 45.2 %collective-permute-start.13 = (bf16[4,64,1024]{2,1,0:T(8,128)(2,1)S(1)}, bf16[4,64,1024]{2,1,0:T(8,128)(2,1)S(1)}, u32[]{:S(2)}, u32[]{:S(2)}) collective-permute-start(bf16[4,64,1024]{2,1,0:T(8,128)(2,1)S(1)} %collective-permute-done.12), channel_id=1, source_target_pairs={{0,2},{2,0},{1,3},{3,1},{4,6},{6,4},{5,7},{7,5},{8,10},{10,8},{9,1... | collective-permute-start | bytes 1572872 | tf_op jit(solution)/shard_map/ppermute | solution.py:87
  114.4 32.3 %copy-start.16 = (bf16[4,64,1024]{2,1,0:T(8,128)(2,1)}, bf16[4,64,1024]{2,1,0:T(8,128)(2,1)S(1)}, u32[]{:S(2)}) copy-start(bf16[4,64,1024]{2,1,0:T(8,128)(2,1)S(1)} %collective-permute-done.5) | copy-start | bytes 1572868
  122.8 33.7 %copy-start.15 = (bf16[4,64,1024]{2,1,0:T(8,128)(2,1)}, bf16[4,64,1024]{2,1,0:T(8,128)(2,1)S(1)}, u32[]{:S(2)}) copy-start(bf16[4,64,1024]{2,1,0:T(8,128)(2,1)S(1)} %collective-permute-done.7) | copy-start | bytes 1572868
  134.0 22.5 %copy-start.11 = (bf16[4,64,1024]{2,1,0:T(8,128)(2,1)}, bf16[4,64,1024]{2,1,0:T(8,128)(2,1)S(1)}, u32[]{:S(2)}) copy-start(bf16[4,64,1024]{2,1,0:T(8,128)(2,1)S(1)} %collective-permute-done.9) | copy-start | bytes 1572868
  145.2 11.2 %copy-start.10 = (bf16[4,64,1024]{2,1,0:T(8,128)(2,1)}, bf16[4,64,1024]{2,1,0:T(8,128)(2,1)S(1)}, u32[]{:S(2)}) copy-start(bf16[4,64,1024]{2,1,0:T(8,128)(2,1)S(1)} %collective-permute-done.11) | copy-start | bytes 1572868
  156.5 9.2 %copy-start.9 = (bf16[4,64,1024]{2,1,0:T(8,128)(2,1)}, bf16[4,64,1024]{2,1,0:T(8,128)(2,1)S(1)}, u32[]{:S(2)}) copy-start(bf16[4,64,1024]{2,1,0:T(8,128)(2,1)S(1)} %collective-permute-done.13) | copy-start | bytes 1572868
  170.9 5.7 %copy-start.2 = (f32[4,8,128,8,128]{2,4,3,1,0:T(8,128)}, f32[4,8,128,8,128]{2,4,3,1,0:T(8,128)S(1)}, u32[]{:S(2)}) copy-start(f32[4,8,128,8,128]{2,4,3,1,0:T(8,128)S(1)} %get-tuple-element.17) | copy-start | bytes 50331652
  176.6 10.6 %copy-start.4 = (bf16[1024,512]{1,0:T(8,128)(2,1)S(1)}, bf16[1024,512]{1,0:T(8,128)(2,1)}, u32[]{:S(2)}) copy-start(bf16[1024,512]{1,0:T(8,128)(2,1)} %param.10) | copy-start | bytes 3145732
  176.6 10.6 %copy-start.14 = (bf16[4,64,1024]{2,1,0:T(8,128)(2,1)S(1)}, bf16[4,64,1024]{2,1,0:T(8,128)(2,1)}, u32[]{:S(2)}) copy-start(bf16[4,64,1024]{2,1,0:T(8,128)(2,1)} %copy-done.13) | copy-start | bytes 1572868
  181.6 17.0 %copy-start.17 = (bf16[4,64,1024]{2,1,0:T(8,128)(2,1)S(1)}, bf16[4,64,1024]{2,1,0:T(8,128)(2,1)}, u32[]{:S(2)}) copy-start(bf16[4,64,1024]{2,1,0:T(8,128)(2,1)} %copy-done.16) | copy-start | bytes 1572868
  182.6 11.3 %all-to-all-start = ((f32[8,8,4,128]{3,1,2,0:T(8,128)}), f32[8,8,4,128]{3,1,2,0:T(8,128)S(1)}, u32[]{:S(2)}, u32[]{:S(2)}) async-start(f32[8,8,4,128]{3,1,2,0:T(8,128)} %convolution_bitcast_fusion.2), calls=%async_computation | async-start | bytes 262144 | tf_op jit(solution)/shard_map/all_to_all | solution.py:124
  194.7 10.6 %all-to-all-start.1 = ((f32[8,8,4,128]{3,1,2,0:T(8,128)}), f32[8,8,4,128]{3,1,2,0:T(8,128)S(1)}, u32[]{:S(2)}, u32[]{:S(2)}) async-start(f32[8,8,4,128]{3,1,2,0:T(8,128)} %broadcast_in_dim.47), calls=%async_computation.1 | async-start | bytes 262144 | tf_op jit(solution)/shard_map/all_to_all | solution.py:129
  213.7 26.9 %copy-start.12 = (bf16[4,64,1024]{2,1,0:T(8,128)(2,1)S(1)}, bf16[4,64,1024]{2,1,0:T(8,128)(2,1)}, u32[]{:S(2)}) copy-start(bf16[4,64,1024]{2,1,0:T(8,128)(2,1)} %copy-done.11) | copy-start | bytes 1572868
  226.5 10.1 %all-to-all-start.2 = ((f32[8,8,4,128]{3,1,2,0:T(8,128)}), f32[8,8,4,128]{3,1,2,0:T(8,128)S(1)}, u32[]{:S(2)}, u32[]{:S(2)}) async-start(f32[8,8,4,128]{3,1,2,0:T(8,128)} %convolution_bitcast_fusion.1), calls=%async_computation.2 | async-start | bytes 262144 | tf_op jit(solution)/shard_map/all_to_all | solution.py:124
  237.2 10.1 %all-to-all-start.3 = ((f32[8,8,4,128]{3,1,2,0:T(8,128)}), f32[8,8,4,128]{3,1,2,0:T(8,128)S(1)}, u32[]{:S(2)}, u32[]{:S(2)}) async-start(f32[8,8,4,128]{3,1,2,0:T(8,128)} %broadcast_in_dim.48), calls=%async_computation.3 | async-start | bytes 262144 | tf_op jit(solution)/shard_map/all_to_all | solution.py:129
  259.4 31.8 %copy-start.7 = (bf16[4,64,1024]{2,1,0:T(8,128)(2,1)S(1)}, bf16[4,64,1024]{2,1,0:T(8,128)(2,1)}, u32[]{:S(2)}) copy-start(bf16[4,64,1024]{2,1,0:T(8,128)(2,1)} %copy-done.6) | copy-start | bytes 1572868
  276.8 10.1 %all-to-all-start.4 = ((f32[8,8,4,128]{3,1,2,0:T(8,128)}), f32[8,8,4,128]{3,1,2,0:T(8,128)S(1)}, u32[]{:S(2)}, u32[]{:S(2)}) async-start(f32[8,8,4,128]{3,1,2,0:T(8,128)} %convolution_bitcast_fusion), calls=%async_computation.4 | async-start | bytes 262144 | tf_op jit(solution)/shard_map/all_to_all | solution.py:124
  287.6 13.9 %all-to-all-start.5 = ((f32[8,8,4,128]{3,1,2,0:T(8,128)}), f32[8,8,4,128]{3,1,2,0:T(8,128)S(1)}, u32[]{:S(2)}, u32[]{:S(2)}) async-start(f32[8,8,4,128]{3,1,2,0:T(8,128)} %broadcast_in_dim.49), calls=%async_computation.5 | async-start | bytes 262144 | tf_op jit(solution)/shard_map/all_to_all | solution.py:129
  301.7 21.1 %copy-start.5 = (bf16[512,1024]{1,0:T(8,128)(2,1)S(1)}, bf16[512,1024]{1,0:T(8,128)(2,1)}, u32[]{:S(2)}) copy-start(bf16[512,1024]{1,0:T(8,128)(2,1)} %param.11) | copy-start | bytes 3145732
  301.7 51.2 %copy-start.1 = (bf16[1024,512]{1,0:T(8,128)(2,1)S(1)}, bf16[1024,512]{1,0:T(8,128)(2,1)}, u32[]{:S(2)}) copy-start(bf16[1024,512]{1,0:T(8,128)(2,1)} %param.9) | copy-start | bytes 3145732
  324.5 25.7 %collective-permute-start.14 = (bf16[1024,512]{1,0:T(8,128)(2,1)}, bf16[1024,512]{1,0:T(8,128)(2,1)S(1)}, u32[]{:S(2)}, u32[]{:S(2)}) collective-permute-start(bf16[1024,512]{1,0:T(8,128)(2,1)} %convolution_convert_fusion.2), channel_id=1, source_target_pairs={{0,2},{2,0},{1,3},{3,1},{4,6},{6,4},{5,7},{7,5},{8,10},{10,8},{9,1... | collective-permute-start | bytes 3145736 | tf_op jit(solution)/shard_map/ppermute | solution.py:150

commit v3 on v2

--- a/solution.py
+++ b/solution.py
@@ -40,9 +40,9 @@
     selector = (slot_ranks[:, None, :] == jnp.arange(capacity, dtype=jnp.int32)[None, :, None]) & (
         wanted[:, None, :] > 0
     )
-    outgoing = jnp.einsum(
-        "dcj,jrf->cdrf", selector.astype(jnp.bfloat16), my_rows, preferred_element_type=jnp.float32
-    ).astype(jnp.bfloat16)
+    send_index = jnp.sum(
+        selector.astype(jnp.int32) * jnp.arange(local_blocks, dtype=jnp.int32)[None, None, :], axis=2
+    )
     my_lists = lax.dynamic_slice_in_dim(tile_lists, device_index * local_blocks, local_blocks, 0)
     my_valid = lax.dynamic_slice_in_dim(all_valid, device_index * local_blocks, local_blocks, 0)
     tile_ids = jnp.arange(block_total, dtype=jnp.int32)
@@ -59,10 +59,10 @@
     key_weights = w_key.reshape(w_key.shape[0], heads_here, HS)
     value_weights = w_value.reshape(w_value.shape[0], heads_here, HS)
     power_of_two = seq_devices & (seq_devices - 1) == 0
-    own_selector = selector[device_index].astype(jnp.bfloat16)
-    key_parts = []
-    value_parts = []
-    for step in range(seq_devices):
+    own_index = send_index[device_index]
+    key_parts = {}
+    value_parts = {}
+    for step in sorted(range(seq_devices), key=lambda k: (k != 0, -k)):
         if step == 0:
             if head_count == 2:
                 other_rows = lax.dynamic_slice_in_dim(
@@ -71,9 +71,7 @@
                 full = jnp.concatenate([my_rows, other_rows], axis=1)
             else:
                 full = act_tiles
-            full = jnp.einsum(
-                "cj,jrf->crf", own_selector, full, preferred_element_type=jnp.float32
-            ).astype(jnp.bfloat16)
+            full = jnp.take(full, own_index, axis=0, mode="clip")
         else:
             if power_of_two:
                 target = jnp.bitwise_xor(device_index, step)
@@ -81,25 +79,21 @@
             else:
                 target = (device_index + step) % seq_devices
                 pairs = [(i, (i + step) % seq_devices) for i in range(seq_devices)]
-            piece = lax.dynamic_index_in_dim(outgoing, target, axis=1, keepdims=False)
+            piece = jnp.take(my_rows, send_index[target], axis=0, mode="clip")
             got = lax.ppermute(piece, ("seq", "sub"), perm=pairs)
             if head_count == 2:
                 partner = lax.ppermute(got, "head", perm=[(0, 1), (1, 0)])
                 full = jnp.concatenate([got, partner], axis=1)
             else:
                 full = lax.all_gather(got, "head", axis=1, tiled=True)
-        key_parts.append(
-            jnp.einsum(
-                "cjf,fhd->chjd", full, key_weights, preferred_element_type=jnp.float32
-            ).astype(jnp.bfloat16)
-        )
-        value_parts.append(
-            jnp.einsum(
-                "cjf,fhd->chjd", full, value_weights, preferred_element_type=jnp.float32
-            ).astype(jnp.bfloat16)
-        )
-    key_all = jnp.concatenate(key_parts, axis=0)
-    value_all = jnp.concatenate(value_parts, axis=0)
+        key_parts[step] = jnp.einsum(
+            "cjf,fhd->chjd", full, key_weights, preferred_element_type=jnp.float32
+        ).astype(jnp.bfloat16)
+        value_parts[step] = jnp.einsum(
+            "cjf,fhd->chjd", full, value_weights, preferred_element_type=jnp.float32
+        ).astype(jnp.bfloat16)
+    key_all = jnp.concatenate([key_parts[k] for k in range(seq_devices)], axis=0)
+    value_all = jnp.concatenate([value_parts[k] for k in range(seq_devices)], axis=0)
     flat_index = slot_index.reshape(-1)
     key_slots = jnp.take(key_all, flat_index, axis=0, mode="clip").reshape(
         local_blocks, maximum_tiles, heads_here, TILE, HS

time: 359 us -> 331 us (0.922); the launches traced: 353 us -> 330 us
  local copies, waits for them, and re-layouts: 57.9 us -> 37.4 us
  matrix products: 84.9 us -> 77.1 us
  waiting for transfers between devices: 110 us -> 114 us
    dynamic_slice x8 -> x1, local copies, waits for them, and re-layouts: 31.3 us -> 0.3 us  [body(): piece = jnp.take(my_rows, send_index[target], axis=0, mode='clip')]
    gather x0 -> x8, local copies, waits for them, and re-layouts: none -> 11.9 us  [the longest x7 9.73 us: body(): piece = jnp.take(my_rows, send_index[target], axis=0, mode='clip')]
    dot_general x2 -> x0, matrix products: 6.2 us -> none  [the longest x1 3.27 us: body(): jnp.einsum('dcj,jrf->cdrf', selector.astype(jnp.bfloat16), my_rows, prefe...]
where the time goes in v3:
time: 331 us; the launch traced here: 330 us
  waiting for transfers between devices  114 us (34%)
  matrix products  77.1 us (23%)
  other arithmetic  60.7 us (18%)
  starting transfers between devices  40.3 us (12%)
  local copies, waits for them, and re-layouts  37.4 us (11%)
    ppermute x7, waiting for transfers between devices, body(): got = lax.ppermute(piece, ('seq', 'sub'), perm=pairs)  39.9 us
    reduce_sum x3, other arithmetic, body(): partial_cols = jnp.sum(weights, axis=2)  33 us
    ppermute x7, waiting for transfers between devices, body(): partner = lax.ppermute(got, 'head', perm=[(0, 1), (1, 0)])  32.3 us
    ppermute x1, waiting for transfers between devices, body(): lax.ppermute(other_part.astype(jnp.bfloat16), 'head', perm=[(0, 1), (1, 0)])  24 us
    reduce_sum x3, other arithmetic, body(): weights = weights / jnp.sum(weights, axis=(3, 4), keepdims=True)  23.4 us
    dot_general x8, matrix products, body(): jnp.einsum('cjf,fhd->chjd', full, value_weights, preferred_element_type=j...  20.9 us
    dot_general x1, matrix products, body(): jnp.einsum('hbimj,bmhjd->bihd', probabilities, value_slots, preferred_ele...  20.4 us
    dot_general x8, matrix products, body(): jnp.einsum('cjf,fhd->chjd', full, key_weights, preferred_element_type=jnp...  18 us
  transfers between devices with their start and end apart: 21, of which 13 were waited for; matrix products, arithmetic and copies ran while one was open for 19% of the time, Pallas kernels for 0%

profile of v3, /device:TPU:0, one launch (start us, length us, event | category | flops | bytes accessed | tf_op | source)
XLA Modules:
  0.0 330.0 jit_solution(140497754371232404)
XLA Ops:
  2.5 1.8 constant_dynamic-slice_fusion.11
  7.6 2.6 collective-permute-start.2
  13.1 2.8 collective-permute-start.6
  18.3 4.1 %convolution_convert_fusion = bf16[1024,512]{1,0:T(8,128)(2,1)} fusion(bf16[1024,1024]{1,0:T(8,128)(2,1)} %param.7, bf16[1024,512]{1,0:T(8,128)(2,1)} %param.8), kind=kOutput, calls=%fused_computation.35 | convolution fusion | flops 1074266112 | bytes 4194304 | tf_op jit(solution)/shard_map/dot_general | solution.py:26
  28.4 2.2 gather_fusion
  32.2 2.8 fusion.27
  35.0 7.5 %collective-permute-done.2 = bf16[4,64,1024]{2,1,0:T(8,128)(2,1)} collective-permute-done((bf16[4,64,1024]{2,1,0:T(8,128)(2,1)}, bf16[4,64,1024]{2,1,0:T(8,128)(2,1)}, u32[]{:S(2)}, u32[]{:S(2)}) %collective-permute-start.2) | collective-permute-done | bytes 524320 | tf_op jit(solution)/shard_map/ppermute | solution.py:83
  44.3 9.1 %collective-permute-done.4 = bf16[4,64,1024]{2,1,0:T(8,128)(2,1)} collective-permute-done((bf16[4,64,1024]{2,1,0:T(8,128)(2,1)}, bf16[4,64,1024]{2,1,0:T(8,128)(2,1)}, u32[]{:S(2)}, u32[]{:S(2)}) %collective-permute-start.4) | collective-permute-done | bytes 524320 | tf_op jit(solution)/shard_map/ppermute | solution.py:83
  58.3 2.6 fusion.45
  61.0 23.2 %collective-permute-done.8 = bf16[4,64,1024]{2,1,0:T(8,128)(2,1)} collective-permute-done((bf16[4,64,1024]{2,1,0:T(8,128)(2,1)}, bf16[4,64,1024]{2,1,0:T(8,128)(2,1)}, u32[]{:S(2)}, u32[]{:S(2)}) %collective-permute-start.8) | collective-permute-done | bytes 524320 | tf_op jit(solution)/shard_map/ppermute | solution.py:83
  88.3 2.5 fusion.47
  90.9 2.7 fusion.49
  93.6 5.6 %collective-permute-done.7 = bf16[4,64,1024]{2,1,0:T(8,128)(2,1)S(1)} collective-permute-done((bf16[4,64,1024]{2,1,0:T(8,128)(2,1)}, bf16[4,64,1024]{2,1,0:T(8,128)(2,1)S(1)}, u32[]{:S(2)}, u32[]{:S(2)}) %collective-permute-start.7) | collective-permute-done | bytes 524320 | tf_op jit(solution)/shard_map/ppermute | solution.py:85
  99.2 2.8 fusion.51
  102.0 8.5 %collective-permute-done.9 = bf16[4,64,1024]{2,1,0:T(8,128)(2,1)S(1)} collective-permute-done((bf16[4,64,1024]{2,1,0:T(8,128)(2,1)}, bf16[4,64,1024]{2,1,0:T(8,128)(2,1)S(1)}, u32[]{:S(2)}, u32[]{:S(2)}) %collective-permute-start.9) | collective-permute-done | bytes 524320 | tf_op jit(solution)/shard_map/ppermute | solution.py:85
  110.4 2.8 fusion.53
  113.2 8.5 %collective-permute-done.11 = bf16[4,64,1024]{2,1,0:T(8,128)(2,1)S(1)} collective-permute-done((bf16[4,64,1024]{2,1,0:T(8,128)(2,1)S(1)}, bf16[4,64,1024]{2,1,0:T(8,128)(2,1)S(1)}, u32[]{:S(2)}, u32[]{:S(2)}) %collective-permute-start.11) | collective-permute-done | bytes 524320 | tf_op jit(solution)/shard_map/ppermute | solution.py:85
  123.2 9.7 %collective-permute-done.13 = bf16[4,64,1024]{2,1,0:T(8,128)(2,1)S(1)} collective-permute-done((bf16[4,64,1024]{2,1,0:T(8,128)(2,1)S(1)}, bf16[4,64,1024]{2,1,0:T(8,128)(2,1)S(1)}, u32[]{:S(2)}, u32[]{:S(2)}) %collective-permute-start.13) | collective-permute-done | bytes 524320 | tf_op jit(solution)/shard_map/ppermute | solution.py:85
  135.2 7.7 %gather_fusion.9 = bf16[64,4,128,128]{3,2,1,0:T(8,128)(2,1)} fusion(bf16[32,4,128,128]{3,2,1,0:T(8,128)(2,1)} %fusion.57, s32[1024]{0:T(1024)S(1)} %pad_clamp_fusion), kind=kCustom, calls=%fused_computation.9 | custom fusion | bytes 16777472 | tf_op jit(solution)/shard_map/jit(_take)/gather | solution.py:98
  142.9 5.1 %select_reduce_fusion = (f32[4,8,128]{2,1,0:T(8,128)S(1)}, f32[4,8,128,8,128]{2,4,3,1,0:T(8,128)S(1)}) fusion(pred[8,8]{1,0:T(8,128)(4,1)S(1)} %constant_dynamic-slice_fusion, bf16[8,8,4,128,128]{4,3,2,1,0:T(8,128)(2,1)} %bitcast.305, bf16[8,128,4,128,1]{3,2,1,0,4:T(4,128)(2,1)S(1)} %bitcast.307), kind=kOutput, calls=%fused_computation.20 | convolution fusion | flops 1086320640 | bytes 26230848 | tf_op jit(solution)/shard_map/bihd,bmhjd->hbimj/dot_general | solution.py:105
  148.1 3.5 %fusion.147 = f32[4,8,128]{2,1,0:T(8,128)S(1)} fusion(f32[4,8,128]{2,1,0:T(8,128)S(1)} %get-tuple-element.17, f32[4,8,128,8,128]{2,4,3,1,0:T(8,128)S(1)} %get-tuple-element.18, pred[8,8]{1,0:T(8,128)(4,1)S(1)} %constant_dynamic-slice_fusion), kind=kLoop, calls=%fused_computation.220 | loop fusion | flops 16773120 | bytes 16810048 | tf_op jit(solution)/shard_map/reduce_sum | solution.py:113
  151.5 2.2 copy-done.2
  153.8 4.9 %divide_reduce_fusion = f32[4,8,8,128]{3,2,1,0:T(8,128)S(1)} fusion(f32[4,8,128]{2,1,0:T(8,128)S(1)} %fusion.147, f32[4,8,128]{2,1,0:T(8,128)S(1)} %get-tuple-element.17, f32[4,8,128,8,128]{2,4,3,1,0:T(8,128)S(1)} %get-tuple-element.18, pred[8,8]{1,0:T(8,128)(4,1)S(1)} %constant_dynamic-slice_fusion), kind=kLoop, calls=%fused_computation.21 | loop fusion | flops 20938752 | bytes 16941120 | tf_op jit(solution)/shard_map/reduce_sum | solution.py:114
  159.8 4.6 %all-to-all-start = ((f32[8,8,4,128]{3,1,2,0:T(8,128)}), f32[8,8,4,128]{3,1,2,0:T(8,128)S(1)}, u32[]{:S(2)}, u32[]{:S(2)}) async-start(f32[8,8,4,128]{3,1,2,0:T(8,128)} %convolution_bitcast_fusion.2), calls=%async_computation | async-start | bytes 262144 | tf_op jit(solution)/shard_map/all_to_all | solution.py:118
  164.4 2.6 fusion.29
  167.0 2.7 fusion.31
  171.8 3.7 %all-to-all-start.1 = ((f32[8,8,4,128]{3,1,2,0:T(8,128)}), f32[8,8,4,128]{3,1,2,0:T(8,128)S(1)}, u32[]{:S(2)}, u32[]{:S(2)}) async-start(f32[8,8,4,128]{3,1,2,0:T(8,128)} %broadcast_in_dim.114), calls=%async_computation.1 | async-start | bytes 262144 | tf_op jit(solution)/shard_map/all_to_all | solution.py:123
  175.5 2.5 fusion.33
  178.1 4.2 %all-to-all-done.1 = f32[8,8,4,128]{3,1,2,0:T(8,128)S(1)} async-done(((f32[8,8,4,128]{3,1,2,0:T(8,128)}), f32[8,8,4,128]{3,1,2,0:T(8,128)S(1)}, u32[]{:S(2)}, u32[]{:S(2)}) %all-to-all-start.1) | async-done | bytes 131104 | tf_op jit(solution)/shard_map/all_to_all | solution.py:123
  182.5 8.2 %fusion.8 = f32[4,8,128]{2,1,0:T(8,128)S(1)} fusion(f32[4,8,8,128]{3,2,1,0:T(8,128)S(1)} %fusion.60, f32[4,8,128]{2,1,0:T(8,128)S(1)} %fusion.147, f32[4,8,128]{2,1,0:T(8,128)S(1)} %get-tuple-element.17, f32[4,8,128,8,128]{2,4,3,1,0:T(8,128)} %copy-done.2, pred[8,8]{1,0:T(8,128)(4,1)S(1)} %constant_dynamic-slice_fusion), kind=kLoop, calls=%fused_computation.23 | loop fusion | flops 25161728 | bytes 16957504 | tf_op jit(solution)/shard_map/reduce_sum | solution.py:113
  190.7 11.7 %fusion.9 = f32[4,8,8,128]{3,2,1,0:T(8,128)S(1)} fusion(f32[4,8,128]{2,1,0:T(8,128)S(1)} %fusion.8, f32[4,8,8,128]{3,2,1,0:T(8,128)S(1)} %fusion.60, f32[4,8,128]{2,1,0:T(8,128)S(1)} %fusion.147, f32[4,8,128]{2,1,0:T(8,128)S(1)} %get-tuple-element.17, f32[4,8,128,8,128]{2,4,3,1,0:T(8,128)} %copy-done.2, pred[8,8]{1,0:T(8,128)(4,1)S(1)} %constant_dynamic-slice_fusion), kind=kLoop, calls=%fused_computation.24 | loop fusion | flops 29327360 | bytes 17088576 | tf_op jit(solution)/shard_map/reduce_sum | solution.py:114
  203.5 3.4 %all-to-all-start.2 = ((f32[8,8,4,128]{3,1,2,0:T(8,128)}), f32[8,8,4,128]{3,1,2,0:T(8,128)S(1)}, u32[]{:S(2)}, u32[]{:S(2)}) async-start(f32[8,8,4,128]{3,1,2,0:T(8,128)} %convolution_bitcast_fusion.1), calls=%async_computation.2 | async-start | bytes 262144 | tf_op jit(solution)/shard_map/all_to_all | solution.py:118
  206.9 2.6 fusion.35
  209.5 4.1 %all-to-all-done.2 = f32[8,8,4,128]{3,1,2,0:T(8,128)S(1)} async-done(((f32[8,8,4,128]{3,1,2,0:T(8,128)}), f32[8,8,4,128]{3,1,2,0:T(8,128)S(1)}, u32[]{:S(2)}, u32[]{:S(2)}) %all-to-all-start.2) | async-done | bytes 131104 | tf_op jit(solution)/shard_map/all_to_all | solution.py:118
  214.3 3.4 %all-to-all-start.3 = ((f32[8,8,4,128]{3,1,2,0:T(8,128)}), f32[8,8,4,128]{3,1,2,0:T(8,128)S(1)}, u32[]{:S(2)}, u32[]{:S(2)}) async-start(f32[8,8,4,128]{3,1,2,0:T(8,128)} %broadcast_in_dim.115), calls=%async_computation.3 | async-start | bytes 262144 | tf_op jit(solution)/shard_map/all_to_all | solution.py:123
  217.6 2.6 fusion.37
  220.2 4.1 %all-to-all-done.3 = f32[8,8,4,128]{3,1,2,0:T(8,128)S(1)} async-done(((f32[8,8,4,128]{3,1,2,0:T(8,128)}), f32[8,8,4,128]{3,1,2,0:T(8,128)S(1)}, u32[]{:S(2)}, u32[]{:S(2)}) %all-to-all-start.3) | async-done | bytes 131104 | tf_op jit(solution)/shard_map/all_to_all | solution.py:123
  224.6 11.8 %fusion.10 = f32[4,8,128]{2,1,0:T(8,128)S(1)} fusion(f32[4,8,8,128]{3,2,1,0:T(8,128)S(1)} %fusion.59, f32[4,8,128]{2,1,0:T(8,128)S(1)} %fusion.8, f32[4,8,8,128]{3,2,1,0:T(8,128)S(1)} %fusion.60, f32[4,8,128]{2,1,0:T(8,128)S(1)} %fusion.147, f32[4,8,128]{2,1,0:T(8,128)S(1)} %get-tuple-element.17, f32[4,8,128,8,128]{2,4,3,1,0:T(8,128)} %copy-done.2, ...), kind=kLoop, calls=%fused_computation.25 | loop fusion | flops 33550336 | bytes 17104960 | tf_op jit(solution)/shard_map/reduce_sum | solution.py:113
  236.4 16.4 %fusion.11 = f32[4,8,8,128]{3,2,1,0:T(8,128)S(1)} fusion(f32[4,8,128]{2,1,0:T(8,128)S(1)} %fusion.10, f32[4,8,8,128]{3,2,1,0:T(8,128)S(1)} %fusion.59, f32[4,8,128]{2,1,0:T(8,128)S(1)} %fusion.8, f32[4,8,8,128]{3,2,1,0:T(8,128)S(1)} %fusion.60, f32[4,8,128]{2,1,0:T(8,128)S(1)} %fusion.147, f32[4,8,128]{2,1,0:T(8,128)S(1)} %get-tuple-element.17, ...), kind=kLoop, calls=%fused_computation.26 | loop fusion | flops 37715968 | bytes 17236032 | tf_op jit(solution)/shard_map/reduce_sum | solution.py:114
  253.9 3.4 %all-to-all-start.4 = ((f32[8,8,4,128]{3,1,2,0:T(8,128)}), f32[8,8,4,128]{3,1,2,0:T(8,128)S(1)}, u32[]{:S(2)}, u32[]{:S(2)}) async-start(f32[8,8,4,128]{3,1,2,0:T(8,128)} %convolution_bitcast_fusion), calls=%async_computation.4 | async-start | bytes 262144 | tf_op jit(solution)/shard_map/all_to_all | solution.py:118
  257.2 2.5 fusion.39
  259.8 4.1 %all-to-all-done.4 = f32[8,8,4,128]{3,1,2,0:T(8,128)S(1)} async-done(((f32[8,8,4,128]{3,1,2,0:T(8,128)}), f32[8,8,4,128]{3,1,2,0:T(8,128)S(1)}, u32[]{:S(2)}, u32[]{:S(2)}) %all-to-all-start.4) | async-done | bytes 131104 | tf_op jit(solution)/shard_map/all_to_all | solution.py:118
  264.6 3.6 %all-to-all-start.5 = ((f32[8,8,4,128]{3,1,2,0:T(8,128)}), f32[8,8,4,128]{3,1,2,0:T(8,128)S(1)}, u32[]{:S(2)}, u32[]{:S(2)}) async-start(f32[8,8,4,128]{3,1,2,0:T(8,128)} %broadcast_in_dim.116), calls=%async_computation.5 | async-start | bytes 262144 | tf_op jit(solution)/shard_map/all_to_all | solution.py:123
  268.3 2.6 fusion.41
  270.8 7.7 %gather_fusion.8 = bf16[64,4,128,128]{3,2,1,0:T(8,128)(2,1)} fusion(bf16[32,4,128,128]{3,2,1,0:T(8,128)(2,1)} %fusion.41, s32[1024]{0:T(1024)S(1)} %pad_clamp_fusion), kind=kCustom, calls=%fused_computation.8 | custom fusion | bytes 16777472 | tf_op jit(solution)/shard_map/jit(_take)/gather | solution.py:101
  278.8 20.4 %fusion.21 = bf16[8,128,4,128]{1,3,2,0:T(8,128)(2,1)S(1)} fusion(bf16[8,8,4,128,128]{4,3,2,1,0:T(8,128)(2,1)} %bitcast.304, f32[4,8,8,128]{3,2,1,0:T(8,128)S(1)} %fusion.58, f32[4,8,128]{2,1,0:T(8,128)S(1)} %fusion.10, f32[4,8,8,128]{3,2,1,0:T(8,128)S(1)} %fusion.59, f32[4,8,128]{2,1,0:T(8,128)S(1)} %fusion.8, f32[4,8,8,128]{3,2,1,0:T(8,128)S(1)} %fusion.60, ...), kind=kOutput, calls=%fused_computation.37 | convolution fusion | flops 1116209152 | bytes 26673216 | tf_op jit(solution)/shard_map/hbimj,bmhjd->bihd/dot_general | solution.py:129
  303.1 24.0 %collective-permute-done.14 = bf16[1024,512]{1,0:T(8,128)(2,1)} collective-permute-done((bf16[1024,512]{1,0:T(8,128)(2,1)}, bf16[1024,512]{1,0:T(8,128)(2,1)}, u32[]{:S(2)}, u32[]{:S(2)}) %collective-permute-start.14) | collective-permute-done | bytes 1048608 | tf_op jit(solution)/shard_map/ppermute | solution.py:144
  327.1 2.9 add_convert_fusion
  (124 shorter events, 44.6 us)
Async XLA Ops:
  0.0 56.2 %copy-start = (bf16[1024,512]{1,0:T(8,128)(2,1)S(1)}, bf16[1024,512]{1,0:T(8,128)(2,1)}, u32[]{:S(2)}) copy-start(bf16[1024,512]{1,0:T(8,128)(2,1)} %param.9) | copy-start | bytes 3145732
  0.0 17.3 %copy-start.3 = (s32[64,8]{0,1:T(8,128)S(1)}, s32[64,8]{0,1:T(8,128)}, u32[]{:S(2)}) copy-start(s32[64,8]{0,1:T(8,128)} %param.12) | copy-start | bytes 6148
  5.7 24.9 %collective-permute-start = (bf16[4,64,1024]{2,1,0:T(8,128)(2,1)}, bf16[4,64,1024]{2,1,0:T(8,128)(2,1)}, u32[]{:S(2)}, u32[]{:S(2)}) collective-permute-start(bf16[4,64,1024]{2,1,0:T(8,128)(2,1)} %gather_fusion.1), channel_id=1, source_target_pairs={{0,1},{1,0},{4,5},{5,4},{8,9},{9,8},{12,13},{13,12},{2,3},{3,2},{6... | collective-permute-start | bytes 1572872 | tf_op jit(solution)/shard_map/ppermute | solution.py:83
  7.6 34.9 %collective-permute-start.2 = (bf16[4,64,1024]{2,1,0:T(8,128)(2,1)}, bf16[4,64,1024]{2,1,0:T(8,128)(2,1)}, u32[]{:S(2)}, u32[]{:S(2)}) collective-permute-start(bf16[4,64,1024]{2,1,0:T(8,128)(2,1)} %gather_fusion.2), channel_id=1, source_target_pairs={{0,4},{1,5},{4,0},{5,1},{8,12},{9,13},{12,8},{13,9},{2,6},{3,7},{6... | collective-permute-start | bytes 1572872 | tf_op jit(solution)/shard_map/ppermute | solution.py:83
  11.6 41.8 %collective-permute-start.4 = (bf16[4,64,1024]{2,1,0:T(8,128)(2,1)}, bf16[4,64,1024]{2,1,0:T(8,128)(2,1)}, u32[]{:S(2)}, u32[]{:S(2)}) collective-permute-start(bf16[4,64,1024]{2,1,0:T(8,128)(2,1)} %gather_fusion.3), channel_id=1, source_target_pairs={{0,5},{1,4},{4,1},{5,0},{8,13},{9,12},{12,9},{13,8},{2,7},{3,6},{6... | collective-permute-start | bytes 1572872 | tf_op jit(solution)/shard_map/ppermute | solution.py:83
  13.1 41.7 %collective-permute-start.6 = (bf16[4,64,1024]{2,1,0:T(8,128)(2,1)}, bf16[4,64,1024]{2,1,0:T(8,128)(2,1)}, u32[]{:S(2)}, u32[]{:S(2)}) collective-permute-start(bf16[4,64,1024]{2,1,0:T(8,128)(2,1)} %gather_fusion.4), channel_id=1, source_target_pairs={{0,8},{1,9},{4,12},{5,13},{8,0},{9,1},{12,4},{13,5},{2,10},{3,11},... | collective-permute-start | bytes 1572872 | tf_op jit(solution)/shard_map/ppermute | solution.py:83
  17.3 66.9 %collective-permute-start.8 = (bf16[4,64,1024]{2,1,0:T(8,128)(2,1)}, bf16[4,64,1024]{2,1,0:T(8,128)(2,1)}, u32[]{:S(2)}, u32[]{:S(2)}) collective-permute-start(bf16[4,64,1024]{2,1,0:T(8,128)(2,1)} %gather_fusion.5), channel_id=1, source_target_pairs={{0,9},{1,8},{4,13},{5,12},{8,1},{9,0},{12,5},{13,4},{2,11},{3,10},... | collective-permute-start | bytes 1572872 | tf_op jit(solution)/shard_map/ppermute | solution.py:83
  30.6 27.2 %collective-permute-start.1 = (bf16[4,64,1024]{2,1,0:T(8,128)(2,1)}, bf16[4,64,1024]{2,1,0:T(8,128)(2,1)S(1)}, u32[]{:S(2)}, u32[]{:S(2)}) collective-permute-start(bf16[4,64,1024]{2,1,0:T(8,128)(2,1)} %collective-permute-done), channel_id=1, source_target_pairs={{0,2},{2,0},{1,3},{3,1},{4,6},{6,4},{5,7},{7,5},{8,10},{10,8},{9,1... | collective-permute-start | bytes 1572872 | tf_op jit(solution)/shard_map/ppermute | solution.py:85
  42.5 43.1 %collective-permute-start.10 = (bf16[4,64,1024]{2,1,0:T(8,128)(2,1)}, bf16[4,64,1024]{2,1,0:T(8,128)(2,1)S(1)}, u32[]{:S(2)}, u32[]{:S(2)}) collective-permute-start(bf16[4,64,1024]{2,1,0:T(8,128)(2,1)} %gather_fusion.6), channel_id=1, source_target_pairs={{0,12},{1,13},{4,8},{5,9},{8,4},{9,5},{12,0},{13,1},{2,14},{3,15},... | collective-permute-start | bytes 1572872 | tf_op jit(solution)/shard_map/ppermute | solution.py:83
  53.4 32.8 %collective-permute-start.12 = (bf16[4,64,1024]{2,1,0:T(8,128)(2,1)}, bf16[4,64,1024]{2,1,0:T(8,128)(2,1)S(1)}, u32[]{:S(2)}, u32[]{:S(2)}) collective-permute-start(bf16[4,64,1024]{2,1,0:T(8,128)(2,1)} %gather_fusion.7), channel_id=1, source_target_pairs={{0,13},{1,12},{4,9},{5,8},{8,5},{9,4},{12,1},{13,0},{2,15},{3,14},... | collective-permute-start | bytes 1572872 | tf_op jit(solution)/shard_map/ppermute | solution.py:83
  54.8 32.9 %collective-permute-start.3 = (bf16[4,64,1024]{2,1,0:T(8,128)(2,1)}, bf16[4,64,1024]{2,1,0:T(8,128)(2,1)S(1)}, u32[]{:S(2)}, u32[]{:S(2)}) collective-permute-start(bf16[4,64,1024]{2,1,0:T(8,128)(2,1)} %collective-permute-done.2), channel_id=1, source_target_pairs={{0,2},{2,0},{1,3},{3,1},{4,6},{6,4},{5,7},{7,5},{8,10},{10,8},{9,1... | collective-permute-start | bytes 1572872 | tf_op jit(solution)/shard_map/ppermute | solution.py:85
  57.8 29.9 %copy-start.14 = (bf16[4,64,1024]{2,1,0:T(8,128)(2,1)}, bf16[4,64,1024]{2,1,0:T(8,128)(2,1)S(1)}, u32[]{:S(2)}) copy-start(bf16[4,64,1024]{2,1,0:T(8,128)(2,1)S(1)} %collective-permute-done.1) | copy-start | bytes 1572868
  57.8 33.1 %collective-permute-start.5 = (bf16[4,64,1024]{2,1,0:T(8,128)(2,1)}, bf16[4,64,1024]{2,1,0:T(8,128)(2,1)S(1)}, u32[]{:S(2)}, u32[]{:S(2)}) collective-permute-start(bf16[4,64,1024]{2,1,0:T(8,128)(2,1)} %collective-permute-done.4), channel_id=1, source_target_pairs={{0,2},{2,0},{1,3},{3,1},{4,6},{6,4},{5,7},{7,5},{8,10},{10,8},{9,1... | collective-permute-start | bytes 1572872 | tf_op jit(solution)/shard_map/ppermute | solution.py:85
  84.2 15.0 %collective-permute-start.7 = (bf16[4,64,1024]{2,1,0:T(8,128)(2,1)}, bf16[4,64,1024]{2,1,0:T(8,128)(2,1)S(1)}, u32[]{:S(2)}, u32[]{:S(2)}) collective-permute-start(bf16[4,64,1024]{2,1,0:T(8,128)(2,1)} %collective-permute-done.6), channel_id=1, source_target_pairs={{0,2},{2,0},{1,3},{3,1},{4,6},{6,4},{5,7},{7,5},{8,10},{10,8},{9,1... | collective-permute-start | bytes 1572872 | tf_op jit(solution)/shard_map/ppermute | solution.py:85
  85.6 36.0 %copy-start.8 = (bf16[4,64,1024]{2,1,0:T(8,128)(2,1)}, bf16[4,64,1024]{2,1,0:T(8,128)(2,1)S(1)}, u32[]{:S(2)}) copy-start(bf16[4,64,1024]{2,1,0:T(8,128)(2,1)S(1)} %collective-permute-done.10) | copy-start | bytes 1572868
  85.6 24.8 %collective-permute-start.9 = (bf16[4,64,1024]{2,1,0:T(8,128)(2,1)}, bf16[4,64,1024]{2,1,0:T(8,128)(2,1)S(1)}, u32[]{:S(2)}, u32[]{:S(2)}) collective-permute-start(bf16[4,64,1024]{2,1,0:T(8,128)(2,1)} %collective-permute-done.8), channel_id=1, source_target_pairs={{0,2},{2,0},{1,3},{3,1},{4,6},{6,4},{5,7},{7,5},{8,10},{10,8},{9,1... | collective-permute-start | bytes 1572872 | tf_op jit(solution)/shard_map/ppermute | solution.py:85
  86.2 46.7 %copy-start.6 = (bf16[4,64,1024]{2,1,0:T(8,128)(2,1)}, bf16[4,64,1024]{2,1,0:T(8,128)(2,1)S(1)}, u32[]{:S(2)}) copy-start(bf16[4,64,1024]{2,1,0:T(8,128)(2,1)S(1)} %collective-permute-done.12) | copy-start | bytes 1572868
  86.2 35.4 %collective-permute-start.11 = (bf16[4,64,1024]{2,1,0:T(8,128)(2,1)S(1)}, bf16[4,64,1024]{2,1,0:T(8,128)(2,1)S(1)}, u32[]{:S(2)}, u32[]{:S(2)}) collective-permute-start(bf16[4,64,1024]{2,1,0:T(8,128)(2,1)S(1)} %collective-permute-done.10), channel_id=1, source_target_pairs={{0,2},{2,0},{1,3},{3,1},{4,6},{6,4},{5,7},{7,5},{8,10},{10,8},{9,1... | collective-permute-start | bytes 1572872 | tf_op jit(solution)/shard_map/ppermute | solution.py:85
  87.7 25.5 %copy-start.20 = (bf16[4,64,1024]{2,1,0:T(8,128)(2,1)}, bf16[4,64,1024]{2,1,0:T(8,128)(2,1)S(1)}, u32[]{:S(2)}) copy-start(bf16[4,64,1024]{2,1,0:T(8,128)(2,1)S(1)} %collective-permute-done.3) | copy-start | bytes 1572868
  87.7 45.2 %collective-permute-start.13 = (bf16[4,64,1024]{2,1,0:T(8,128)(2,1)S(1)}, bf16[4,64,1024]{2,1,0:T(8,128)(2,1)S(1)}, u32[]{:S(2)}, u32[]{:S(2)}) collective-permute-start(bf16[4,64,1024]{2,1,0:T(8,128)(2,1)S(1)} %collective-permute-done.12), channel_id=1, source_target_pairs={{0,2},{2,0},{1,3},{3,1},{4,6},{6,4},{5,7},{7,5},{8,10},{10,8},{9,1... | collective-permute-start | bytes 1572872 | tf_op jit(solution)/shard_map/ppermute | solution.py:85
  90.9 32.3 %copy-start.18 = (bf16[4,64,1024]{2,1,0:T(8,128)(2,1)}, bf16[4,64,1024]{2,1,0:T(8,128)(2,1)S(1)}, u32[]{:S(2)}) copy-start(bf16[4,64,1024]{2,1,0:T(8,128)(2,1)S(1)} %collective-permute-done.5) | copy-start | bytes 1572868
  99.2 33.7 %copy-start.16 = (bf16[4,64,1024]{2,1,0:T(8,128)(2,1)}, bf16[4,64,1024]{2,1,0:T(8,128)(2,1)S(1)}, u32[]{:S(2)}) copy-start(bf16[4,64,1024]{2,1,0:T(8,128)(2,1)S(1)} %collective-permute-done.7) | copy-start | bytes 1572868
  110.4 22.5 %copy-start.12 = (bf16[4,64,1024]{2,1,0:T(8,128)(2,1)}, bf16[4,64,1024]{2,1,0:T(8,128)(2,1)S(1)}, u32[]{:S(2)}) copy-start(bf16[4,64,1024]{2,1,0:T(8,128)(2,1)S(1)} %collective-permute-done.9) | copy-start | bytes 1572868
  121.7 11.2 %copy-start.11 = (bf16[4,64,1024]{2,1,0:T(8,128)(2,1)}, bf16[4,64,1024]{2,1,0:T(8,128)(2,1)S(1)}, u32[]{:S(2)}) copy-start(bf16[4,64,1024]{2,1,0:T(8,128)(2,1)S(1)} %collective-permute-done.11) | copy-start | bytes 1572868
  132.9 0.8 copy-start.10
  148.1 5.7 %copy-start.2 = (f32[4,8,128,8,128]{2,4,3,1,0:T(8,128)}, f32[4,8,128,8,128]{2,4,3,1,0:T(8,128)S(1)}, u32[]{:S(2)}) copy-start(f32[4,8,128,8,128]{2,4,3,1,0:T(8,128)S(1)} %get-tuple-element.18) | copy-start | bytes 50331652
  153.8 10.6 %copy-start.4 = (bf16[1024,512]{1,0:T(8,128)(2,1)S(1)}, bf16[1024,512]{1,0:T(8,128)(2,1)}, u32[]{:S(2)}) copy-start(bf16[1024,512]{1,0:T(8,128)(2,1)} %param.10) | copy-start | bytes 3145732
  153.8 10.6 %copy-start.15 = (bf16[4,64,1024]{2,1,0:T(8,128)(2,1)S(1)}, bf16[4,64,1024]{2,1,0:T(8,128)(2,1)}, u32[]{:S(2)}) copy-start(bf16[4,64,1024]{2,1,0:T(8,128)(2,1)} %copy-done.14) | copy-start | bytes 1572868
  158.7 16.8 %copy-start.19 = (bf16[4,64,1024]{2,1,0:T(8,128)(2,1)S(1)}, bf16[4,64,1024]{2,1,0:T(8,128)(2,1)}, u32[]{:S(2)}) copy-start(bf16[4,64,1024]{2,1,0:T(8,128)(2,1)} %copy-done.18) | copy-start | bytes 1572868
  159.8 11.4 %all-to-all-start = ((f32[8,8,4,128]{3,1,2,0:T(8,128)}), f32[8,8,4,128]{3,1,2,0:T(8,128)S(1)}, u32[]{:S(2)}, u32[]{:S(2)}) async-start(f32[8,8,4,128]{3,1,2,0:T(8,128)} %convolution_bitcast_fusion.2), calls=%async_computation | async-start | bytes 262144 | tf_op jit(solution)/shard_map/all_to_all | solution.py:118
  171.8 10.4 %all-to-all-start.1 = ((f32[8,8,4,128]{3,1,2,0:T(8,128)}), f32[8,8,4,128]{3,1,2,0:T(8,128)S(1)}, u32[]{:S(2)}, u32[]{:S(2)}) async-start(f32[8,8,4,128]{3,1,2,0:T(8,128)} %broadcast_in_dim.114), calls=%async_computation.1 | async-start | bytes 262144 | tf_op jit(solution)/shard_map/all_to_all | solution.py:123
  190.7 16.2 %copy-start.17 = (bf16[4,64,1024]{2,1,0:T(8,128)(2,1)S(1)}, bf16[4,64,1024]{2,1,0:T(8,128)(2,1)}, u32[]{:S(2)}) copy-start(bf16[4,64,1024]{2,1,0:T(8,128)(2,1)} %copy-done.16) | copy-start | bytes 1572868
  190.7 26.9 %copy-start.13 = (bf16[4,64,1024]{2,1,0:T(8,128)(2,1)S(1)}, bf16[4,64,1024]{2,1,0:T(8,128)(2,1)}, u32[]{:S(2)}) copy-start(bf16[4,64,1024]{2,1,0:T(8,128)(2,1)} %copy-done.12) | copy-start | bytes 1572868
  203.5 10.1 %all-to-all-start.2 = ((f32[8,8,4,128]{3,1,2,0:T(8,128)}), f32[8,8,4,128]{3,1,2,0:T(8,128)S(1)}, u32[]{:S(2)}, u32[]{:S(2)}) async-start(f32[8,8,4,128]{3,1,2,0:T(8,128)} %convolution_bitcast_fusion.1), calls=%async_computation.2 | async-start | bytes 262144 | tf_op jit(solution)/shard_map/all_to_all | solution.py:118
  214.3 10.1 %all-to-all-start.3 = ((f32[8,8,4,128]{3,1,2,0:T(8,128)}), f32[8,8,4,128]{3,1,2,0:T(8,128)S(1)}, u32[]{:S(2)}, u32[]{:S(2)}) async-start(f32[8,8,4,128]{3,1,2,0:T(8,128)} %broadcast_in_dim.115), calls=%async_computation.3 | async-start | bytes 262144 | tf_op jit(solution)/shard_map/all_to_all | solution.py:123
  236.4 20.8 %copy-start.9 = (bf16[4,64,1024]{2,1,0:T(8,128)(2,1)S(1)}, bf16[4,64,1024]{2,1,0:T(8,128)(2,1)}, u32[]{:S(2)}) copy-start(bf16[4,64,1024]{2,1,0:T(8,128)(2,1)} %copy-done.8) | copy-start | bytes 1572868
  236.4 31.8 %copy-start.7 = (bf16[4,64,1024]{2,1,0:T(8,128)(2,1)S(1)}, bf16[4,64,1024]{2,1,0:T(8,128)(2,1)}, u32[]{:S(2)}) copy-start(bf16[4,64,1024]{2,1,0:T(8,128)(2,1)} %copy-done.6) | copy-start | bytes 1572868
  253.9 10.1 %all-to-all-start.4 = ((f32[8,8,4,128]{3,1,2,0:T(8,128)}), f32[8,8,4,128]{3,1,2,0:T(8,128)S(1)}, u32[]{:S(2)}, u32[]{:S(2)}) async-start(f32[8,8,4,128]{3,1,2,0:T(8,128)} %convolution_bitcast_fusion), calls=%async_computation.4 | async-start | bytes 262144 | tf_op jit(solution)/shard_map/all_to_all | solution.py:118
  264.6 13.9 %all-to-all-start.5 = ((f32[8,8,4,128]{3,1,2,0:T(8,128)}), f32[8,8,4,128]{3,1,2,0:T(8,128)S(1)}, u32[]{:S(2)}, u32[]{:S(2)}) async-start(f32[8,8,4,128]{3,1,2,0:T(8,128)} %broadcast_in_dim.116), calls=%async_computation.5 | async-start | bytes 262144 | tf_op jit(solution)/shard_map/all_to_all | solution.py:123
  278.8 21.1 %copy-start.5 = (bf16[512,1024]{1,0:T(8,128)(2,1)S(1)}, bf16[512,1024]{1,0:T(8,128)(2,1)}, u32[]{:S(2)}) copy-start(bf16[512,1024]{1,0:T(8,128)(2,1)} %param.11) | copy-start | bytes 3145732
  278.8 51.3 %copy-start.1 = (bf16[1024,512]{1,0:T(8,128)(2,1)S(1)}, bf16[1024,512]{1,0:T(8,128)(2,1)}, u32[]{:S(2)}) copy-start(bf16[1024,512]{1,0:T(8,128)(2,1)} %param.9) | copy-start | bytes 3145732
  301.6 25.5 %collective-permute-start.14 = (bf16[1024,512]{1,0:T(8,128)(2,1)}, bf16[1024,512]{1,0:T(8,128)(2,1)}, u32[]{:S(2)}, u32[]{:S(2)}) collective-permute-start(bf16[1024,512]{1,0:T(8,128)(2,1)} %convolution_convert_fusion.1), channel_id=1, source_target_pairs={{0,2},{2,0},{1,3},{3,1},{4,6},{6,4},{5,7},{7,5},{8,10},{10,8},{9,1... | collective-permute-start | bytes 3145736 | tf_op jit(solution)/shard_map/ppermute | solution.py:144

commit v4 on v3

--- a/solution.py
+++ b/solution.py
@@ -62,6 +62,7 @@
     own_index = send_index[device_index]
     key_parts = {}
     value_parts = {}
+    previous_far = None
     for step in sorted(range(seq_devices), key=lambda k: (k != 0, -k)):
         if step == 0:
             if head_count == 2:
@@ -80,7 +81,11 @@
                 target = (device_index + step) % seq_devices
                 pairs = [(i, (i + step) % seq_devices) for i in range(seq_devices)]
             piece = jnp.take(my_rows, send_index[target], axis=0, mode="clip")
+            if step >= seq_devices // 2 and previous_far is not None:
+                piece, _ = lax.optimization_barrier((piece, previous_far))
             got = lax.ppermute(piece, ("seq", "sub"), perm=pairs)
+            if step >= seq_devices // 2:
+                previous_far = got
             if head_count == 2:
                 partner = lax.ppermute(got, "head", perm=[(0, 1), (1, 0)])
                 full = jnp.concatenate([got, partner], axis=1)

time: 331 us -> 346 us (1.045)
  waiting for transfers between devices: 114 us -> 122 us
  local copies, waits for them, and re-layouts: 37.4 us -> 41.4 us
    ppermute x7, waiting for transfers between devices: 39.9 us -> 62.5 us  [body(): got = lax.ppermute(piece, ('seq', 'sub'), perm=pairs)]
    ppermute x7, waiting for transfers between devices: 32.3 us -> 16.1 us  [body(): partner = lax.ppermute(got, 'head', perm=[(0, 1), (1, 0)])]
  transfers between devices with their start and end apart: 21 -> 21, of which waited for: 13 -> 12; matrix products, arithmetic and copies ran while one was open for 19% -> 19% of each run, Pallas kernels for 0% -> 0%
where the time goes in v4:
time: 346 us; the launch traced here: 345 us
  waiting for transfers between devices  122 us (35%)
  matrix products  78.1 us (23%)
  other arithmetic  60.6 us (18%)
  starting transfers between devices  42.3 us (12%)
  local copies, waits for them, and re-layouts  41.4 us (12%)
    ppermute x7, waiting for transfers between devices, body(): got = lax.ppermute(piece, ('seq', 'sub'), perm=pairs)  62.5 us
    reduce_sum x3, other arithmetic, body(): partial_cols = jnp.sum(weights, axis=2)  32.6 us
    ppermute x1, waiting for transfers between devices, body(): lax.ppermute(other_part.astype(jnp.bfloat16), 'head', perm=[(0, 1), (1, 0)])  24 us
    reduce_sum x3, other arithmetic, body(): weights = weights / jnp.sum(weights, axis=(3, 4), keepdims=True)  23.7 us
    dot_general x8, matrix products, body(): jnp.einsum('cjf,fhd->chjd', full, value_weights, preferred_element_type=j...  22.1 us
    dot_general x1, matrix products, body(): jnp.einsum('hbimj,bmhjd->bihd', probabilities, value_slots, preferred_ele...  20.4 us
    dot_general x8, matrix products, body(): jnp.einsum('cjf,fhd->chjd', full, key_weights, preferred_element_type=jnp...  17.8 us
    ppermute x7, waiting for transfers between devices, body(): partner = lax.ppermute(got, 'head', perm=[(0, 1), (1, 0)])  16.1 us
  transfers between devices with their start and end apart: 21, of which 12 were waited for; matrix products, arithmetic and copies ran while one was open for 19% of the time, Pallas kernels for 0%

profile of v4, /device:TPU:0, one launch (start us, length us, event | category | flops | bytes accessed | tf_op | source)
XLA Modules:
  0.0 344.7 jit_solution(13049692171494432103)
XLA Ops:
  7.6 2.6 collective-permute-start.2
  13.1 3.7 %collective-permute-start.6 = (bf16[4,64,1024]{2,1,0:T(8,128)(2,1)}, bf16[4,64,1024]{2,1,0:T(8,128)(2,1)}, u32[]{:S(2)}, u32[]{:S(2)}) collective-permute-start(bf16[4,64,1024]{2,1,0:T(8,128)(2,1)} %gather_fusion.7), channel_id=1, source_target_pairs={{0,13},{1,12},{4,9},{5,8},{8,5},{9,4},{12,1},{13,0},{2,15},{3,14},... | collective-permute-start | bytes 1572872 | tf_op jit(solution)/shard_map/ppermute | solution.py:86
  18.9 4.1 %convolution_convert_fusion = bf16[1024,512]{1,0:T(8,128)(2,1)} fusion(bf16[1024,1024]{1,0:T(8,128)(2,1)} %param.7, bf16[1024,512]{1,0:T(8,128)(2,1)} %param.8), kind=kOutput, calls=%fused_computation.35 | convolution fusion | flops 1074266112 | bytes 4194304 | tf_op jit(solution)/shard_map/dot_general | solution.py:26
  22.9 24.4 %collective-permute-done.6 = bf16[4,64,1024]{2,1,0:T(8,128)(2,1)} collective-permute-done((bf16[4,64,1024]{2,1,0:T(8,128)(2,1)}, bf16[4,64,1024]{2,1,0:T(8,128)(2,1)}, u32[]{:S(2)}, u32[]{:S(2)}) %collective-permute-start.6) | collective-permute-done | bytes 524320 | tf_op jit(solution)/shard_map/ppermute | solution.py:86
  51.8 2.4 reshape.137
  55.8 2.3 gather_fusion
  59.7 4.0 %collective-permute-done.7 = bf16[4,64,1024]{2,1,0:T(8,128)(2,1)} collective-permute-done((bf16[4,64,1024]{2,1,0:T(8,128)(2,1)}, bf16[4,64,1024]{2,1,0:T(8,128)(2,1)}, u32[]{:S(2)}, u32[]{:S(2)}) %collective-permute-start.7) | collective-permute-done | bytes 524320 | tf_op jit(solution)/shard_map/ppermute | solution.py:86
  63.7 2.7 collective-permute-start.8
  66.4 2.8 fusion.27
  74.3 15.1 %collective-permute-done.8 = bf16[4,64,1024]{2,1,0:T(8,128)(2,1)S(1)} collective-permute-done((bf16[4,64,1024]{2,1,0:T(8,128)(2,1)}, bf16[4,64,1024]{2,1,0:T(8,128)(2,1)S(1)}, u32[]{:S(2)}, u32[]{:S(2)}) %collective-permute-start.8) | collective-permute-done | bytes 524320 | tf_op jit(solution)/shard_map/ppermute | solution.py:86
  91.5 3.0 fusion.29
  94.5 2.6 fusion.45
  97.1 19.0 %collective-permute-done.9 = bf16[4,64,1024]{2,1,0:T(8,128)(2,1)S(1)} collective-permute-done((bf16[4,64,1024]{2,1,0:T(8,128)(2,1)S(1)}, bf16[4,64,1024]{2,1,0:T(8,128)(2,1)S(1)}, u32[]{:S(2)}, u32[]{:S(2)}) %collective-permute-start.9) | collective-permute-done | bytes 524320 | tf_op jit(solution)/shard_map/ppermute | solution.py:86
  117.4 2.5 fusion.47
  121.4 2.7 fusion.49
  124.2 6.7 %collective-permute-done.10 = bf16[4,64,1024]{2,1,0:T(8,128)(2,1)S(1)} collective-permute-done((bf16[4,64,1024]{2,1,0:T(8,128)(2,1)S(1)}, bf16[4,64,1024]{2,1,0:T(8,128)(2,1)S(1)}, u32[]{:S(2)}, u32[]{:S(2)}) %collective-permute-start.10) | collective-permute-done | bytes 524320 | tf_op jit(solution)/shard_map/ppermute | solution.py:90
  132.4 9.4 %collective-permute-done.11 = bf16[4,64,1024]{2,1,0:T(8,128)(2,1)S(1)} collective-permute-done((bf16[4,64,1024]{2,1,0:T(8,128)(2,1)S(1)}, bf16[4,64,1024]{2,1,0:T(8,128)(2,1)S(1)}, u32[]{:S(2)}, u32[]{:S(2)}) %collective-permute-start.11) | collective-permute-done | bytes 524320 | tf_op jit(solution)/shard_map/ppermute | solution.py:90
  143.3 2.7 fusion.55
  146.9 2.6 fusion.57
  149.4 7.8 %gather_fusion.9 = bf16[64,4,128,128]{3,2,1,0:T(8,128)(2,1)} fusion(bf16[32,4,128,128]{3,2,1,0:T(8,128)(2,1)} %fusion.57, s32[1024]{0:T(1024)S(1)} %pad_clamp_fusion), kind=kCustom, calls=%fused_computation.9 | custom fusion | bytes 16777472 | tf_op jit(solution)/shard_map/jit(_take)/gather | solution.py:103
  157.2 5.1 %select_reduce_fusion = (f32[4,8,128]{2,1,0:T(8,128)S(1)}, f32[4,8,128,8,128]{2,4,3,1,0:T(8,128)S(1)}) fusion(pred[8,8]{1,0:T(8,128)(4,1)S(1)} %constant_dynamic-slice_fusion, bf16[8,8,4,128,128]{4,3,2,1,0:T(8,128)(2,1)} %bitcast.305, bf16[8,128,4,128,1]{3,2,1,0,4:T(4,128)(2,1)S(1)} %bitcast.307), kind=kOutput, calls=%fused_computation.20 | convolution fusion | flops 1086320640 | bytes 26230848 | tf_op jit(solution)/shard_map/bihd,bmhjd->hbimj/dot_general | solution.py:110
  162.4 3.5 %fusion.147 = f32[4,8,128]{2,1,0:T(8,128)S(1)} fusion(f32[4,8,128]{2,1,0:T(8,128)S(1)} %get-tuple-element.23, f32[4,8,128,8,128]{2,4,3,1,0:T(8,128)S(1)} %get-tuple-element.24, pred[8,8]{1,0:T(8,128)(4,1)S(1)} %constant_dynamic-slice_fusion), kind=kLoop, calls=%fused_computation.220 | loop fusion | flops 16773120 | bytes 16810048 | tf_op jit(solution)/shard_map/reduce_sum | solution.py:118
  168.1 4.9 %divide_reduce_fusion = f32[4,8,8,128]{3,2,1,0:T(8,128)S(1)} fusion(f32[4,8,128]{2,1,0:T(8,128)S(1)} %fusion.147, f32[4,8,128]{2,1,0:T(8,128)S(1)} %get-tuple-element.23, f32[4,8,128,8,128]{2,4,3,1,0:T(8,128)S(1)} %get-tuple-element.24, pred[8,8]{1,0:T(8,128)(4,1)S(1)} %constant_dynamic-slice_fusion), kind=kLoop, calls=%fused_computation.21 | loop fusion | flops 20938752 | bytes 16941120 | tf_op jit(solution)/shard_map/reduce_sum | solution.py:119
  174.0 3.4 all-to-all-start
  177.4 2.9 fusion.31
  180.3 3.8 %all-to-all-done = f32[8,8,4,128]{3,1,2,0:T(8,128)S(1)} async-done(((f32[8,8,4,128]{3,1,2,0:T(8,128)}), f32[8,8,4,128]{3,1,2,0:T(8,128)S(1)}, u32[]{:S(2)}, u32[]{:S(2)}) %all-to-all-start) | async-done | bytes 131104 | tf_op jit(solution)/shard_map/all_to_all | solution.py:123
  184.8 3.6 %all-to-all-start.1 = ((f32[8,8,4,128]{3,1,2,0:T(8,128)}), f32[8,8,4,128]{3,1,2,0:T(8,128)S(1)}, u32[]{:S(2)}, u32[]{:S(2)}) async-start(f32[8,8,4,128]{3,1,2,0:T(8,128)} %broadcast_in_dim.114), calls=%async_computation.1 | async-start | bytes 262144 | tf_op jit(solution)/shard_map/all_to_all | solution.py:128
  188.4 2.9 fusion.33
  191.3 3.6 %all-to-all-done.1 = f32[8,8,4,128]{3,1,2,0:T(8,128)S(1)} async-done(((f32[8,8,4,128]{3,1,2,0:T(8,128)}), f32[8,8,4,128]{3,1,2,0:T(8,128)S(1)}, u32[]{:S(2)}, u32[]{:S(2)}) %all-to-all-start.1) | async-done | bytes 131104 | tf_op jit(solution)/shard_map/all_to_all | solution.py:128
  195.1 8.5 %fusion.8 = f32[4,8,128]{2,1,0:T(8,128)S(1)} fusion(f32[4,8,8,128]{3,2,1,0:T(8,128)S(1)} %fusion.60, f32[4,8,128]{2,1,0:T(8,128)S(1)} %fusion.147, f32[4,8,128]{2,1,0:T(8,128)S(1)} %get-tuple-element.23, f32[4,8,128,8,128]{2,4,3,1,0:T(8,128)} %copy-done.2, pred[8,8]{1,0:T(8,128)(4,1)S(1)} %constant_dynamic-slice_fusion), kind=kLoop, calls=%fused_computation.23 | loop fusion | flops 25161728 | bytes 16957504 | tf_op jit(solution)/shard_map/reduce_sum | solution.py:118
  205.8 11.3 %fusion.9 = f32[4,8,8,128]{3,2,1,0:T(8,128)S(1)} fusion(f32[4,8,128]{2,1,0:T(8,128)S(1)} %fusion.8, f32[4,8,8,128]{3,2,1,0:T(8,128)S(1)} %fusion.60, f32[4,8,128]{2,1,0:T(8,128)S(1)} %fusion.147, f32[4,8,128]{2,1,0:T(8,128)S(1)} %get-tuple-element.23, f32[4,8,128,8,128]{2,4,3,1,0:T(8,128)S(1)} %copy-done.3, pred[8,8]{1,0:T(8,128)(4,1)S(1)} %constant_dynamic-slice_fusion), kind=kLoop, calls=%fused_computation.24 | loop fusion | flops 29327360 | bytes 17088576 | tf_op jit(solution)/shard_map/reduce_sum | solution.py:119
  218.2 3.4 all-to-all-start.2
  221.6 2.8 fusion.35
  224.4 3.9 %all-to-all-done.2 = f32[8,8,4,128]{3,1,2,0:T(8,128)S(1)} async-done(((f32[8,8,4,128]{3,1,2,0:T(8,128)}), f32[8,8,4,128]{3,1,2,0:T(8,128)S(1)}, u32[]{:S(2)}, u32[]{:S(2)}) %all-to-all-start.2) | async-done | bytes 131104 | tf_op jit(solution)/shard_map/all_to_all | solution.py:123
  229.0 3.4 all-to-all-start.3
  232.3 2.6 fusion.37
  234.9 4.1 %all-to-all-done.3 = f32[8,8,4,128]{3,1,2,0:T(8,128)S(1)} async-done(((f32[8,8,4,128]{3,1,2,0:T(8,128)}), f32[8,8,4,128]{3,1,2,0:T(8,128)S(1)}, u32[]{:S(2)}, u32[]{:S(2)}) %all-to-all-start.3) | async-done | bytes 131104 | tf_op jit(solution)/shard_map/all_to_all | solution.py:128
  239.3 11.8 %fusion.10 = f32[4,8,128]{2,1,0:T(8,128)S(1)} fusion(f32[4,8,8,128]{3,2,1,0:T(8,128)S(1)} %fusion.59, f32[4,8,128]{2,1,0:T(8,128)S(1)} %fusion.8, f32[4,8,8,128]{3,2,1,0:T(8,128)S(1)} %fusion.60, f32[4,8,128]{2,1,0:T(8,128)S(1)} %fusion.147, f32[4,8,128]{2,1,0:T(8,128)S(1)} %get-tuple-element.23, f32[4,8,128,8,128]{2,4,3,1,0:T(8,128)} %copy-done.2, ...), kind=kLoop, calls=%fused_computation.25 | loop fusion | flops 33550336 | bytes 17104960 | tf_op jit(solution)/shard_map/reduce_sum | solution.py:118
  251.1 16.3 %fusion.11 = f32[4,8,8,128]{3,2,1,0:T(8,128)S(1)} fusion(f32[4,8,128]{2,1,0:T(8,128)S(1)} %fusion.10, f32[4,8,8,128]{3,2,1,0:T(8,128)S(1)} %fusion.59, f32[4,8,128]{2,1,0:T(8,128)S(1)} %fusion.8, f32[4,8,8,128]{3,2,1,0:T(8,128)S(1)} %fusion.60, f32[4,8,128]{2,1,0:T(8,128)S(1)} %fusion.147, f32[4,8,128]{2,1,0:T(8,128)S(1)} %get-tuple-element.23, ...), kind=kLoop, calls=%fused_computation.26 | loop fusion | flops 37715968 | bytes 17236032 | tf_op jit(solution)/shard_map/reduce_sum | solution.py:119
  268.5 3.4 all-to-all-start.4
  271.9 2.7 fusion.39
  274.6 4.0 %all-to-all-done.4 = f32[8,8,4,128]{3,1,2,0:T(8,128)S(1)} async-done(((f32[8,8,4,128]{3,1,2,0:T(8,128)}), f32[8,8,4,128]{3,1,2,0:T(8,128)S(1)}, u32[]{:S(2)}, u32[]{:S(2)}) %all-to-all-start.4) | async-done | bytes 131104 | tf_op jit(solution)/shard_map/all_to_all | solution.py:123
  279.3 3.6 %all-to-all-start.5 = ((f32[8,8,4,128]{3,1,2,0:T(8,128)}), f32[8,8,4,128]{3,1,2,0:T(8,128)S(1)}, u32[]{:S(2)}, u32[]{:S(2)}) async-start(f32[8,8,4,128]{3,1,2,0:T(8,128)} %broadcast_in_dim.116), calls=%async_computation.5 | async-start | bytes 262144 | tf_op jit(solution)/shard_map/all_to_all | solution.py:128
  282.9 2.6 fusion.41
  285.5 7.7 %gather_fusion.8 = bf16[64,4,128,128]{3,2,1,0:T(8,128)(2,1)} fusion(bf16[32,4,128,128]{3,2,1,0:T(8,128)(2,1)} %fusion.41, s32[1024]{0:T(1024)S(1)} %pad_clamp_fusion), kind=kCustom, calls=%fused_computation.8 | custom fusion | bytes 16777472 | tf_op jit(solution)/shard_map/jit(_take)/gather | solution.py:106
  293.5 20.4 %fusion.21 = bf16[8,128,4,128]{1,3,2,0:T(8,128)(2,1)S(1)} fusion(bf16[8,8,4,128,128]{4,3,2,1,0:T(8,128)(2,1)} %bitcast.304, f32[4,8,8,128]{3,2,1,0:T(8,128)S(1)} %fusion.58, f32[4,8,128]{2,1,0:T(8,128)S(1)} %fusion.10, f32[4,8,8,128]{3,2,1,0:T(8,128)S(1)} %fusion.59, f32[4,8,128]{2,1,0:T(8,128)S(1)} %fusion.8, f32[4,8,8,128]{3,2,1,0:T(8,128)S(1)} %fusion.60, ...), kind=kOutput, calls=%fused_computation.37 | convolution fusion | flops 1116209152 | bytes 26673216 | tf_op jit(solution)/shard_map/hbimj,bmhjd->bihd/dot_general | solution.py:134
  317.7 24.0 %collective-permute-done.14 = bf16[1024,512]{1,0:T(8,128)(2,1)} collective-permute-done((bf16[1024,512]{1,0:T(8,128)(2,1)}, bf16[1024,512]{1,0:T(8,128)(2,1)}, u32[]{:S(2)}, u32[]{:S(2)}) %collective-permute-start.14) | collective-permute-done | bytes 1048608 | tf_op jit(solution)/shard_map/ppermute | solution.py:149
  341.8 3.0 add_convert_fusion
  (123 shorter events, 48.5 us)
Async XLA Ops:
  0.0 69.2 %copy-start = (bf16[1024,512]{1,0:T(8,128)(2,1)S(1)}, bf16[1024,512]{1,0:T(8,128)(2,1)}, u32[]{:S(2)}) copy-start(bf16[1024,512]{1,0:T(8,128)(2,1)} %param.9) | copy-start | bytes 3145732
  0.0 16.7 %copy-start.6 = (s32[64,8]{0,1:T(8,128)S(1)}, s32[64,8]{0,1:T(8,128)}, u32[]{:S(2)}) copy-start(s32[64,8]{0,1:T(8,128)} %param.12) | copy-start | bytes 6148
  5.7 52.4 %collective-permute-start = (bf16[4,64,1024]{2,1,0:T(8,128)(2,1)}, bf16[4,64,1024]{2,1,0:T(8,128)(2,1)}, u32[]{:S(2)}, u32[]{:S(2)}) collective-permute-start(bf16[4,64,1024]{2,1,0:T(8,128)(2,1)} %gather_fusion.1), channel_id=1, source_target_pairs={{0,1},{1,0},{4,5},{5,4},{8,9},{9,8},{12,13},{13,12},{2,3},{3,2},{6... | collective-permute-start | bytes 1572872 | tf_op jit(solution)/shard_map/ppermute | solution.py:86
  7.6 64.7 %collective-permute-start.2 = (bf16[4,64,1024]{2,1,0:T(8,128)(2,1)}, bf16[4,64,1024]{2,1,0:T(8,128)(2,1)}, u32[]{:S(2)}, u32[]{:S(2)}) collective-permute-start(bf16[4,64,1024]{2,1,0:T(8,128)(2,1)} %gather_fusion.2), channel_id=1, source_target_pairs={{0,4},{1,5},{4,0},{5,1},{8,12},{9,13},{12,8},{13,9},{2,6},{3,7},{6... | collective-permute-start | bytes 1572872 | tf_op jit(solution)/shard_map/ppermute | solution.py:86
  11.6 61.2 %collective-permute-start.4 = (bf16[4,64,1024]{2,1,0:T(8,128)(2,1)}, bf16[4,64,1024]{2,1,0:T(8,128)(2,1)}, u32[]{:S(2)}, u32[]{:S(2)}) collective-permute-start(bf16[4,64,1024]{2,1,0:T(8,128)(2,1)} %gather_fusion.3), channel_id=1, source_target_pairs={{0,5},{1,4},{4,1},{5,0},{8,13},{9,12},{12,9},{13,8},{2,7},{3,6},{6... | collective-permute-start | bytes 1572872 | tf_op jit(solution)/shard_map/ppermute | solution.py:86
  13.1 34.3 %collective-permute-start.6 = (bf16[4,64,1024]{2,1,0:T(8,128)(2,1)}, bf16[4,64,1024]{2,1,0:T(8,128)(2,1)}, u32[]{:S(2)}, u32[]{:S(2)}) collective-permute-start(bf16[4,64,1024]{2,1,0:T(8,128)(2,1)} %gather_fusion.7), channel_id=1, source_target_pairs={{0,13},{1,12},{4,9},{5,8},{8,5},{9,4},{12,1},{13,0},{2,15},{3,14},... | collective-permute-start | bytes 1572872 | tf_op jit(solution)/shard_map/ppermute | solution.py:86
  47.4 16.3 %collective-permute-start.7 = (bf16[4,64,1024]{2,1,0:T(8,128)(2,1)}, bf16[4,64,1024]{2,1,0:T(8,128)(2,1)}, u32[]{:S(2)}, u32[]{:S(2)}) collective-permute-start(bf16[4,64,1024]{2,1,0:T(8,128)(2,1)} %gather_fusion.6), channel_id=1, source_target_pairs={{0,12},{1,13},{4,8},{5,9},{8,4},{9,5},{12,0},{13,1},{2,14},{3,15},... | collective-permute-start | bytes 1572872 | tf_op jit(solution)/shard_map/ppermute | solution.py:86
  55.8 35.0 %copy-start.5 = (bf16[4,64,1024]{2,1,0:T(8,128)(2,1)S(1)}, bf16[4,64,1024]{2,1,0:T(8,128)(2,1)}, u32[]{:S(2)}) copy-start(bf16[4,64,1024]{2,1,0:T(8,128)(2,1)} %gather_fusion.4) | copy-start | bytes 1572868
  58.2 32.7 %collective-permute-start.1 = (bf16[4,64,1024]{2,1,0:T(8,128)(2,1)}, bf16[4,64,1024]{2,1,0:T(8,128)(2,1)S(1)}, u32[]{:S(2)}, u32[]{:S(2)}) collective-permute-start(bf16[4,64,1024]{2,1,0:T(8,128)(2,1)} %collective-permute-done), channel_id=1, source_target_pairs={{0,2},{2,0},{1,3},{3,1},{4,6},{6,4},{5,7},{7,5},{8,10},{10,8},{9,1... | collective-permute-start | bytes 1572872 | tf_op jit(solution)/shard_map/ppermute | solution.py:90
  63.7 25.7 %collective-permute-start.8 = (bf16[4,64,1024]{2,1,0:T(8,128)(2,1)}, bf16[4,64,1024]{2,1,0:T(8,128)(2,1)S(1)}, u32[]{:S(2)}, u32[]{:S(2)}) collective-permute-start(bf16[4,64,1024]{2,1,0:T(8,128)(2,1)} %gather_fusion.5), channel_id=1, source_target_pairs={{0,9},{1,8},{4,13},{5,12},{8,1},{9,0},{12,5},{13,4},{2,11},{3,10},... | collective-permute-start | bytes 1572872 | tf_op jit(solution)/shard_map/ppermute | solution.py:86
  70.8 75.3 %collective-permute-start.13 = (bf16[4,64,1024]{2,1,0:T(8,128)(2,1)}, bf16[4,64,1024]{2,1,0:T(8,128)(2,1)S(1)}, u32[]{:S(2)}, u32[]{:S(2)}) collective-permute-start(bf16[4,64,1024]{2,1,0:T(8,128)(2,1)} %collective-permute-done.6), channel_id=1, source_target_pairs={{0,2},{2,0},{1,3},{3,1},{4,6},{6,4},{5,7},{7,5},{8,10},{10,8},{9,1... | collective-permute-start | bytes 1572872 | tf_op jit(solution)/shard_map/ppermute | solution.py:90
  72.3 44.3 %collective-permute-start.3 = (bf16[4,64,1024]{2,1,0:T(8,128)(2,1)}, bf16[4,64,1024]{2,1,0:T(8,128)(2,1)S(1)}, u32[]{:S(2)}, u32[]{:S(2)}) collective-permute-start(bf16[4,64,1024]{2,1,0:T(8,128)(2,1)} %collective-permute-done.2), channel_id=1, source_target_pairs={{0,2},{2,0},{1,3},{3,1},{4,6},{6,4},{5,7},{7,5},{8,10},{10,8},{9,1... | collective-permute-start | bytes 1572872 | tf_op jit(solution)/shard_map/ppermute | solution.py:90
  72.8 48.6 %collective-permute-start.5 = (bf16[4,64,1024]{2,1,0:T(8,128)(2,1)}, bf16[4,64,1024]{2,1,0:T(8,128)(2,1)S(1)}, u32[]{:S(2)}, u32[]{:S(2)}) collective-permute-start(bf16[4,64,1024]{2,1,0:T(8,128)(2,1)} %collective-permute-done.4), channel_id=1, source_target_pairs={{0,2},{2,0},{1,3},{3,1},{4,6},{6,4},{5,7},{7,5},{8,10},{10,8},{9,1... | collective-permute-start | bytes 1572872 | tf_op jit(solution)/shard_map/ppermute | solution.py:90
  89.4 52.4 %copy-start.11 = (bf16[4,64,1024]{2,1,0:T(8,128)(2,1)}, bf16[4,64,1024]{2,1,0:T(8,128)(2,1)S(1)}, u32[]{:S(2)}) copy-start(bf16[4,64,1024]{2,1,0:T(8,128)(2,1)S(1)} %collective-permute-done.8) | copy-start | bytes 1572868
  89.4 53.9 %collective-permute-start.12 = (bf16[4,64,1024]{2,1,0:T(8,128)(2,1)}, bf16[4,64,1024]{2,1,0:T(8,128)(2,1)S(1)}, u32[]{:S(2)}, u32[]{:S(2)}) collective-permute-start(bf16[4,64,1024]{2,1,0:T(8,128)(2,1)} %collective-permute-done.7), channel_id=1, source_target_pairs={{0,2},{2,0},{1,3},{3,1},{4,6},{6,4},{5,7},{7,5},{8,10},{10,8},{9,1... | collective-permute-start | bytes 1572872 | tf_op jit(solution)/shard_map/ppermute | solution.py:90
  90.9 25.2 %collective-permute-start.9 = (bf16[4,64,1024]{2,1,0:T(8,128)(2,1)S(1)}, bf16[4,64,1024]{2,1,0:T(8,128)(2,1)S(1)}, u32[]{:S(2)}, u32[]{:S(2)}) collective-permute-start(bf16[4,64,1024]{2,1,0:T(8,128)(2,1)S(1)} %copy-done.5), channel_id=1, source_target_pairs={{0,8},{1,9},{4,12},{5,13},{8,0},{9,1},{12,4},{13,5},{2,10},{3,11},... | collective-permute-start | bytes 1572872 | tf_op jit(solution)/shard_map/ppermute | solution.py:86
  116.1 27.2 %copy-start.14 = (bf16[4,64,1024]{2,1,0:T(8,128)(2,1)}, bf16[4,64,1024]{2,1,0:T(8,128)(2,1)S(1)}, u32[]{:S(2)}) copy-start(bf16[4,64,1024]{2,1,0:T(8,128)(2,1)S(1)} %collective-permute-done.9) | copy-start | bytes 1572868
  116.1 14.8 %collective-permute-start.10 = (bf16[4,64,1024]{2,1,0:T(8,128)(2,1)S(1)}, bf16[4,64,1024]{2,1,0:T(8,128)(2,1)S(1)}, u32[]{:S(2)}, u32[]{:S(2)}) collective-permute-start(bf16[4,64,1024]{2,1,0:T(8,128)(2,1)S(1)} %collective-permute-done.9), channel_id=1, source_target_pairs={{0,2},{2,0},{1,3},{3,1},{4,6},{6,4},{5,7},{7,5},{8,10},{10,8},{9,1... | collective-permute-start | bytes 1572872 | tf_op jit(solution)/shard_map/ppermute | solution.py:90
  116.6 0.8 copy-start.19
  119.9 21.8 %collective-permute-start.11 = (bf16[4,64,1024]{2,1,0:T(8,128)(2,1)S(1)}, bf16[4,64,1024]{2,1,0:T(8,128)(2,1)S(1)}, u32[]{:S(2)}, u32[]{:S(2)}) collective-permute-start(bf16[4,64,1024]{2,1,0:T(8,128)(2,1)S(1)} %collective-permute-done.8), channel_id=1, source_target_pairs={{0,2},{2,0},{1,3},{3,1},{4,6},{6,4},{5,7},{7,5},{8,10},{10,8},{9,1... | collective-permute-start | bytes 1572872 | tf_op jit(solution)/shard_map/ppermute | solution.py:90
  121.4 24.6 %copy-start.15 = (bf16[4,64,1024]{2,1,0:T(8,128)(2,1)}, bf16[4,64,1024]{2,1,0:T(8,128)(2,1)S(1)}, u32[]{:S(2)}) copy-start(bf16[4,64,1024]{2,1,0:T(8,128)(2,1)S(1)} %collective-permute-done.5) | copy-start | bytes 1572868
  130.9 15.2 %copy-start.18 = (bf16[4,64,1024]{2,1,0:T(8,128)(2,1)}, bf16[4,64,1024]{2,1,0:T(8,128)(2,1)S(1)}, u32[]{:S(2)}) copy-start(bf16[4,64,1024]{2,1,0:T(8,128)(2,1)S(1)} %collective-permute-done.10) | copy-start | bytes 1572868
  141.8 4.3 %copy-start.17 = (bf16[4,64,1024]{2,1,0:T(8,128)(2,1)}, bf16[4,64,1024]{2,1,0:T(8,128)(2,1)S(1)}, u32[]{:S(2)}) copy-start(bf16[4,64,1024]{2,1,0:T(8,128)(2,1)S(1)} %collective-permute-done.11) | copy-start | bytes 1572868
  143.3 2.8 copy-start.13
  146.1 0.8 copy-start.9
  149.4 7.8 %copy-start.4 = (bf16[8,128,4,128]{3,2,1,0:T(4,128)(2,1)S(1)}, bf16[8,128,4,128]{3,2,1,0:T(4,128)(2,1)}, u32[]{:S(2)}) copy-start(bf16[8,128,4,128]{3,2,1,0:T(4,128)(2,1)} %reshape.137) | copy-start | bytes 3145732
  162.4 5.7 %copy-start.2 = (f32[4,8,128,8,128]{2,4,3,1,0:T(8,128)}, f32[4,8,128,8,128]{2,4,3,1,0:T(8,128)S(1)}, u32[]{:S(2)}) copy-start(f32[4,8,128,8,128]{2,4,3,1,0:T(8,128)S(1)} %get-tuple-element.24) | copy-start | bytes 50331652
  168.1 9.4 %copy-start.20 = (bf16[4,64,1024]{2,1,0:T(8,128)(2,1)S(1)}, bf16[4,64,1024]{2,1,0:T(8,128)(2,1)}, u32[]{:S(2)}) copy-start(bf16[4,64,1024]{2,1,0:T(8,128)(2,1)} %copy-done.19) | copy-start | bytes 1572868
  168.1 20.3 %copy-start.16 = (bf16[4,64,1024]{2,1,0:T(8,128)(2,1)S(1)}, bf16[4,64,1024]{2,1,0:T(8,128)(2,1)}, u32[]{:S(2)}) copy-start(bf16[4,64,1024]{2,1,0:T(8,128)(2,1)} %copy-done.15) | copy-start | bytes 1572868
  174.0 10.1 %all-to-all-start = ((f32[8,8,4,128]{3,1,2,0:T(8,128)}), f32[8,8,4,128]{3,1,2,0:T(8,128)S(1)}, u32[]{:S(2)}, u32[]{:S(2)}) async-start(f32[8,8,4,128]{3,1,2,0:T(8,128)} %convolution_bitcast_fusion.2), calls=%async_computation | async-start | bytes 262144 | tf_op jit(solution)/shard_map/all_to_all | solution.py:123
  184.8 10.1 %all-to-all-start.1 = ((f32[8,8,4,128]{3,1,2,0:T(8,128)}), f32[8,8,4,128]{3,1,2,0:T(8,128)S(1)}, u32[]{:S(2)}, u32[]{:S(2)}) async-start(f32[8,8,4,128]{3,1,2,0:T(8,128)} %broadcast_in_dim.114), calls=%async_computation.1 | async-start | bytes 262144 | tf_op jit(solution)/shard_map/all_to_all | solution.py:128
  195.1 10.7 %copy-start.3 = (f32[4,8,128,8,128]{2,4,3,1,0:T(8,128)S(1)}, f32[4,8,128,8,128]{2,4,3,1,0:T(8,128)}, u32[]{:S(2)}) copy-start(f32[4,8,128,8,128]{2,4,3,1,0:T(8,128)} %copy-done.2) | copy-start | bytes 50331652
  205.8 15.8 %copy-start.7 = (bf16[1024,512]{1,0:T(8,128)(2,1)S(1)}, bf16[1024,512]{1,0:T(8,128)(2,1)}, u32[]{:S(2)}) copy-start(bf16[1024,512]{1,0:T(8,128)(2,1)} %param.10) | copy-start | bytes 3145732
  205.8 26.5 %copy-start.12 = (bf16[4,64,1024]{2,1,0:T(8,128)(2,1)S(1)}, bf16[4,64,1024]{2,1,0:T(8,128)(2,1)}, u32[]{:S(2)}) copy-start(bf16[4,64,1024]{2,1,0:T(8,128)(2,1)} %copy-done.11) | copy-start | bytes 1572868
  218.2 10.1 %all-to-all-start.2 = ((f32[8,8,4,128]{3,1,2,0:T(8,128)}), f32[8,8,4,128]{3,1,2,0:T(8,128)S(1)}, u32[]{:S(2)}, u32[]{:S(2)}) async-start(f32[8,8,4,128]{3,1,2,0:T(8,128)} %convolution_bitcast_fusion.1), calls=%async_computation.2 | async-start | bytes 262144 | tf_op jit(solution)/shard_map/all_to_all | solution.py:123
  229.0 10.1 %all-to-all-start.3 = ((f32[8,8,4,128]{3,1,2,0:T(8,128)}), f32[8,8,4,128]{3,1,2,0:T(8,128)S(1)}, u32[]{:S(2)}, u32[]{:S(2)}) async-start(f32[8,8,4,128]{3,1,2,0:T(8,128)} %broadcast_in_dim.115), calls=%async_computation.3 | async-start | bytes 262144 | tf_op jit(solution)/shard_map/all_to_all | solution.py:128
  251.1 31.8 %copy-start.10 = (bf16[4,64,1024]{2,1,0:T(8,128)(2,1)S(1)}, bf16[4,64,1024]{2,1,0:T(8,128)(2,1)}, u32[]{:S(2)}) copy-start(bf16[4,64,1024]{2,1,0:T(8,128)(2,1)} %copy-done.9) | copy-start | bytes 1572868
  268.5 10.1 %all-to-all-start.4 = ((f32[8,8,4,128]{3,1,2,0:T(8,128)}), f32[8,8,4,128]{3,1,2,0:T(8,128)S(1)}, u32[]{:S(2)}, u32[]{:S(2)}) async-start(f32[8,8,4,128]{3,1,2,0:T(8,128)} %convolution_bitcast_fusion), calls=%async_computation.4 | async-start | bytes 262144 | tf_op jit(solution)/shard_map/all_to_all | solution.py:123
  279.3 13.9 %all-to-all-start.5 = ((f32[8,8,4,128]{3,1,2,0:T(8,128)}), f32[8,8,4,128]{3,1,2,0:T(8,128)S(1)}, u32[]{:S(2)}, u32[]{:S(2)}) async-start(f32[8,8,4,128]{3,1,2,0:T(8,128)} %broadcast_in_dim.116), calls=%async_computation.5 | async-start | bytes 262144 | tf_op jit(solution)/shard_map/all_to_all | solution.py:128
  293.4 21.1 %copy-start.8 = (bf16[512,1024]{1,0:T(8,128)(2,1)S(1)}, bf16[512,1024]{1,0:T(8,128)(2,1)}, u32[]{:S(2)}) copy-start(bf16[512,1024]{1,0:T(8,128)(2,1)} %param.11) | copy-start | bytes 3145732
  293.5 51.3 %copy-start.1 = (bf16[1024,512]{1,0:T(8,128)(2,1)S(1)}, bf16[1024,512]{1,0:T(8,128)(2,1)}, u32[]{:S(2)}) copy-start(bf16[1024,512]{1,0:T(8,128)(2,1)} %param.9) | copy-start | bytes 3145732
  316.3 25.5 %collective-permute-start.14 = (bf16[1024,512]{1,0:T(8,128)(2,1)}, bf16[1024,512]{1,0:T(8,128)(2,1)}, u32[]{:S(2)}, u32[]{:S(2)}) collective-permute-start(bf16[1024,512]{1,0:T(8,128)(2,1)} %convolution_convert_fusion.1), channel_id=1, source_target_pairs={{0,2},{2,0},{1,3},{3,1},{4,6},{6,4},{5,7},{7,5},{8,10},{10,8},{9,1... | collective-permute-start | bytes 3145736 | tf_op jit(solution)/shard_map/ppermute | solution.py:149

commit v5 on v3

--- a/solution.py
+++ b/solution.py
@@ -108,10 +108,11 @@
     valid_mask = my_valid[None, :, None, :, None]
     row_max = jnp.max(jnp.where(valid_mask, scores, -1e30), axis=(3, 4), keepdims=True)
     weights = jnp.where(valid_mask, jnp.exp(scores - row_max), 0.0)
+    column_scale = jnp.ones(weights.shape[:2] + weights.shape[3:], jnp.float32)
     onehot = matches.astype(jnp.float32)
     for round_number in range(BALANCING_ROUNDS):
-        weights = weights / jnp.sum(weights, axis=(3, 4), keepdims=True)
-        partial_cols = jnp.sum(weights, axis=2)
+        row_scale = 1.0 / jnp.sum(weights * column_scale[:, :, None], axis=(3, 4))
+        partial_cols = column_scale * jnp.sum(weights * row_scale[:, :, :, None, None], axis=2)
         column_complete = jnp.einsum(
             "bmt,hbmj->thj", onehot, partial_cols, precision=lax.Precision.HIGHEST
         ).reshape(seq_devices, local_blocks, heads_here, TILE)
@@ -124,8 +125,10 @@
             spread, ("seq", "sub"), split_axis=0, concat_axis=0, tiled=True
         ).reshape(block_total, heads_here, TILE)
         per_slot = jnp.einsum("bmt,thj->hbmj", onehot, totals, precision=lax.Precision.HIGHEST)
-        weights = weights / jnp.maximum(per_slot[:, :, None, :, :], COLUMN_FLOOR)
-    probabilities = weights.astype(jnp.bfloat16)
+        column_scale = column_scale / jnp.maximum(per_slot, COLUMN_FLOOR)
+    probabilities = (
+        weights * row_scale[:, :, :, None, None] * column_scale[:, :, None]
+    ).astype(jnp.bfloat16)
     attended = jnp.einsum(
         "hbimj,bmhjd->bihd", probabilities, value_slots, preferred_element_type=jnp.float32
     )

time: 331 us -> 309 us (0.934)
  other arithmetic: 60.7 us -> 44.9 us
  matrix products: 77.1 us -> 69 us
    reduce_sum x6, other arithmetic: 56.5 us -> 40.5 us  [the longest x3 21.7 us: body(): jnp.sum(weights * row_scale[:, :, :, None, None], axis=2)]
    dot_general x1, matrix products: 20.4 us -> 13.8 us  [body(): jnp.einsum('hbimj,bmhjd->bihd', probabilities, value_slots, preferred_ele...]
  transfers between devices with their start and end apart: 21 -> 21, of which waited for: 13 -> 13; matrix products, arithmetic and copies ran while one was open for 19% -> 21% of each run, Pallas kernels for 0% -> 0%
where the time goes in v5:
time: 309 us; the launch traced here: 307 us
  waiting for transfers between devices  114 us (37%)
  matrix products  69 us (22%)
  other arithmetic  44.9 us (15%)
  starting transfers between devices  40.1 us (13%)
  local copies, waits for them, and re-layouts  38.7 us (13%)
    ppermute x7, waiting for transfers between devices, body(): got = lax.ppermute(piece, ('seq', 'sub'), perm=pairs)  39.9 us
    ppermute x7, waiting for transfers between devices, body(): partner = lax.ppermute(got, 'head', perm=[(0, 1), (1, 0)])  32.3 us
    ppermute x1, waiting for transfers between devices, body(): lax.ppermute(other_part.astype(jnp.bfloat16), 'head', perm=[(0, 1), (1, 0)])  24.3 us
    reduce_sum x3, other arithmetic, body(): jnp.sum(weights * row_scale[:, :, :, None, None], axis=2)  21.7 us
    dot_general x8, matrix products, body(): jnp.einsum('cjf,fhd->chjd', full, value_weights, preferred_element_type=j...  21 us
    reduce_sum x3, other arithmetic, body(): row_scale = 1.0 / jnp.sum(weights * column_scale[:, :, None], axis=(3, 4))  18.8 us
    dot_general x8, matrix products, body(): jnp.einsum('cjf,fhd->chjd', full, key_weights, preferred_element_type=jnp...  18 us
    dot_general x1, matrix products, body(): jnp.einsum('hbimj,bmhjd->bihd', probabilities, value_slots, preferred_ele...  13.8 us
  transfers between devices with their start and end apart: 21, of which 13 were waited for; matrix products, arithmetic and copies ran while one was open for 21% of the time, Pallas kernels for 0%

profile of v5, /device:TPU:0, one launch (start us, length us, event | category | flops | bytes accessed | tf_op | source)
XLA Modules:
  0.0 307.5 jit_solution(16581671725778070468)
XLA Ops:
  2.5 1.8 constant_dynamic-slice_fusion.11
  7.6 2.6 collective-permute-start.2
  13.1 2.8 collective-permute-start.6
  18.3 4.1 %convolution_convert_fusion = bf16[1024,512]{1,0:T(8,128)(2,1)} fusion(bf16[1024,1024]{1,0:T(8,128)(2,1)} %param.7, bf16[1024,512]{1,0:T(8,128)(2,1)} %param.8), kind=kOutput, calls=%fused_computation.26 | convolution fusion | flops 1074266112 | bytes 4194304 | tf_op jit(solution)/shard_map/dot_general | solution.py:26
  28.4 2.2 gather_fusion
  32.2 2.8 fusion.15
  35.0 7.6 %collective-permute-done.2 = bf16[4,64,1024]{2,1,0:T(8,128)(2,1)} collective-permute-done((bf16[4,64,1024]{2,1,0:T(8,128)(2,1)}, bf16[4,64,1024]{2,1,0:T(8,128)(2,1)}, u32[]{:S(2)}, u32[]{:S(2)}) %collective-permute-start.2) | collective-permute-done | bytes 524320 | tf_op jit(solution)/shard_map/ppermute | solution.py:83
  44.3 9.1 %collective-permute-done.4 = bf16[4,64,1024]{2,1,0:T(8,128)(2,1)} collective-permute-done((bf16[4,64,1024]{2,1,0:T(8,128)(2,1)}, bf16[4,64,1024]{2,1,0:T(8,128)(2,1)}, u32[]{:S(2)}, u32[]{:S(2)}) %collective-permute-start.4) | collective-permute-done | bytes 524320 | tf_op jit(solution)/shard_map/ppermute | solution.py:83
  58.3 2.6 fusion.33
  61.0 23.2 %collective-permute-done.8 = bf16[4,64,1024]{2,1,0:T(8,128)(2,1)} collective-permute-done((bf16[4,64,1024]{2,1,0:T(8,128)(2,1)}, bf16[4,64,1024]{2,1,0:T(8,128)(2,1)}, u32[]{:S(2)}, u32[]{:S(2)}) %collective-permute-start.8) | collective-permute-done | bytes 524320 | tf_op jit(solution)/shard_map/ppermute | solution.py:83
  88.3 2.5 fusion.35
  90.9 2.7 fusion.37
  93.6 5.6 %collective-permute-done.7 = bf16[4,64,1024]{2,1,0:T(8,128)(2,1)S(1)} collective-permute-done((bf16[4,64,1024]{2,1,0:T(8,128)(2,1)}, bf16[4,64,1024]{2,1,0:T(8,128)(2,1)S(1)}, u32[]{:S(2)}, u32[]{:S(2)}) %collective-permute-start.7) | collective-permute-done | bytes 524320 | tf_op jit(solution)/shard_map/ppermute | solution.py:85
  99.2 2.8 fusion.39
  102.0 8.5 %collective-permute-done.9 = bf16[4,64,1024]{2,1,0:T(8,128)(2,1)S(1)} collective-permute-done((bf16[4,64,1024]{2,1,0:T(8,128)(2,1)}, bf16[4,64,1024]{2,1,0:T(8,128)(2,1)S(1)}, u32[]{:S(2)}, u32[]{:S(2)}) %collective-permute-start.9) | collective-permute-done | bytes 524320 | tf_op jit(solution)/shard_map/ppermute | solution.py:85
  110.4 2.8 fusion.41
  113.2 8.5 %collective-permute-done.11 = bf16[4,64,1024]{2,1,0:T(8,128)(2,1)S(1)} collective-permute-done((bf16[4,64,1024]{2,1,0:T(8,128)(2,1)S(1)}, bf16[4,64,1024]{2,1,0:T(8,128)(2,1)S(1)}, u32[]{:S(2)}, u32[]{:S(2)}) %collective-permute-start.11) | collective-permute-done | bytes 524320 | tf_op jit(solution)/shard_map/ppermute | solution.py:85
  123.2 9.7 %collective-permute-done.13 = bf16[4,64,1024]{2,1,0:T(8,128)(2,1)S(1)} collective-permute-done((bf16[4,64,1024]{2,1,0:T(8,128)(2,1)S(1)}, bf16[4,64,1024]{2,1,0:T(8,128)(2,1)S(1)}, u32[]{:S(2)}, u32[]{:S(2)}) %collective-permute-start.13) | collective-permute-done | bytes 524320 | tf_op jit(solution)/shard_map/ppermute | solution.py:85
  135.2 7.7 %gather_fusion.9 = bf16[64,4,128,128]{3,2,1,0:T(8,128)(2,1)} fusion(bf16[32,4,128,128]{3,2,1,0:T(8,128)(2,1)} %fusion.45, s32[1024]{0:T(1024)S(1)} %pad_clamp_fusion), kind=kCustom, calls=%fused_computation.9 | custom fusion | bytes 16777472 | tf_op jit(solution)/shard_map/jit(_take)/gather | solution.py:98
  142.9 5.1 %select_reduce_fusion = (f32[4,8,128]{2,1,0:T(8,128)S(1)}, f32[4,8,128,8,128]{2,4,3,1,0:T(8,128)S(1)}) fusion(pred[8,8]{1,0:T(8,128)(4,1)S(1)} %constant_dynamic-slice_fusion, bf16[8,8,4,128,128]{4,3,2,1,0:T(8,128)(2,1)} %bitcast.305, bf16[8,128,4,128,1]{3,2,1,0,4:T(4,128)(2,1)S(1)} %bitcast.307), kind=kOutput, calls=%fused_computation.16 | convolution fusion | flops 1086320640 | bytes 26230848 | tf_op jit(solution)/shard_map/bihd,bmhjd->hbimj/dot_general | solution.py:105
  148.0 3.5 %fusion.126 = f32[4,8,128]{2,1,0:T(8,128)S(1)} fusion(f32[4,8,128]{2,1,0:T(8,128)S(1)} %get-tuple-element.17, f32[4,8,128,8,128]{2,4,3,1,0:T(8,128)S(1)} %get-tuple-element.18, pred[8,8]{1,0:T(8,128)(4,1)S(1)} %constant_dynamic-slice_fusion), kind=kLoop, calls=%fused_computation.204 | loop fusion | flops 16773120 | bytes 16810048 | tf_op jit(solution)/shard_map/reduce_sum | solution.py:114
  151.5 2.2 copy-done.2
  153.7 4.9 %multiply_reduce_fusion.3 = f32[4,8,8,128]{3,2,1,0:T(8,128)S(1)} fusion(f32[4,8,128]{2,1,0:T(8,128)S(1)} %broadcast_divide_fusion.2, f32[4,8,128]{2,1,0:T(8,128)S(1)} %get-tuple-element.17, f32[4,8,128,8,128]{2,4,3,1,0:T(8,128)S(1)} %get-tuple-element.18, pred[8,8]{1,0:T(8,128)(4,1)S(1)} %constant_dynamic-slice_fusion), kind=kLoop, calls=%fused_computation.14 | loop fusion | flops 20938752 | bytes 16941120 | tf_op jit(solution)/shard_map/reduce_sum | solution.py:115
  159.7 4.6 %all-to-all-start = ((f32[8,8,4,128]{3,1,2,0:T(8,128)}), f32[8,8,4,128]{3,1,2,0:T(8,128)S(1)}, u32[]{:S(2)}, u32[]{:S(2)}) async-start(f32[8,8,4,128]{3,1,2,0:T(8,128)} %convolution_bitcast_fusion.2), calls=%async_computation | async-start | bytes 262144 | tf_op jit(solution)/shard_map/all_to_all | solution.py:119
  164.3 2.7 fusion.17
  167.0 2.7 fusion.19
  171.8 3.8 %all-to-all-start.1 = ((f32[8,8,4,128]{3,1,2,0:T(8,128)}), f32[8,8,4,128]{3,1,2,0:T(8,128)S(1)}, u32[]{:S(2)}, u32[]{:S(2)}) async-start(f32[8,8,4,128]{3,1,2,0:T(8,128)} %broadcast_in_dim.119), calls=%async_computation.1 | async-start | bytes 262144 | tf_op jit(solution)/shard_map/all_to_all | solution.py:124
  175.5 2.5 fusion.21
  178.1 4.2 %all-to-all-done.1 = f32[8,8,4,128]{3,1,2,0:T(8,128)S(1)} async-done(((f32[8,8,4,128]{3,1,2,0:T(8,128)}), f32[8,8,4,128]{3,1,2,0:T(8,128)S(1)}, u32[]{:S(2)}, u32[]{:S(2)}) %all-to-all-start.1) | async-done | bytes 131104 | tf_op jit(solution)/shard_map/all_to_all | solution.py:124
  182.5 7.7 %multiply_reduce_fusion.2 = f32[4,8,128]{2,1,0:T(8,128)S(1)} fusion(f32[4,8,8,128]{3,2,1,0:T(8,128)S(1)} %divide_bitcast_fusion.1, f32[4,8,128]{2,1,0:T(8,128)S(1)} %get-tuple-element.17, f32[4,8,128,8,128]{2,4,3,1,0:T(8,128)} %copy-done.2, pred[8,8]{1,0:T(8,128)(4,1)S(1)} %constant_dynamic-slice_fusion), kind=kLoop, calls=%fused_computation.13 | loop fusion | flops 20967424 | bytes 16941120 | tf_op jit(solution)/shard_map/reduce_sum | solution.py:114
  190.3 8.4 %multiply_reduce_fusion.1 = f32[4,8,8,128]{3,2,1,0:T(8,128)S(1)} fusion(f32[4,8,128]{2,1,0:T(8,128)S(1)} %broadcast_divide_fusion.1, f32[4,8,128]{2,1,0:T(8,128)S(1)} %get-tuple-element.17, f32[4,8,128,8,128]{2,4,3,1,0:T(8,128)} %copy-done.2, pred[8,8]{1,0:T(8,128)(4,1)S(1)} %constant_dynamic-slice_fusion), kind=kLoop, calls=%fused_computation.12 | loop fusion | flops 20938752 | bytes 16941120 | tf_op jit(solution)/shard_map/reduce_sum | solution.py:115
  199.7 3.4 %all-to-all-start.2 = ((f32[8,8,4,128]{3,1,2,0:T(8,128)}), f32[8,8,4,128]{3,1,2,0:T(8,128)S(1)}, u32[]{:S(2)}, u32[]{:S(2)}) async-start(f32[8,8,4,128]{3,1,2,0:T(8,128)} %copy.168), calls=%async_computation.2 | async-start | bytes 262144 | tf_op jit(solution)/shard_map/all_to_all | solution.py:119
  203.1 2.6 fusion.23
  205.6 4.1 %all-to-all-done.2 = f32[8,8,4,128]{3,1,2,0:T(8,128)S(1)} async-done(((f32[8,8,4,128]{3,1,2,0:T(8,128)}), f32[8,8,4,128]{3,1,2,0:T(8,128)S(1)}, u32[]{:S(2)}, u32[]{:S(2)}) %all-to-all-start.2) | async-done | bytes 131104 | tf_op jit(solution)/shard_map/all_to_all | solution.py:119
  210.4 3.4 %all-to-all-start.3 = ((f32[8,8,4,128]{3,1,2,0:T(8,128)}), f32[8,8,4,128]{3,1,2,0:T(8,128)S(1)}, u32[]{:S(2)}, u32[]{:S(2)}) async-start(f32[8,8,4,128]{3,1,2,0:T(8,128)} %broadcast_in_dim.120), calls=%async_computation.3 | async-start | bytes 262144 | tf_op jit(solution)/shard_map/all_to_all | solution.py:124
  213.8 2.6 fusion.25
  216.4 4.1 %all-to-all-done.3 = f32[8,8,4,128]{3,1,2,0:T(8,128)S(1)} async-done(((f32[8,8,4,128]{3,1,2,0:T(8,128)}), f32[8,8,4,128]{3,1,2,0:T(8,128)S(1)}, u32[]{:S(2)}, u32[]{:S(2)}) %all-to-all-start.3) | async-done | bytes 131104 | tf_op jit(solution)/shard_map/all_to_all | solution.py:124
  220.8 7.7 %multiply_reduce_fusion = f32[4,8,128]{2,1,0:T(8,128)S(1)} fusion(f32[4,8,8,128]{3,2,1,0:T(8,128)S(1)} %divide_bitcast_fusion, f32[4,8,128]{2,1,0:T(8,128)S(1)} %get-tuple-element.17, f32[4,8,128,8,128]{2,4,3,1,0:T(8,128)} %copy-done.2, pred[8,8]{1,0:T(8,128)(4,1)S(1)} %constant_dynamic-slice_fusion), kind=kLoop, calls=%fused_computation.11 | loop fusion | flops 20967424 | bytes 16941120 | tf_op jit(solution)/shard_map/reduce_sum | solution.py:114
  228.5 8.4 %multiply_reduce_fusion.4 = f32[4,8,8,128]{3,2,1,0:T(8,128)S(1)} fusion(f32[4,8,128]{2,1,0:T(8,128)S(1)} %broadcast_divide_fusion, f32[4,8,128]{2,1,0:T(8,128)S(1)} %get-tuple-element.17, f32[4,8,128,8,128]{2,4,3,1,0:T(8,128)} %copy-done.2, pred[8,8]{1,0:T(8,128)(4,1)S(1)} %constant_dynamic-slice_fusion), kind=kLoop, calls=%fused_computation.17 | loop fusion | flops 20938752 | bytes 16941120 | tf_op jit(solution)/shard_map/reduce_sum | solution.py:115
  237.9 3.4 %all-to-all-start.4 = ((f32[8,8,4,128]{3,1,2,0:T(8,128)}), f32[8,8,4,128]{3,1,2,0:T(8,128)S(1)}, u32[]{:S(2)}, u32[]{:S(2)}) async-start(f32[8,8,4,128]{3,1,2,0:T(8,128)} %copy.170), calls=%async_computation.4 | async-start | bytes 262144 | tf_op jit(solution)/shard_map/all_to_all | solution.py:119
  241.3 2.5 fusion.27
  243.8 4.1 %all-to-all-done.4 = f32[8,8,4,128]{3,1,2,0:T(8,128)S(1)} async-done(((f32[8,8,4,128]{3,1,2,0:T(8,128)}), f32[8,8,4,128]{3,1,2,0:T(8,128)S(1)}, u32[]{:S(2)}, u32[]{:S(2)}) %all-to-all-start.4) | async-done | bytes 131104 | tf_op jit(solution)/shard_map/all_to_all | solution.py:119
  248.6 3.4 %all-to-all-start.5 = ((f32[8,8,4,128]{3,1,2,0:T(8,128)}), f32[8,8,4,128]{3,1,2,0:T(8,128)S(1)}, u32[]{:S(2)}, u32[]{:S(2)}) async-start(f32[8,8,4,128]{3,1,2,0:T(8,128)} %broadcast_in_dim.121), calls=%async_computation.5 | async-start | bytes 262144 | tf_op jit(solution)/shard_map/all_to_all | solution.py:124
  252.0 2.6 fusion.29
  254.6 7.7 %gather_fusion.8 = bf16[64,4,128,128]{3,2,1,0:T(8,128)(2,1)} fusion(bf16[32,4,128,128]{3,2,1,0:T(8,128)(2,1)} %fusion.29, s32[1024]{0:T(1024)S(1)} %pad_clamp_fusion), kind=kCustom, calls=%fused_computation.8 | custom fusion | bytes 16777472 | tf_op jit(solution)/shard_map/jit(_take)/gather | solution.py:101
  262.5 13.8 %fusion.9 = bf16[8,128,4,128]{1,3,2,0:T(8,128)(2,1)S(1)} fusion(bf16[8,8,4,128,128]{4,3,2,1,0:T(8,128)(2,1)} %bitcast.304, f32[4,8,8,128]{3,2,1,0:T(8,128)S(1)} %fusion.49, f32[4,8,128]{2,1,0:T(8,128)S(1)} %broadcast_divide_fusion, f32[4,8,128]{2,1,0:T(8,128)S(1)} %get-tuple-element.17, f32[4,8,128,8,128]{2,4,3,1,0:T(8,128)} %copy-done.2, ...), kind=kOutput, calls=%fused_computation.28 | convolution fusion | flops 1099431936 | bytes 26378304 | tf_op jit(solution)/shard_map/hbimj,bmhjd->bihd/dot_general | solution.py:132
  280.2 24.3 %collective-permute-done.14 = bf16[1024,512]{1,0:T(8,128)(2,1)} collective-permute-done((bf16[1024,512]{1,0:T(8,128)(2,1)}, bf16[1024,512]{1,0:T(8,128)(2,1)}, u32[]{:S(2)}, u32[]{:S(2)}) %collective-permute-start.14) | collective-permute-done | bytes 1048608 | tf_op jit(solution)/shard_map/ppermute | solution.py:147
  304.5 3.0 add_convert_fusion
  (131 shorter events, 44.5 us)
Async XLA Ops:
  0.0 56.2 %copy-start = (bf16[1024,512]{1,0:T(8,128)(2,1)S(1)}, bf16[1024,512]{1,0:T(8,128)(2,1)}, u32[]{:S(2)}) copy-start(bf16[1024,512]{1,0:T(8,128)(2,1)} %param.9) | copy-start | bytes 3145732
  2.5 14.8 %copy-start.3 = (s32[64,8]{0,1:T(8,128)S(1)}, s32[64,8]{0,1:T(8,128)}, u32[]{:S(2)}) copy-start(s32[64,8]{0,1:T(8,128)} %param.12) | copy-start | bytes 6148
  5.7 24.9 %collective-permute-start = (bf16[4,64,1024]{2,1,0:T(8,128)(2,1)}, bf16[4,64,1024]{2,1,0:T(8,128)(2,1)}, u32[]{:S(2)}, u32[]{:S(2)}) collective-permute-start(bf16[4,64,1024]{2,1,0:T(8,128)(2,1)} %gather_fusion.1), channel_id=1, source_target_pairs={{0,1},{1,0},{4,5},{5,4},{8,9},{9,8},{12,13},{13,12},{2,3},{3,2},{6... | collective-permute-start | bytes 1572872 | tf_op jit(solution)/shard_map/ppermute | solution.py:83
  7.6 34.9 %collective-permute-start.2 = (bf16[4,64,1024]{2,1,0:T(8,128)(2,1)}, bf16[4,64,1024]{2,1,0:T(8,128)(2,1)}, u32[]{:S(2)}, u32[]{:S(2)}) collective-permute-start(bf16[4,64,1024]{2,1,0:T(8,128)(2,1)} %gather_fusion.2), channel_id=1, source_target_pairs={{0,4},{1,5},{4,0},{5,1},{8,12},{9,13},{12,8},{13,9},{2,6},{3,7},{6... | collective-permute-start | bytes 1572872 | tf_op jit(solution)/shard_map/ppermute | solution.py:83
  11.6 41.8 %collective-permute-start.4 = (bf16[4,64,1024]{2,1,0:T(8,128)(2,1)}, bf16[4,64,1024]{2,1,0:T(8,128)(2,1)}, u32[]{:S(2)}, u32[]{:S(2)}) collective-permute-start(bf16[4,64,1024]{2,1,0:T(8,128)(2,1)} %gather_fusion.3), channel_id=1, source_target_pairs={{0,5},{1,4},{4,1},{5,0},{8,13},{9,12},{12,9},{13,8},{2,7},{3,6},{6... | collective-permute-start | bytes 1572872 | tf_op jit(solution)/shard_map/ppermute | solution.py:83
  13.1 41.7 %collective-permute-start.6 = (bf16[4,64,1024]{2,1,0:T(8,128)(2,1)}, bf16[4,64,1024]{2,1,0:T(8,128)(2,1)}, u32[]{:S(2)}, u32[]{:S(2)}) collective-permute-start(bf16[4,64,1024]{2,1,0:T(8,128)(2,1)} %gather_fusion.4), channel_id=1, source_target_pairs={{0,8},{1,9},{4,12},{5,13},{8,0},{9,1},{12,4},{13,5},{2,10},{3,11},... | collective-permute-start | bytes 1572872 | tf_op jit(solution)/shard_map/ppermute | solution.py:83
  17.3 66.9 %collective-permute-start.8 = (bf16[4,64,1024]{2,1,0:T(8,128)(2,1)}, bf16[4,64,1024]{2,1,0:T(8,128)(2,1)}, u32[]{:S(2)}, u32[]{:S(2)}) collective-permute-start(bf16[4,64,1024]{2,1,0:T(8,128)(2,1)} %gather_fusion.5), channel_id=1, source_target_pairs={{0,9},{1,8},{4,13},{5,12},{8,1},{9,0},{12,5},{13,4},{2,11},{3,10},... | collective-permute-start | bytes 1572872 | tf_op jit(solution)/shard_map/ppermute | solution.py:83
  30.6 27.2 %collective-permute-start.1 = (bf16[4,64,1024]{2,1,0:T(8,128)(2,1)}, bf16[4,64,1024]{2,1,0:T(8,128)(2,1)S(1)}, u32[]{:S(2)}, u32[]{:S(2)}) collective-permute-start(bf16[4,64,1024]{2,1,0:T(8,128)(2,1)} %collective-permute-done), channel_id=1, source_target_pairs={{0,2},{2,0},{1,3},{3,1},{4,6},{6,4},{5,7},{7,5},{8,10},{10,8},{9,1... | collective-permute-start | bytes 1572872 | tf_op jit(solution)/shard_map/ppermute | solution.py:85
  42.5 43.1 %collective-permute-start.10 = (bf16[4,64,1024]{2,1,0:T(8,128)(2,1)}, bf16[4,64,1024]{2,1,0:T(8,128)(2,1)S(1)}, u32[]{:S(2)}, u32[]{:S(2)}) collective-permute-start(bf16[4,64,1024]{2,1,0:T(8,128)(2,1)} %gather_fusion.6), channel_id=1, source_target_pairs={{0,12},{1,13},{4,8},{5,9},{8,4},{9,5},{12,0},{13,1},{2,14},{3,15},... | collective-permute-start | bytes 1572872 | tf_op jit(solution)/shard_map/ppermute | solution.py:83
  53.4 32.8 %collective-permute-start.12 = (bf16[4,64,1024]{2,1,0:T(8,128)(2,1)}, bf16[4,64,1024]{2,1,0:T(8,128)(2,1)S(1)}, u32[]{:S(2)}, u32[]{:S(2)}) collective-permute-start(bf16[4,64,1024]{2,1,0:T(8,128)(2,1)} %gather_fusion.7), channel_id=1, source_target_pairs={{0,13},{1,12},{4,9},{5,8},{8,5},{9,4},{12,1},{13,0},{2,15},{3,14},... | collective-permute-start | bytes 1572872 | tf_op jit(solution)/shard_map/ppermute | solution.py:83
  54.8 32.9 %collective-permute-start.3 = (bf16[4,64,1024]{2,1,0:T(8,128)(2,1)}, bf16[4,64,1024]{2,1,0:T(8,128)(2,1)S(1)}, u32[]{:S(2)}, u32[]{:S(2)}) collective-permute-start(bf16[4,64,1024]{2,1,0:T(8,128)(2,1)} %collective-permute-done.2), channel_id=1, source_target_pairs={{0,2},{2,0},{1,3},{3,1},{4,6},{6,4},{5,7},{7,5},{8,10},{10,8},{9,1... | collective-permute-start | bytes 1572872 | tf_op jit(solution)/shard_map/ppermute | solution.py:85
  57.8 29.9 %copy-start.16 = (bf16[4,64,1024]{2,1,0:T(8,128)(2,1)}, bf16[4,64,1024]{2,1,0:T(8,128)(2,1)S(1)}, u32[]{:S(2)}) copy-start(bf16[4,64,1024]{2,1,0:T(8,128)(2,1)S(1)} %collective-permute-done.1) | copy-start | bytes 1572868
  57.8 33.1 %collective-permute-start.5 = (bf16[4,64,1024]{2,1,0:T(8,128)(2,1)}, bf16[4,64,1024]{2,1,0:T(8,128)(2,1)S(1)}, u32[]{:S(2)}, u32[]{:S(2)}) collective-permute-start(bf16[4,64,1024]{2,1,0:T(8,128)(2,1)} %collective-permute-done.4), channel_id=1, source_target_pairs={{0,2},{2,0},{1,3},{3,1},{4,6},{6,4},{5,7},{7,5},{8,10},{10,8},{9,1... | collective-permute-start | bytes 1572872 | tf_op jit(solution)/shard_map/ppermute | solution.py:85
  84.2 15.0 %collective-permute-start.7 = (bf16[4,64,1024]{2,1,0:T(8,128)(2,1)}, bf16[4,64,1024]{2,1,0:T(8,128)(2,1)S(1)}, u32[]{:S(2)}, u32[]{:S(2)}) collective-permute-start(bf16[4,64,1024]{2,1,0:T(8,128)(2,1)} %collective-permute-done.6), channel_id=1, source_target_pairs={{0,2},{2,0},{1,3},{3,1},{4,6},{6,4},{5,7},{7,5},{8,10},{10,8},{9,1... | collective-permute-start | bytes 1572872 | tf_op jit(solution)/shard_map/ppermute | solution.py:85
  85.6 36.0 %copy-start.8 = (bf16[4,64,1024]{2,1,0:T(8,128)(2,1)}, bf16[4,64,1024]{2,1,0:T(8,128)(2,1)S(1)}, u32[]{:S(2)}) copy-start(bf16[4,64,1024]{2,1,0:T(8,128)(2,1)S(1)} %collective-permute-done.10) | copy-start | bytes 1572868
  85.6 24.8 %collective-permute-start.9 = (bf16[4,64,1024]{2,1,0:T(8,128)(2,1)}, bf16[4,64,1024]{2,1,0:T(8,128)(2,1)S(1)}, u32[]{:S(2)}, u32[]{:S(2)}) collective-permute-start(bf16[4,64,1024]{2,1,0:T(8,128)(2,1)} %collective-permute-done.8), channel_id=1, source_target_pairs={{0,2},{2,0},{1,3},{3,1},{4,6},{6,4},{5,7},{7,5},{8,10},{10,8},{9,1... | collective-permute-start | bytes 1572872 | tf_op jit(solution)/shard_map/ppermute | solution.py:85
  86.2 46.7 %copy-start.6 = (bf16[4,64,1024]{2,1,0:T(8,128)(2,1)}, bf16[4,64,1024]{2,1,0:T(8,128)(2,1)S(1)}, u32[]{:S(2)}) copy-start(bf16[4,64,1024]{2,1,0:T(8,128)(2,1)S(1)} %collective-permute-done.12) | copy-start | bytes 1572868
  86.2 35.4 %collective-permute-start.11 = (bf16[4,64,1024]{2,1,0:T(8,128)(2,1)S(1)}, bf16[4,64,1024]{2,1,0:T(8,128)(2,1)S(1)}, u32[]{:S(2)}, u32[]{:S(2)}) collective-permute-start(bf16[4,64,1024]{2,1,0:T(8,128)(2,1)S(1)} %collective-permute-done.10), channel_id=1, source_target_pairs={{0,2},{2,0},{1,3},{3,1},{4,6},{6,4},{5,7},{7,5},{8,10},{10,8},{9,1... | collective-permute-start | bytes 1572872 | tf_op jit(solution)/shard_map/ppermute | solution.py:85
  87.7 5.9 %copy-start.20 = (bf16[4,64,1024]{2,1,0:T(8,128)(2,1)}, bf16[4,64,1024]{2,1,0:T(8,128)(2,1)S(1)}, u32[]{:S(2)}) copy-start(bf16[4,64,1024]{2,1,0:T(8,128)(2,1)S(1)} %collective-permute-done.3) | copy-start | bytes 1572868
  87.7 45.2 %collective-permute-start.13 = (bf16[4,64,1024]{2,1,0:T(8,128)(2,1)S(1)}, bf16[4,64,1024]{2,1,0:T(8,128)(2,1)S(1)}, u32[]{:S(2)}, u32[]{:S(2)}) collective-permute-start(bf16[4,64,1024]{2,1,0:T(8,128)(2,1)S(1)} %collective-permute-done.12), channel_id=1, source_target_pairs={{0,2},{2,0},{1,3},{3,1},{4,6},{6,4},{5,7},{7,5},{8,10},{10,8},{9,1... | collective-permute-start | bytes 1572872 | tf_op jit(solution)/shard_map/ppermute | solution.py:85
  90.9 11.1 %copy-start.18 = (bf16[4,64,1024]{2,1,0:T(8,128)(2,1)}, bf16[4,64,1024]{2,1,0:T(8,128)(2,1)S(1)}, u32[]{:S(2)}) copy-start(bf16[4,64,1024]{2,1,0:T(8,128)(2,1)S(1)} %collective-permute-done.5) | copy-start | bytes 1572868
  99.2 14.0 %copy-start.14 = (bf16[4,64,1024]{2,1,0:T(8,128)(2,1)}, bf16[4,64,1024]{2,1,0:T(8,128)(2,1)S(1)}, u32[]{:S(2)}) copy-start(bf16[4,64,1024]{2,1,0:T(8,128)(2,1)S(1)} %collective-permute-done.7) | copy-start | bytes 1572868
  110.4 12.7 %copy-start.12 = (bf16[4,64,1024]{2,1,0:T(8,128)(2,1)}, bf16[4,64,1024]{2,1,0:T(8,128)(2,1)S(1)}, u32[]{:S(2)}) copy-start(bf16[4,64,1024]{2,1,0:T(8,128)(2,1)S(1)} %collective-permute-done.9) | copy-start | bytes 1572868
  121.7 11.2 %copy-start.11 = (bf16[4,64,1024]{2,1,0:T(8,128)(2,1)}, bf16[4,64,1024]{2,1,0:T(8,128)(2,1)S(1)}, u32[]{:S(2)}) copy-start(bf16[4,64,1024]{2,1,0:T(8,128)(2,1)S(1)} %collective-permute-done.11) | copy-start | bytes 1572868
  132.9 0.8 copy-start.10
  148.0 5.7 %copy-start.2 = (f32[4,8,128,8,128]{2,4,3,1,0:T(8,128)}, f32[4,8,128,8,128]{2,4,3,1,0:T(8,128)S(1)}, u32[]{:S(2)}) copy-start(f32[4,8,128,8,128]{2,4,3,1,0:T(8,128)S(1)} %get-tuple-element.18) | copy-start | bytes 50331652
  153.7 10.6 %copy-start.4 = (bf16[1024,512]{1,0:T(8,128)(2,1)S(1)}, bf16[1024,512]{1,0:T(8,128)(2,1)}, u32[]{:S(2)}) copy-start(bf16[1024,512]{1,0:T(8,128)(2,1)} %param.10) | copy-start | bytes 3145732
  153.7 10.6 %copy-start.17 = (bf16[4,64,1024]{2,1,0:T(8,128)(2,1)S(1)}, bf16[4,64,1024]{2,1,0:T(8,128)(2,1)}, u32[]{:S(2)}) copy-start(bf16[4,64,1024]{2,1,0:T(8,128)(2,1)} %copy-done.16) | copy-start | bytes 1572868
  159.7 11.3 %all-to-all-start = ((f32[8,8,4,128]{3,1,2,0:T(8,128)}), f32[8,8,4,128]{3,1,2,0:T(8,128)S(1)}, u32[]{:S(2)}, u32[]{:S(2)}) async-start(f32[8,8,4,128]{3,1,2,0:T(8,128)} %convolution_bitcast_fusion.2), calls=%async_computation | async-start | bytes 262144 | tf_op jit(solution)/shard_map/all_to_all | solution.py:119
  164.3 11.2 %copy-start.19 = (bf16[4,64,1024]{2,1,0:T(8,128)(2,1)S(1)}, bf16[4,64,1024]{2,1,0:T(8,128)(2,1)}, u32[]{:S(2)}) copy-start(bf16[4,64,1024]{2,1,0:T(8,128)(2,1)} %copy-done.18) | copy-start | bytes 1572868
  171.8 10.5 %all-to-all-start.1 = ((f32[8,8,4,128]{3,1,2,0:T(8,128)}), f32[8,8,4,128]{3,1,2,0:T(8,128)S(1)}, u32[]{:S(2)}, u32[]{:S(2)}) async-start(f32[8,8,4,128]{3,1,2,0:T(8,128)} %broadcast_in_dim.119), calls=%async_computation.1 | async-start | bytes 262144 | tf_op jit(solution)/shard_map/all_to_all | solution.py:124
  190.2 12.8 %copy-start.15 = (bf16[4,64,1024]{2,1,0:T(8,128)(2,1)S(1)}, bf16[4,64,1024]{2,1,0:T(8,128)(2,1)}, u32[]{:S(2)}) copy-start(bf16[4,64,1024]{2,1,0:T(8,128)(2,1)} %copy-done.14) | copy-start | bytes 1572868
  198.7 15.1 %copy-start.13 = (bf16[4,64,1024]{2,1,0:T(8,128)(2,1)S(1)}, bf16[4,64,1024]{2,1,0:T(8,128)(2,1)}, u32[]{:S(2)}) copy-start(bf16[4,64,1024]{2,1,0:T(8,128)(2,1)} %copy-done.12) | copy-start | bytes 1572868
  199.7 10.1 %all-to-all-start.2 = ((f32[8,8,4,128]{3,1,2,0:T(8,128)}), f32[8,8,4,128]{3,1,2,0:T(8,128)S(1)}, u32[]{:S(2)}, u32[]{:S(2)}) async-start(f32[8,8,4,128]{3,1,2,0:T(8,128)} %copy.168), calls=%async_computation.2 | async-start | bytes 262144 | tf_op jit(solution)/shard_map/all_to_all | solution.py:119
  210.4 10.1 %all-to-all-start.3 = ((f32[8,8,4,128]{3,1,2,0:T(8,128)}), f32[8,8,4,128]{3,1,2,0:T(8,128)S(1)}, u32[]{:S(2)}, u32[]{:S(2)}) async-start(f32[8,8,4,128]{3,1,2,0:T(8,128)} %broadcast_in_dim.120), calls=%async_computation.3 | async-start | bytes 262144 | tf_op jit(solution)/shard_map/all_to_all | solution.py:124
  228.5 12.8 %copy-start.9 = (bf16[4,64,1024]{2,1,0:T(8,128)(2,1)S(1)}, bf16[4,64,1024]{2,1,0:T(8,128)(2,1)}, u32[]{:S(2)}) copy-start(bf16[4,64,1024]{2,1,0:T(8,128)(2,1)} %copy-done.8) | copy-start | bytes 1572868
  236.9 15.1 %copy-start.7 = (bf16[4,64,1024]{2,1,0:T(8,128)(2,1)S(1)}, bf16[4,64,1024]{2,1,0:T(8,128)(2,1)}, u32[]{:S(2)}) copy-start(bf16[4,64,1024]{2,1,0:T(8,128)(2,1)} %copy-done.6) | copy-start | bytes 1572868
  237.9 10.1 %all-to-all-start.4 = ((f32[8,8,4,128]{3,1,2,0:T(8,128)}), f32[8,8,4,128]{3,1,2,0:T(8,128)S(1)}, u32[]{:S(2)}, u32[]{:S(2)}) async-start(f32[8,8,4,128]{3,1,2,0:T(8,128)} %copy.170), calls=%async_computation.4 | async-start | bytes 262144 | tf_op jit(solution)/shard_map/all_to_all | solution.py:119
  248.6 13.6 %all-to-all-start.5 = ((f32[8,8,4,128]{3,1,2,0:T(8,128)}), f32[8,8,4,128]{3,1,2,0:T(8,128)S(1)}, u32[]{:S(2)}, u32[]{:S(2)}) async-start(f32[8,8,4,128]{3,1,2,0:T(8,128)} %broadcast_in_dim.121), calls=%async_computation.5 | async-start | bytes 262144 | tf_op jit(solution)/shard_map/all_to_all | solution.py:124
  262.5 14.5 %copy-start.5 = (bf16[512,1024]{1,0:T(8,128)(2,1)S(1)}, bf16[512,1024]{1,0:T(8,128)(2,1)}, u32[]{:S(2)}) copy-start(bf16[512,1024]{1,0:T(8,128)(2,1)} %param.11) | copy-start | bytes 3145732
  277.0 30.5 %copy-start.1 = (bf16[1024,512]{1,0:T(8,128)(2,1)S(1)}, bf16[1024,512]{1,0:T(8,128)(2,1)}, u32[]{:S(2)}) copy-start(bf16[1024,512]{1,0:T(8,128)(2,1)} %param.9) | copy-start | bytes 3145732
  278.7 25.8 %collective-permute-start.14 = (bf16[1024,512]{1,0:T(8,128)(2,1)}, bf16[1024,512]{1,0:T(8,128)(2,1)}, u32[]{:S(2)}, u32[]{:S(2)}) collective-permute-start(bf16[1024,512]{1,0:T(8,128)(2,1)} %convolution_convert_fusion.1), channel_id=1, source_target_pairs={{0,2},{2,0},{1,3},{3,1},{4,6},{6,4},{5,7},{7,5},{8,10},{10,8},{9,1... | collective-permute-start | bytes 3145736 | tf_op jit(solution)/shard_map/ppermute | solution.py:147

commit v6 on v5

--- a/solution.py
+++ b/solution.py
@@ -129,12 +129,12 @@
     probabilities = (
         weights * row_scale[:, :, :, None, None] * column_scale[:, :, None]
     ).astype(jnp.bfloat16)
-    attended = jnp.einsum(
-        "hbimj,bmhjd->bihd", probabilities, value_slots, preferred_element_type=jnp.float32
-    )
-    attended = attended.astype(jnp.bfloat16).reshape(row_count, heads_here * HS)
     head_count = lax.axis_size("head")
     if head_count != 2:
+        attended = jnp.einsum(
+            "hbimj,bmhjd->bihd", probabilities, value_slots, preferred_element_type=jnp.float32
+        )
+        attended = attended.astype(jnp.bfloat16).reshape(row_count, heads_here * HS)
         partial_out = jnp.dot(attended, w_out, preferred_element_type=jnp.float32)
         return lax.psum_scatter(
             partial_out.astype(jnp.bfloat16), "head", scatter_dimension=1, tiled=True
@@ -143,10 +143,23 @@
     width = w_out.shape[1] // 2
     other_cols = lax.dynamic_slice_in_dim(w_out, (1 - head_index) * width, width, 1)
     my_cols = lax.dynamic_slice_in_dim(w_out, head_index * width, width, 1)
-    other_part = jnp.dot(attended, other_cols, preferred_element_type=jnp.float32)
-    received = lax.ppermute(other_part.astype(jnp.bfloat16), "head", perm=[(0, 1), (1, 0)])
-    my_part = jnp.dot(attended, my_cols, preferred_element_type=jnp.float32)
-    return (my_part + received.astype(jnp.float32)).astype(jnp.bfloat16)
+    pieces = 2 if local_blocks % 2 == 0 else 1
+    piece_blocks = local_blocks // pieces
+    outputs = []
+    for piece_number in range(pieces):
+        block_range = slice(piece_number * piece_blocks, (piece_number + 1) * piece_blocks)
+        attended = jnp.einsum(
+            "hbimj,bmhjd->bihd",
+            probabilities[:, block_range],
+            value_slots[block_range],
+            preferred_element_type=jnp.float32,
+        )
+        attended = attended.astype(jnp.bfloat16).reshape(piece_blocks * TILE, heads_here * HS)
+        other_part = jnp.dot(attended, other_cols, preferred_element_type=jnp.float32)
+        received = lax.ppermute(other_part.astype(jnp.bfloat16), "head", perm=[(0, 1), (1, 0)])
+        my_part = jnp.dot(attended, my_cols, preferred_element_type=jnp.float32)
+        outputs.append((my_part + received.astype(jnp.float32)).astype(jnp.bfloat16))
+    return jnp.concatenate(outputs, axis=0)
 
 
 def solution(mesh):

time: 309 us -> 309 us (level)
  waiting for transfers between devices: 114 us -> 100 us
  local copies, waits for them, and re-layouts: 38.7 us -> 48.4 us
  other arithmetic: 44.9 us -> 53.6 us
  matrix products: 69 us -> 61.4 us
  starting transfers between devices: 40.1 us -> 43.6 us
    ppermute x1 -> x2, waiting for transfers between devices: 24.3 us -> 14.1 us  [body(): lax.ppermute(other_part.astype(jnp.bfloat16), 'head', perm=[(0, 1), (1, 0)])]
    slice x0 -> x2, local copies, waits for them, and re-layouts: none -> 8.75 us  [the longest x1 6.04 us: body(): value_slots[block_range]]
    convert_element_type x0 -> x1, other arithmetic: none -> 7.7 us  [body(): probabilities = (weights * row_scale[:, :, :, None, None] * column_scale[...]
    dot_general x1 -> x2, matrix products: 13.8 us -> 6.19 us  [body(): jnp.einsum('hbimj,bmhjd->bihd', probabilities[:, block_range], value_slot...]
    all_to_all x3, waiting for transfers between devices: 9.56 us -> 3.96 us  [body(): lax.all_to_all(column_complete, ('seq', 'sub'), split_axis=0, concat_axis...]
  transfers between devices with their start and end apart: 21 -> 22, of which waited for: 13 -> 13; matrix products, arithmetic and copies ran while one was open for 21% -> 25% of each run, Pallas kernels for 0% -> 0%
where the time goes in v6:
time: 309 us; the launch traced here: 308 us
  waiting for transfers between devices  100 us (32%)
  matrix products  61.4 us (20%)
  other arithmetic  53.6 us (17%)
  local copies, waits for them, and re-layouts  48.4 us (16%)
  starting transfers between devices  43.6 us (14%)
    ppermute x7, waiting for transfers between devices, body(): got = lax.ppermute(piece, ('seq', 'sub'), perm=pairs)  39.9 us
    ppermute x7, waiting for transfers between devices, body(): partner = lax.ppermute(got, 'head', perm=[(0, 1), (1, 0)])  32.3 us
    reduce_sum x3, other arithmetic, body(): jnp.sum(weights * row_scale[:, :, :, None, None], axis=2)  21.7 us
    dot_general x8, matrix products, body(): jnp.einsum('cjf,fhd->chjd', full, value_weights, preferred_element_type=j...  19.1 us
    reduce_sum x3, other arithmetic, body(): row_scale = 1.0 / jnp.sum(weights * column_scale[:, :, None], axis=(3, 4))  18.8 us
    dot_general x8, matrix products, body(): jnp.einsum('cjf,fhd->chjd', full, key_weights, preferred_element_type=jnp...  18 us
    ppermute x2, waiting for transfers between devices, body(): lax.ppermute(other_part.astype(jnp.bfloat16), 'head', perm=[(0, 1), (1, 0)])  14.1 us
    all_to_all x3, starting transfers between devices, body(): lax.all_to_all(spread, ('seq', 'sub'), split_axis=0, concat_axis=0, tiled...  13.5 us
  transfers between devices with their start and end apart: 22, of which 13 were waited for; matrix products, arithmetic and copies ran while one was open for 25% of the time, Pallas kernels for 0%

profile of v6, /device:TPU:0, one launch (start us, length us, event | category | flops | bytes accessed | tf_op | source)
XLA Modules:
  0.0 307.8 jit_solution(17240103119106352766)
XLA Ops:
  7.6 2.6 collective-permute-start.2
  13.1 2.8 collective-permute-start.6
  18.3 4.1 %convolution_convert_fusion = bf16[1024,512]{1,0:T(8,128)(2,1)} fusion(bf16[1024,1024]{1,0:T(8,128)(2,1)} %param.7, bf16[1024,512]{1,0:T(8,128)(2,1)} %param.8), kind=kOutput, calls=%fused_computation.27 | convolution fusion | flops 1074266112 | bytes 4194304 | tf_op jit(solution)/shard_map/dot_general | solution.py:26
  28.4 2.2 gather_fusion
  32.2 2.8 fusion.29
  35.0 7.6 %collective-permute-done.2 = bf16[4,64,1024]{2,1,0:T(8,128)(2,1)} collective-permute-done((bf16[4,64,1024]{2,1,0:T(8,128)(2,1)}, bf16[4,64,1024]{2,1,0:T(8,128)(2,1)}, u32[]{:S(2)}, u32[]{:S(2)}) %collective-permute-start.2) | collective-permute-done | bytes 524320 | tf_op jit(solution)/shard_map/ppermute | solution.py:83
  44.3 9.1 %collective-permute-done.4 = bf16[4,64,1024]{2,1,0:T(8,128)(2,1)} collective-permute-done((bf16[4,64,1024]{2,1,0:T(8,128)(2,1)}, bf16[4,64,1024]{2,1,0:T(8,128)(2,1)}, u32[]{:S(2)}, u32[]{:S(2)}) %collective-permute-start.4) | collective-permute-done | bytes 524320 | tf_op jit(solution)/shard_map/ppermute | solution.py:83
  58.3 2.6 fusion.47
  61.0 23.2 %collective-permute-done.8 = bf16[4,64,1024]{2,1,0:T(8,128)(2,1)} collective-permute-done((bf16[4,64,1024]{2,1,0:T(8,128)(2,1)}, bf16[4,64,1024]{2,1,0:T(8,128)(2,1)}, u32[]{:S(2)}, u32[]{:S(2)}) %collective-permute-start.8) | collective-permute-done | bytes 524320 | tf_op jit(solution)/shard_map/ppermute | solution.py:83
  88.3 2.5 fusion.49
  90.9 2.7 fusion.51
  93.6 5.6 %collective-permute-done.7 = bf16[4,64,1024]{2,1,0:T(8,128)(2,1)S(1)} collective-permute-done((bf16[4,64,1024]{2,1,0:T(8,128)(2,1)}, bf16[4,64,1024]{2,1,0:T(8,128)(2,1)S(1)}, u32[]{:S(2)}, u32[]{:S(2)}) %collective-permute-start.7) | collective-permute-done | bytes 524320 | tf_op jit(solution)/shard_map/ppermute | solution.py:85
  99.2 2.8 fusion.53
  102.0 8.5 %collective-permute-done.9 = bf16[4,64,1024]{2,1,0:T(8,128)(2,1)S(1)} collective-permute-done((bf16[4,64,1024]{2,1,0:T(8,128)(2,1)}, bf16[4,64,1024]{2,1,0:T(8,128)(2,1)S(1)}, u32[]{:S(2)}, u32[]{:S(2)}) %collective-permute-start.9) | collective-permute-done | bytes 524320 | tf_op jit(solution)/shard_map/ppermute | solution.py:85
  110.4 2.8 fusion.55
  113.2 8.5 %collective-permute-done.11 = bf16[4,64,1024]{2,1,0:T(8,128)(2,1)S(1)} collective-permute-done((bf16[4,64,1024]{2,1,0:T(8,128)(2,1)S(1)}, bf16[4,64,1024]{2,1,0:T(8,128)(2,1)S(1)}, u32[]{:S(2)}, u32[]{:S(2)}) %collective-permute-start.11) | collective-permute-done | bytes 524320 | tf_op jit(solution)/shard_map/ppermute | solution.py:85
  123.2 9.7 %collective-permute-done.13 = bf16[4,64,1024]{2,1,0:T(8,128)(2,1)S(1)} collective-permute-done((bf16[4,64,1024]{2,1,0:T(8,128)(2,1)S(1)}, bf16[4,64,1024]{2,1,0:T(8,128)(2,1)S(1)}, u32[]{:S(2)}, u32[]{:S(2)}) %collective-permute-start.13) | collective-permute-done | bytes 524320 | tf_op jit(solution)/shard_map/ppermute | solution.py:85
  135.2 7.7 %gather_fusion.9 = bf16[64,4,128,128]{3,2,1,0:T(8,128)(2,1)} fusion(bf16[32,4,128,128]{3,2,1,0:T(8,128)(2,1)} %fusion.59, s32[1024]{0:T(1024)S(1)} %pad_clamp_fusion), kind=kCustom, calls=%fused_computation.9 | custom fusion | bytes 16777472 | tf_op jit(solution)/shard_map/jit(_take)/gather | solution.py:98
  142.9 5.1 %select_reduce_fusion = (f32[4,8,128]{2,1,0:T(8,128)S(1)}, f32[4,8,128,8,128]{2,4,3,1,0:T(8,128)S(1)}) fusion(pred[8,8]{1,0:T(8,128)(4,1)S(1)} %constant_dynamic-slice_fusion, bf16[8,8,4,128,128]{4,3,2,1,0:T(8,128)(2,1)} %bitcast.323, bf16[8,128,4,128,1]{3,2,1,0,4:T(4,128)(2,1)S(1)} %bitcast.327), kind=kOutput, calls=%fused_computation.16 | convolution fusion | flops 1086320640 | bytes 26230848 | tf_op jit(solution)/shard_map/bihd,bmhjd->hbimj/dot_general | solution.py:105
  148.1 3.5 %fusion.161 = f32[4,8,128]{2,1,0:T(8,128)S(1)} fusion(f32[4,8,128]{2,1,0:T(8,128)S(1)} %get-tuple-element.21, f32[4,8,128,8,128]{2,4,3,1,0:T(8,128)S(1)} %get-tuple-element.22, pred[8,8]{1,0:T(8,128)(4,1)S(1)} %constant_dynamic-slice_fusion), kind=kLoop, calls=%fused_computation.223 | loop fusion | flops 16773120 | bytes 16810048 | tf_op jit(solution)/shard_map/reduce_sum | solution.py:114
  151.6 2.2 copy-done.2
  153.8 4.9 %multiply_reduce_fusion.3 = f32[4,8,8,128]{3,2,1,0:T(8,128)S(1)} fusion(f32[4,8,128]{2,1,0:T(8,128)S(1)} %broadcast_divide_fusion.2, f32[4,8,128]{2,1,0:T(8,128)S(1)} %get-tuple-element.21, f32[4,8,128,8,128]{2,4,3,1,0:T(8,128)S(1)} %get-tuple-element.22, pred[8,8]{1,0:T(8,128)(4,1)S(1)} %constant_dynamic-slice_fusion), kind=kLoop, calls=%fused_computation.14 | loop fusion | flops 20938752 | bytes 16941120 | tf_op jit(solution)/shard_map/reduce_sum | solution.py:115
  159.8 4.6 %all-to-all-start = ((f32[8,8,4,128]{3,1,2,0:T(8,128)}), f32[8,8,4,128]{3,1,2,0:T(8,128)S(1)}, u32[]{:S(2)}, u32[]{:S(2)}) async-start(f32[8,8,4,128]{3,1,2,0:T(8,128)} %convolution_bitcast_fusion.2), calls=%async_computation | async-start | bytes 262144 | tf_op jit(solution)/shard_map/all_to_all | solution.py:119
  164.4 2.7 fusion.31
  167.1 2.8 fusion.33
  169.8 2.5 fusion.35
  173.0 5.1 %all-to-all-start.1 = ((f32[8,8,4,128]{3,1,2,0:T(8,128)}), f32[8,8,4,128]{3,1,2,0:T(8,128)S(1)}, u32[]{:S(2)}, u32[]{:S(2)}) async-start(f32[8,8,4,128]{3,1,2,0:T(8,128)} %broadcast_in_dim.119), calls=%async_computation.1 | async-start | bytes 262144 | tf_op jit(solution)/shard_map/all_to_all | solution.py:124
  178.1 2.6 fusion.37
  180.7 4.2 %all-to-all-done.1 = f32[8,8,4,128]{3,1,2,0:T(8,128)S(1)} async-done(((f32[8,8,4,128]{3,1,2,0:T(8,128)}), f32[8,8,4,128]{3,1,2,0:T(8,128)S(1)}, u32[]{:S(2)}, u32[]{:S(2)}) %all-to-all-start.1) | async-done | bytes 131104 | tf_op jit(solution)/shard_map/all_to_all | solution.py:124
  185.2 7.7 %multiply_reduce_fusion.2 = f32[4,8,128]{2,1,0:T(8,128)S(1)} fusion(f32[4,8,8,128]{3,2,1,0:T(8,128)S(1)} %divide_bitcast_fusion.1, f32[4,8,128]{2,1,0:T(8,128)S(1)} %get-tuple-element.21, f32[4,8,128,8,128]{2,4,3,1,0:T(8,128)} %copy-done.2, pred[8,8]{1,0:T(8,128)(4,1)S(1)} %constant_dynamic-slice_fusion), kind=kLoop, calls=%fused_computation.13 | loop fusion | flops 20967424 | bytes 16941120 | tf_op jit(solution)/shard_map/reduce_sum | solution.py:114
  192.9 8.4 %multiply_reduce_fusion.1 = f32[4,8,8,128]{3,2,1,0:T(8,128)S(1)} fusion(f32[4,8,128]{2,1,0:T(8,128)S(1)} %broadcast_divide_fusion.1, f32[4,8,128]{2,1,0:T(8,128)S(1)} %get-tuple-element.21, f32[4,8,128,8,128]{2,4,3,1,0:T(8,128)} %copy-done.2, pred[8,8]{1,0:T(8,128)(4,1)S(1)} %constant_dynamic-slice_fusion), kind=kLoop, calls=%fused_computation.12 | loop fusion | flops 20938752 | bytes 16941120 | tf_op jit(solution)/shard_map/reduce_sum | solution.py:115
  202.3 3.4 %all-to-all-start.2 = ((f32[8,8,4,128]{3,1,2,0:T(8,128)}), f32[8,8,4,128]{3,1,2,0:T(8,128)S(1)}, u32[]{:S(2)}, u32[]{:S(2)}) async-start(f32[8,8,4,128]{3,1,2,0:T(8,128)} %copy.148), calls=%async_computation.2 | async-start | bytes 262144 | tf_op jit(solution)/shard_map/all_to_all | solution.py:119
  205.6 2.7 fusion.39
  208.4 4.0 %all-to-all-done.2 = f32[8,8,4,128]{3,1,2,0:T(8,128)S(1)} async-done(((f32[8,8,4,128]{3,1,2,0:T(8,128)}), f32[8,8,4,128]{3,1,2,0:T(8,128)S(1)}, u32[]{:S(2)}, u32[]{:S(2)}) %all-to-all-start.2) | async-done | bytes 131104 | tf_op jit(solution)/shard_map/all_to_all | solution.py:119
  213.0 3.4 %all-to-all-start.3 = ((f32[8,8,4,128]{3,1,2,0:T(8,128)}), f32[8,8,4,128]{3,1,2,0:T(8,128)S(1)}, u32[]{:S(2)}, u32[]{:S(2)}) async-start(f32[8,8,4,128]{3,1,2,0:T(8,128)} %broadcast_in_dim.120), calls=%async_computation.3 | async-start | bytes 262144 | tf_op jit(solution)/shard_map/all_to_all | solution.py:124
  217.9 5.2 %all-to-all-done.3 = f32[8,8,4,128]{3,1,2,0:T(8,128)S(1)} async-done(((f32[8,8,4,128]{3,1,2,0:T(8,128)}), f32[8,8,4,128]{3,1,2,0:T(8,128)S(1)}, u32[]{:S(2)}, u32[]{:S(2)}) %all-to-all-start.3) | async-done | bytes 131104 | tf_op jit(solution)/shard_map/all_to_all | solution.py:124
  223.4 7.7 %multiply_reduce_fusion = f32[4,8,128]{2,1,0:T(8,128)S(1)} fusion(f32[4,8,8,128]{3,2,1,0:T(8,128)S(1)} %divide_bitcast_fusion, f32[4,8,128]{2,1,0:T(8,128)S(1)} %get-tuple-element.21, f32[4,8,128,8,128]{2,4,3,1,0:T(8,128)} %copy-done.2, pred[8,8]{1,0:T(8,128)(4,1)S(1)} %constant_dynamic-slice_fusion), kind=kLoop, calls=%fused_computation.11 | loop fusion | flops 20967424 | bytes 16941120 | tf_op jit(solution)/shard_map/reduce_sum | solution.py:114
  231.1 8.4 %multiply_reduce_fusion.4 = f32[4,8,8,128]{3,2,1,0:T(8,128)S(1)} fusion(f32[4,8,128]{2,1,0:T(8,128)S(1)} %broadcast_divide_fusion, f32[4,8,128]{2,1,0:T(8,128)S(1)} %get-tuple-element.21, f32[4,8,128,8,128]{2,4,3,1,0:T(8,128)} %copy-done.2, pred[8,8]{1,0:T(8,128)(4,1)S(1)} %constant_dynamic-slice_fusion), kind=kLoop, calls=%fused_computation.17 | loop fusion | flops 20938752 | bytes 16941120 | tf_op jit(solution)/shard_map/reduce_sum | solution.py:115
  240.5 3.4 %all-to-all-start.4 = ((f32[8,8,4,128]{3,1,2,0:T(8,128)}), f32[8,8,4,128]{3,1,2,0:T(8,128)S(1)}, u32[]{:S(2)}, u32[]{:S(2)}) async-start(f32[8,8,4,128]{3,1,2,0:T(8,128)} %copy.150), calls=%async_computation.4 | async-start | bytes 262144 | tf_op jit(solution)/shard_map/all_to_all | solution.py:119
  245.4 7.7 %gather_fusion.8 = bf16[64,4,128,128]{3,2,1,0:T(8,128)(2,1)} fusion(bf16[32,4,128,128]{3,2,1,0:T(8,128)(2,1)} %fusion.43, s32[1024]{0:T(1024)S(1)} %pad_clamp_fusion), kind=kCustom, calls=%fused_computation.8 | custom fusion | bytes 16777472 | tf_op jit(solution)/shard_map/jit(_take)/gather | solution.py:101
  253.8 5.0 %all-to-all-start.5 = ((f32[8,8,4,128]{3,1,2,0:T(8,128)}), f32[8,8,4,128]{3,1,2,0:T(8,128)S(1)}, u32[]{:S(2)}, u32[]{:S(2)}) async-start(f32[8,8,4,128]{3,1,2,0:T(8,128)} %broadcast_in_dim.121), calls=%async_computation.5 | async-start | bytes 262144 | tf_op jit(solution)/shard_map/all_to_all | solution.py:124
  258.8 6.0 %fusion.162 = (bf16[32,4,128,128]{3,2,1,0:T(8,128)(2,1)}, bf16[32,4,128,128]{3,2,1,0:T(8,128)(2,1)}) fusion(bf16[64,4,128,128]{3,2,1,0:T(8,128)(2,1)} %gather_fusion.8), kind=kLoop, calls=%fused_computation.224 | loop fusion | bytes 16777216 | tf_op jit(solution)/shard_map/slice | solution.py:154
  265.8 7.7 %multiply_convert_fusion = bf16[4,8,128,8,128]{2,4,3,1,0:T(8,128)(2,1)S(1)} fusion(f32[4,8,8,128]{3,2,1,0:T(8,128)S(1)} %fusion.73, f32[4,8,128]{2,1,0:T(8,128)S(1)} %broadcast_divide_fusion, f32[4,8,128]{2,1,0:T(8,128)S(1)} %get-tuple-element.21, f32[4,8,128,8,128]{2,4,3,1,0:T(8,128)} %copy-done.2, pred[8,8]{1,0:T(8,128)(4,1)S(1)} %constant_dynamic-slice_fusion), kind=kLoop, calls=%fused_computation.10 | loop fusion | flops 25165824 | bytes 25329728 | tf_op jit(solution)/shard_map/convert_element_type | solution.py:131
  273.5 2.7 fusion.163
  281.6 4.8 %fusion.65 = bf16[4,128,4,128]{1,3,2,0:T(8,128)(2,1)S(1)} fusion(bf16[4,4,128,8,128]{2,4,3,1,0:T(8,128)(2,1)} %get-tuple-element.16, bf16[4,8,4,128,128]{4,3,2,1,0:T(8,128)(2,1)} %bitcast.324), kind=kOutput, calls=%fused_computation.83 | convolution fusion | flops 537133056 | bytes 8912896 | tf_op jit(solution)/shard_map/hbimj,bmhjd->bihd/dot_general | solution.py:151
  286.8 2.3 convolution_convert_fusion.1
  289.6 5.5 %collective-permute-done.14 = bf16[512,512]{1,0:T(8,128)(2,1)S(1)} collective-permute-done((bf16[512,512]{1,0:T(8,128)(2,1)}, bf16[512,512]{1,0:T(8,128)(2,1)S(1)}, u32[]{:S(2)}, u32[]{:S(2)}) %collective-permute-start.14) | collective-permute-done | bytes 524320 | tf_op jit(solution)/shard_map/ppermute | solution.py:159
  296.6 8.6 %collective-permute-done.15 = bf16[512,512]{1,0:T(8,128)(2,1)S(1)} collective-permute-done((bf16[512,512]{1,0:T(8,128)(2,1)}, bf16[512,512]{1,0:T(8,128)(2,1)S(1)}, u32[]{:S(2)}, u32[]{:S(2)}) %collective-permute-start.15) | collective-permute-done | bytes 524320 | tf_op jit(solution)/shard_map/ppermute | solution.py:159
  (145 shorter events, 55.0 us)
Async XLA Ops:
  0.0 56.2 %copy-start = (bf16[1024,512]{1,0:T(8,128)(2,1)S(1)}, bf16[1024,512]{1,0:T(8,128)(2,1)}, u32[]{:S(2)}) copy-start(bf16[1024,512]{1,0:T(8,128)(2,1)} %param.9) | copy-start | bytes 3145732
  2.5 14.8 %copy-start.4 = (s32[64,8]{0,1:T(8,128)S(1)}, s32[64,8]{0,1:T(8,128)}, u32[]{:S(2)}) copy-start(s32[64,8]{0,1:T(8,128)} %param.12) | copy-start | bytes 6148
  5.7 24.9 %collective-permute-start = (bf16[4,64,1024]{2,1,0:T(8,128)(2,1)}, bf16[4,64,1024]{2,1,0:T(8,128)(2,1)}, u32[]{:S(2)}, u32[]{:S(2)}) collective-permute-start(bf16[4,64,1024]{2,1,0:T(8,128)(2,1)} %gather_fusion.1), channel_id=1, source_target_pairs={{0,1},{1,0},{4,5},{5,4},{8,9},{9,8},{12,13},{13,12},{2,3},{3,2},{6... | collective-permute-start | bytes 1572872 | tf_op jit(solution)/shard_map/ppermute | solution.py:83
  7.6 34.9 %collective-permute-start.2 = (bf16[4,64,1024]{2,1,0:T(8,128)(2,1)}, bf16[4,64,1024]{2,1,0:T(8,128)(2,1)}, u32[]{:S(2)}, u32[]{:S(2)}) collective-permute-start(bf16[4,64,1024]{2,1,0:T(8,128)(2,1)} %gather_fusion.2), channel_id=1, source_target_pairs={{0,4},{1,5},{4,0},{5,1},{8,12},{9,13},{12,8},{13,9},{2,6},{3,7},{6... | collective-permute-start | bytes 1572872 | tf_op jit(solution)/shard_map/ppermute | solution.py:83
  11.6 41.8 %collective-permute-start.4 = (bf16[4,64,1024]{2,1,0:T(8,128)(2,1)}, bf16[4,64,1024]{2,1,0:T(8,128)(2,1)}, u32[]{:S(2)}, u32[]{:S(2)}) collective-permute-start(bf16[4,64,1024]{2,1,0:T(8,128)(2,1)} %gather_fusion.3), channel_id=1, source_target_pairs={{0,5},{1,4},{4,1},{5,0},{8,13},{9,12},{12,9},{13,8},{2,7},{3,6},{6... | collective-permute-start | bytes 1572872 | tf_op jit(solution)/shard_map/ppermute | solution.py:83
  13.1 41.7 %collective-permute-start.6 = (bf16[4,64,1024]{2,1,0:T(8,128)(2,1)}, bf16[4,64,1024]{2,1,0:T(8,128)(2,1)}, u32[]{:S(2)}, u32[]{:S(2)}) collective-permute-start(bf16[4,64,1024]{2,1,0:T(8,128)(2,1)} %gather_fusion.4), channel_id=1, source_target_pairs={{0,8},{1,9},{4,12},{5,13},{8,0},{9,1},{12,4},{13,5},{2,10},{3,11},... | collective-permute-start | bytes 1572872 | tf_op jit(solution)/shard_map/ppermute | solution.py:83
  17.3 66.9 %collective-permute-start.8 = (bf16[4,64,1024]{2,1,0:T(8,128)(2,1)}, bf16[4,64,1024]{2,1,0:T(8,128)(2,1)}, u32[]{:S(2)}, u32[]{:S(2)}) collective-permute-start(bf16[4,64,1024]{2,1,0:T(8,128)(2,1)} %gather_fusion.5), channel_id=1, source_target_pairs={{0,9},{1,8},{4,13},{5,12},{8,1},{9,0},{12,5},{13,4},{2,11},{3,10},... | collective-permute-start | bytes 1572872 | tf_op jit(solution)/shard_map/ppermute | solution.py:83
  30.6 27.2 %collective-permute-start.1 = (bf16[4,64,1024]{2,1,0:T(8,128)(2,1)}, bf16[4,64,1024]{2,1,0:T(8,128)(2,1)S(1)}, u32[]{:S(2)}, u32[]{:S(2)}) collective-permute-start(bf16[4,64,1024]{2,1,0:T(8,128)(2,1)} %collective-permute-done), channel_id=1, source_target_pairs={{0,2},{2,0},{1,3},{3,1},{4,6},{6,4},{5,7},{7,5},{8,10},{10,8},{9,1... | collective-permute-start | bytes 1572872 | tf_op jit(solution)/shard_map/ppermute | solution.py:85
  42.5 43.1 %collective-permute-start.10 = (bf16[4,64,1024]{2,1,0:T(8,128)(2,1)}, bf16[4,64,1024]{2,1,0:T(8,128)(2,1)S(1)}, u32[]{:S(2)}, u32[]{:S(2)}) collective-permute-start(bf16[4,64,1024]{2,1,0:T(8,128)(2,1)} %gather_fusion.6), channel_id=1, source_target_pairs={{0,12},{1,13},{4,8},{5,9},{8,4},{9,5},{12,0},{13,1},{2,14},{3,15},... | collective-permute-start | bytes 1572872 | tf_op jit(solution)/shard_map/ppermute | solution.py:83
  53.4 32.8 %collective-permute-start.12 = (bf16[4,64,1024]{2,1,0:T(8,128)(2,1)}, bf16[4,64,1024]{2,1,0:T(8,128)(2,1)S(1)}, u32[]{:S(2)}, u32[]{:S(2)}) collective-permute-start(bf16[4,64,1024]{2,1,0:T(8,128)(2,1)} %gather_fusion.7), channel_id=1, source_target_pairs={{0,13},{1,12},{4,9},{5,8},{8,5},{9,4},{12,1},{13,0},{2,15},{3,14},... | collective-permute-start | bytes 1572872 | tf_op jit(solution)/shard_map/ppermute | solution.py:83
  54.8 32.9 %collective-permute-start.3 = (bf16[4,64,1024]{2,1,0:T(8,128)(2,1)}, bf16[4,64,1024]{2,1,0:T(8,128)(2,1)S(1)}, u32[]{:S(2)}, u32[]{:S(2)}) collective-permute-start(bf16[4,64,1024]{2,1,0:T(8,128)(2,1)} %collective-permute-done.2), channel_id=1, source_target_pairs={{0,2},{2,0},{1,3},{3,1},{4,6},{6,4},{5,7},{7,5},{8,10},{10,8},{9,1... | collective-permute-start | bytes 1572872 | tf_op jit(solution)/shard_map/ppermute | solution.py:85
  57.8 29.9 %copy-start.16 = (bf16[4,64,1024]{2,1,0:T(8,128)(2,1)}, bf16[4,64,1024]{2,1,0:T(8,128)(2,1)S(1)}, u32[]{:S(2)}) copy-start(bf16[4,64,1024]{2,1,0:T(8,128)(2,1)S(1)} %collective-permute-done.1) | copy-start | bytes 1572868
  57.8 33.1 %collective-permute-start.5 = (bf16[4,64,1024]{2,1,0:T(8,128)(2,1)}, bf16[4,64,1024]{2,1,0:T(8,128)(2,1)S(1)}, u32[]{:S(2)}, u32[]{:S(2)}) collective-permute-start(bf16[4,64,1024]{2,1,0:T(8,128)(2,1)} %collective-permute-done.4), channel_id=1, source_target_pairs={{0,2},{2,0},{1,3},{3,1},{4,6},{6,4},{5,7},{7,5},{8,10},{10,8},{9,1... | collective-permute-start | bytes 1572872 | tf_op jit(solution)/shard_map/ppermute | solution.py:85
  84.2 15.0 %collective-permute-start.7 = (bf16[4,64,1024]{2,1,0:T(8,128)(2,1)}, bf16[4,64,1024]{2,1,0:T(8,128)(2,1)S(1)}, u32[]{:S(2)}, u32[]{:S(2)}) collective-permute-start(bf16[4,64,1024]{2,1,0:T(8,128)(2,1)} %collective-permute-done.6), channel_id=1, source_target_pairs={{0,2},{2,0},{1,3},{3,1},{4,6},{6,4},{5,7},{7,5},{8,10},{10,8},{9,1... | collective-permute-start | bytes 1572872 | tf_op jit(solution)/shard_map/ppermute | solution.py:85
  85.6 36.0 %copy-start.9 = (bf16[4,64,1024]{2,1,0:T(8,128)(2,1)}, bf16[4,64,1024]{2,1,0:T(8,128)(2,1)S(1)}, u32[]{:S(2)}) copy-start(bf16[4,64,1024]{2,1,0:T(8,128)(2,1)S(1)} %collective-permute-done.10) | copy-start | bytes 1572868
  85.6 24.8 %collective-permute-start.9 = (bf16[4,64,1024]{2,1,0:T(8,128)(2,1)}, bf16[4,64,1024]{2,1,0:T(8,128)(2,1)S(1)}, u32[]{:S(2)}, u32[]{:S(2)}) collective-permute-start(bf16[4,64,1024]{2,1,0:T(8,128)(2,1)} %collective-permute-done.8), channel_id=1, source_target_pairs={{0,2},{2,0},{1,3},{3,1},{4,6},{6,4},{5,7},{7,5},{8,10},{10,8},{9,1... | collective-permute-start | bytes 1572872 | tf_op jit(solution)/shard_map/ppermute | solution.py:85
  86.2 46.7 %copy-start.7 = (bf16[4,64,1024]{2,1,0:T(8,128)(2,1)}, bf16[4,64,1024]{2,1,0:T(8,128)(2,1)S(1)}, u32[]{:S(2)}) copy-start(bf16[4,64,1024]{2,1,0:T(8,128)(2,1)S(1)} %collective-permute-done.12) | copy-start | bytes 1572868
  86.2 35.4 %collective-permute-start.11 = (bf16[4,64,1024]{2,1,0:T(8,128)(2,1)S(1)}, bf16[4,64,1024]{2,1,0:T(8,128)(2,1)S(1)}, u32[]{:S(2)}, u32[]{:S(2)}) collective-permute-start(bf16[4,64,1024]{2,1,0:T(8,128)(2,1)S(1)} %collective-permute-done.10), channel_id=1, source_target_pairs={{0,2},{2,0},{1,3},{3,1},{4,6},{6,4},{5,7},{7,5},{8,10},{10,8},{9,1... | collective-permute-start | bytes 1572872 | tf_op jit(solution)/shard_map/ppermute | solution.py:85
  87.7 5.9 %copy-start.20 = (bf16[4,64,1024]{2,1,0:T(8,128)(2,1)}, bf16[4,64,1024]{2,1,0:T(8,128)(2,1)S(1)}, u32[]{:S(2)}) copy-start(bf16[4,64,1024]{2,1,0:T(8,128)(2,1)S(1)} %collective-permute-done.3) | copy-start | bytes 1572868
  87.7 45.2 %collective-permute-start.13 = (bf16[4,64,1024]{2,1,0:T(8,128)(2,1)S(1)}, bf16[4,64,1024]{2,1,0:T(8,128)(2,1)S(1)}, u32[]{:S(2)}, u32[]{:S(2)}) collective-permute-start(bf16[4,64,1024]{2,1,0:T(8,128)(2,1)S(1)} %collective-permute-done.12), channel_id=1, source_target_pairs={{0,2},{2,0},{1,3},{3,1},{4,6},{6,4},{5,7},{7,5},{8,10},{10,8},{9,1... | collective-permute-start | bytes 1572872 | tf_op jit(solution)/shard_map/ppermute | solution.py:85
  90.9 11.1 %copy-start.21 = (bf16[4,64,1024]{2,1,0:T(8,128)(2,1)}, bf16[4,64,1024]{2,1,0:T(8,128)(2,1)S(1)}, u32[]{:S(2)}) copy-start(bf16[4,64,1024]{2,1,0:T(8,128)(2,1)S(1)} %collective-permute-done.5) | copy-start | bytes 1572868
  99.2 14.0 %copy-start.18 = (bf16[4,64,1024]{2,1,0:T(8,128)(2,1)}, bf16[4,64,1024]{2,1,0:T(8,128)(2,1)S(1)}, u32[]{:S(2)}) copy-start(bf16[4,64,1024]{2,1,0:T(8,128)(2,1)S(1)} %collective-permute-done.7) | copy-start | bytes 1572868
  110.4 12.7 %copy-start.15 = (bf16[4,64,1024]{2,1,0:T(8,128)(2,1)}, bf16[4,64,1024]{2,1,0:T(8,128)(2,1)S(1)}, u32[]{:S(2)}) copy-start(bf16[4,64,1024]{2,1,0:T(8,128)(2,1)S(1)} %collective-permute-done.9) | copy-start | bytes 1572868
  121.7 11.2 %copy-start.13 = (bf16[4,64,1024]{2,1,0:T(8,128)(2,1)}, bf16[4,64,1024]{2,1,0:T(8,128)(2,1)S(1)}, u32[]{:S(2)}) copy-start(bf16[4,64,1024]{2,1,0:T(8,128)(2,1)S(1)} %collective-permute-done.11) | copy-start | bytes 1572868
  132.9 0.8 copy-start.11
  148.1 5.7 %copy-start.2 = (f32[4,8,128,8,128]{2,4,3,1,0:T(8,128)}, f32[4,8,128,8,128]{2,4,3,1,0:T(8,128)S(1)}, u32[]{:S(2)}) copy-start(f32[4,8,128,8,128]{2,4,3,1,0:T(8,128)S(1)} %get-tuple-element.22) | copy-start | bytes 50331652
  153.8 10.6 %copy-start.5 = (bf16[1024,512]{1,0:T(8,128)(2,1)S(1)}, bf16[1024,512]{1,0:T(8,128)(2,1)}, u32[]{:S(2)}) copy-start(bf16[1024,512]{1,0:T(8,128)(2,1)} %param.10) | copy-start | bytes 3145732
  153.8 10.6 %copy-start.17 = (bf16[4,64,1024]{2,1,0:T(8,128)(2,1)S(1)}, bf16[4,64,1024]{2,1,0:T(8,128)(2,1)}, u32[]{:S(2)}) copy-start(bf16[4,64,1024]{2,1,0:T(8,128)(2,1)} %copy-done.16) | copy-start | bytes 1572868
  159.8 12.6 %all-to-all-start = ((f32[8,8,4,128]{3,1,2,0:T(8,128)}), f32[8,8,4,128]{3,1,2,0:T(8,128)S(1)}, u32[]{:S(2)}, u32[]{:S(2)}) async-start(f32[8,8,4,128]{3,1,2,0:T(8,128)} %convolution_bitcast_fusion.2), calls=%async_computation | async-start | bytes 262144 | tf_op jit(solution)/shard_map/all_to_all | solution.py:119
  164.4 5.5 %copy-start.22 = (bf16[4,64,1024]{2,1,0:T(8,128)(2,1)S(1)}, bf16[4,64,1024]{2,1,0:T(8,128)(2,1)}, u32[]{:S(2)}) copy-start(bf16[4,64,1024]{2,1,0:T(8,128)(2,1)} %copy-done.21) | copy-start | bytes 1572868
  167.1 11.1 %copy-start.19 = (bf16[4,64,1024]{2,1,0:T(8,128)(2,1)S(1)}, bf16[4,64,1024]{2,1,0:T(8,128)(2,1)}, u32[]{:S(2)}) copy-start(bf16[4,64,1024]{2,1,0:T(8,128)(2,1)} %copy-done.18) | copy-start | bytes 1572868
  173.0 11.8 %all-to-all-start.1 = ((f32[8,8,4,128]{3,1,2,0:T(8,128)}), f32[8,8,4,128]{3,1,2,0:T(8,128)S(1)}, u32[]{:S(2)}, u32[]{:S(2)}) async-start(f32[8,8,4,128]{3,1,2,0:T(8,128)} %broadcast_in_dim.119), calls=%async_computation.1 | async-start | bytes 262144 | tf_op jit(solution)/shard_map/all_to_all | solution.py:124
  201.2 15.1 %copy-start.10 = (bf16[4,64,1024]{2,1,0:T(8,128)(2,1)S(1)}, bf16[4,64,1024]{2,1,0:T(8,128)(2,1)}, u32[]{:S(2)}) copy-start(bf16[4,64,1024]{2,1,0:T(8,128)(2,1)} %copy-done.9) | copy-start | bytes 1572868
  201.2 15.1 %copy-start.14 = (bf16[4,64,1024]{2,1,0:T(8,128)(2,1)S(1)}, bf16[4,64,1024]{2,1,0:T(8,128)(2,1)}, u32[]{:S(2)}) copy-start(bf16[4,64,1024]{2,1,0:T(8,128)(2,1)} %copy-done.13) | copy-start | bytes 1572868
  202.3 10.1 %all-to-all-start.2 = ((f32[8,8,4,128]{3,1,2,0:T(8,128)}), f32[8,8,4,128]{3,1,2,0:T(8,128)S(1)}, u32[]{:S(2)}, u32[]{:S(2)}) async-start(f32[8,8,4,128]{3,1,2,0:T(8,128)} %copy.148), calls=%async_computation.2 | async-start | bytes 262144 | tf_op jit(solution)/shard_map/all_to_all | solution.py:119
  213.0 10.1 %all-to-all-start.3 = ((f32[8,8,4,128]{3,1,2,0:T(8,128)}), f32[8,8,4,128]{3,1,2,0:T(8,128)S(1)}, u32[]{:S(2)}, u32[]{:S(2)}) async-start(f32[8,8,4,128]{3,1,2,0:T(8,128)} %broadcast_in_dim.120), calls=%async_computation.3 | async-start | bytes 262144 | tf_op jit(solution)/shard_map/all_to_all | solution.py:124
  231.1 12.8 %copy-start.8 = (bf16[4,64,1024]{2,1,0:T(8,128)(2,1)S(1)}, bf16[4,64,1024]{2,1,0:T(8,128)(2,1)}, u32[]{:S(2)}) copy-start(bf16[4,64,1024]{2,1,0:T(8,128)(2,1)} %copy-done.7) | copy-start | bytes 1572868
  231.1 12.8 %copy-start.12 = (bf16[4,64,1024]{2,1,0:T(8,128)(2,1)S(1)}, bf16[4,64,1024]{2,1,0:T(8,128)(2,1)}, u32[]{:S(2)}) copy-start(bf16[4,64,1024]{2,1,0:T(8,128)(2,1)} %copy-done.11) | copy-start | bytes 1572868
  240.5 12.6 %all-to-all-start.4 = ((f32[8,8,4,128]{3,1,2,0:T(8,128)}), f32[8,8,4,128]{3,1,2,0:T(8,128)S(1)}, u32[]{:S(2)}, u32[]{:S(2)}) async-start(f32[8,8,4,128]{3,1,2,0:T(8,128)} %copy.150), calls=%async_computation.4 | async-start | bytes 262144 | tf_op jit(solution)/shard_map/all_to_all | solution.py:119
  253.8 11.7 %all-to-all-start.5 = ((f32[8,8,4,128]{3,1,2,0:T(8,128)}), f32[8,8,4,128]{3,1,2,0:T(8,128)S(1)}, u32[]{:S(2)}, u32[]{:S(2)}) async-start(f32[8,8,4,128]{3,1,2,0:T(8,128)} %broadcast_in_dim.121), calls=%async_computation.5 | async-start | bytes 262144 | tf_op jit(solution)/shard_map/all_to_all | solution.py:124
  273.5 3.7 %copy-start.3 = (bf16[32,4,128,128]{3,2,1,0:T(8,128)(2,1)S(1)}, bf16[32,4,128,128]{3,2,1,0:T(8,128)(2,1)}, u32[]{:S(2)}) copy-start(bf16[32,4,128,128]{3,2,1,0:T(8,128)(2,1)} %get-tuple-element.13) | copy-start | bytes 12582916
  277.2 1.7 copy-start.6
  280.2 15.0 %collective-permute-start.14 = (bf16[512,512]{1,0:T(8,128)(2,1)}, bf16[512,512]{1,0:T(8,128)(2,1)S(1)}, u32[]{:S(2)}, u32[]{:S(2)}) collective-permute-start(bf16[512,512]{1,0:T(8,128)(2,1)} %convolution_convert_fusion.2), channel_id=1, source_target_pairs={{0,2},{2,0},{1,3},{3,1},{4,6},{6,4},{5,7},{7,5},{8,10},{10,8},{9,1... | collective-permute-start | bytes 1572872 | tf_op jit(solution)/shard_map/ppermute | solution.py:159
  286.5 21.3 %copy-start.1 = (bf16[1024,512]{1,0:T(8,128)(2,1)S(1)}, bf16[1024,512]{1,0:T(8,128)(2,1)}, u32[]{:S(2)}) copy-start(bf16[1024,512]{1,0:T(8,128)(2,1)} %param.9) | copy-start | bytes 3145732
  289.1 16.2 %collective-permute-start.15 = (bf16[512,512]{1,0:T(8,128)(2,1)}, bf16[512,512]{1,0:T(8,128)(2,1)S(1)}, u32[]{:S(2)}, u32[]{:S(2)}) collective-permute-start(bf16[512,512]{1,0:T(8,128)(2,1)} %convolution_convert_fusion.1), channel_id=1, source_target_pairs={{0,2},{2,0},{1,3},{3,1},{4,6},{6,4},{5,7},{7,5},{8,10},{10,8},{9,1... | collective-permute-start | bytes 1572872 | tf_op jit(solution)/shard_map/ppermute | solution.py:159

commit v7 on v5

--- a/solution.py
+++ b/solution.py
@@ -107,7 +107,7 @@
     ) * HS ** (-0.5)
     valid_mask = my_valid[None, :, None, :, None]
     row_max = jnp.max(jnp.where(valid_mask, scores, -1e30), axis=(3, 4), keepdims=True)
-    weights = jnp.where(valid_mask, jnp.exp(scores - row_max), 0.0)
+    weights = lax.optimization_barrier(jnp.where(valid_mask, jnp.exp(scores - row_max), 0.0))
     column_scale = jnp.ones(weights.shape[:2] + weights.shape[3:], jnp.float32)
     onehot = matches.astype(jnp.float32)
     for round_number in range(BALANCING_ROUNDS):

time: 309 us -> 319 us (1.032)
  other arithmetic: 44.9 us -> 58.7 us
    select_n x0 -> x1, other arithmetic: none -> 6.72 us  [body(): jnp.where(valid_mask, jnp.exp(scores - row_max), 0.0)]
    reduce_sum x3, other arithmetic: 18.8 us -> 22.9 us  [body(): row_scale = 1.0 / jnp.sum(weights * column_scale[:, :, None], axis=(3, 4))]
  transfers between devices with their start and end apart: 21 -> 21, of which waited for: 13 -> 13; matrix products, arithmetic and copies ran while one was open for 21% -> 20% of each run, Pallas kernels for 0% -> 0%
where the time goes in v7:
time: 319 us; the launch traced here: 317 us
  waiting for transfers between devices  114 us (36%)
  matrix products  67.1 us (21%)
  other arithmetic  58.7 us (18%)
  starting transfers between devices  40.3 us (13%)
  local copies, waits for them, and re-layouts  36.6 us (11%)
    ppermute x7, waiting for transfers between devices, body(): got = lax.ppermute(piece, ('seq', 'sub'), perm=pairs)  39.9 us
    ppermute x7, waiting for transfers between devices, body(): partner = lax.ppermute(got, 'head', perm=[(0, 1), (1, 0)])  32.3 us
    reduce_sum x3, other arithmetic, body(): jnp.sum(weights * row_scale[:, :, :, None, None], axis=2)  24.8 us
    ppermute x1, waiting for transfers between devices, body(): lax.ppermute(other_part.astype(jnp.bfloat16), 'head', perm=[(0, 1), (1, 0)])  24 us
    reduce_sum x3, other arithmetic, body(): row_scale = 1.0 / jnp.sum(weights * column_scale[:, :, None], axis=(3, 4))  22.9 us
    dot_general x8, matrix products, body(): jnp.einsum('cjf,fhd->chjd', full, value_weights, preferred_element_type=j...  21 us
    dot_general x8, matrix products, body(): jnp.einsum('cjf,fhd->chjd', full, key_weights, preferred_element_type=jnp...  18 us
    dot_general x1, matrix products, body(): jnp.einsum('hbimj,bmhjd->bihd', probabilities, value_slots, preferred_ele...  11.8 us
  transfers between devices with their start and end apart: 21, of which 13 were waited for; matrix products, arithmetic and copies ran while one was open for 20% of the time, Pallas kernels for 0%

profile of v7, /device:TPU:0, one launch (start us, length us, event | category | flops | bytes accessed | tf_op | source)
XLA Modules:
  0.0 317.3 jit_solution(2475316525428806160)
XLA Ops:
  2.5 1.8 constant_dynamic-slice_fusion.11
  7.6 2.6 collective-permute-start.2
  13.1 2.8 collective-permute-start.6
  18.3 4.1 %convolution_convert_fusion = bf16[1024,512]{1,0:T(8,128)(2,1)} fusion(bf16[1024,1024]{1,0:T(8,128)(2,1)} %param.7, bf16[1024,512]{1,0:T(8,128)(2,1)} %param.8), kind=kOutput, calls=%fused_computation.26 | convolution fusion | flops 1074266112 | bytes 4194304 | tf_op jit(solution)/shard_map/dot_general | solution.py:26
  28.4 2.2 gather_fusion
  32.2 2.8 fusion.15
  35.0 7.6 %collective-permute-done.2 = bf16[4,64,1024]{2,1,0:T(8,128)(2,1)} collective-permute-done((bf16[4,64,1024]{2,1,0:T(8,128)(2,1)}, bf16[4,64,1024]{2,1,0:T(8,128)(2,1)}, u32[]{:S(2)}, u32[]{:S(2)}) %collective-permute-start.2) | collective-permute-done | bytes 524320 | tf_op jit(solution)/shard_map/ppermute | solution.py:83
  44.3 9.1 %collective-permute-done.4 = bf16[4,64,1024]{2,1,0:T(8,128)(2,1)} collective-permute-done((bf16[4,64,1024]{2,1,0:T(8,128)(2,1)}, bf16[4,64,1024]{2,1,0:T(8,128)(2,1)}, u32[]{:S(2)}, u32[]{:S(2)}) %collective-permute-start.4) | collective-permute-done | bytes 524320 | tf_op jit(solution)/shard_map/ppermute | solution.py:83
  58.3 2.6 fusion.33
  61.0 23.2 %collective-permute-done.8 = bf16[4,64,1024]{2,1,0:T(8,128)(2,1)} collective-permute-done((bf16[4,64,1024]{2,1,0:T(8,128)(2,1)}, bf16[4,64,1024]{2,1,0:T(8,128)(2,1)}, u32[]{:S(2)}, u32[]{:S(2)}) %collective-permute-start.8) | collective-permute-done | bytes 524320 | tf_op jit(solution)/shard_map/ppermute | solution.py:83
  88.3 2.5 fusion.35
  90.9 2.7 fusion.37
  93.6 5.6 %collective-permute-done.7 = bf16[4,64,1024]{2,1,0:T(8,128)(2,1)S(1)} collective-permute-done((bf16[4,64,1024]{2,1,0:T(8,128)(2,1)}, bf16[4,64,1024]{2,1,0:T(8,128)(2,1)S(1)}, u32[]{:S(2)}, u32[]{:S(2)}) %collective-permute-start.7) | collective-permute-done | bytes 524320 | tf_op jit(solution)/shard_map/ppermute | solution.py:85
  99.2 2.8 fusion.39
  102.0 8.5 %collective-permute-done.9 = bf16[4,64,1024]{2,1,0:T(8,128)(2,1)S(1)} collective-permute-done((bf16[4,64,1024]{2,1,0:T(8,128)(2,1)}, bf16[4,64,1024]{2,1,0:T(8,128)(2,1)S(1)}, u32[]{:S(2)}, u32[]{:S(2)}) %collective-permute-start.9) | collective-permute-done | bytes 524320 | tf_op jit(solution)/shard_map/ppermute | solution.py:85
  110.4 2.8 fusion.41
  113.2 8.5 %collective-permute-done.11 = bf16[4,64,1024]{2,1,0:T(8,128)(2,1)S(1)} collective-permute-done((bf16[4,64,1024]{2,1,0:T(8,128)(2,1)S(1)}, bf16[4,64,1024]{2,1,0:T(8,128)(2,1)S(1)}, u32[]{:S(2)}, u32[]{:S(2)}) %collective-permute-start.11) | collective-permute-done | bytes 524320 | tf_op jit(solution)/shard_map/ppermute | solution.py:85
  123.2 9.7 %collective-permute-done.13 = bf16[4,64,1024]{2,1,0:T(8,128)(2,1)S(1)} collective-permute-done((bf16[4,64,1024]{2,1,0:T(8,128)(2,1)S(1)}, bf16[4,64,1024]{2,1,0:T(8,128)(2,1)S(1)}, u32[]{:S(2)}, u32[]{:S(2)}) %collective-permute-start.13) | collective-permute-done | bytes 524320 | tf_op jit(solution)/shard_map/ppermute | solution.py:85
  135.2 7.7 %gather_fusion.9 = bf16[64,4,128,128]{3,2,1,0:T(8,128)(2,1)} fusion(bf16[32,4,128,128]{3,2,1,0:T(8,128)(2,1)} %fusion.45, s32[1024]{0:T(1024)S(1)} %pad_clamp_fusion), kind=kCustom, calls=%fused_computation.9 | custom fusion | bytes 16777472 | tf_op jit(solution)/shard_map/jit(_take)/gather | solution.py:98
  142.9 5.1 %select_reduce_fusion = (f32[4,8,128]{2,1,0:T(8,128)S(1)}, f32[4,8,128,8,128]{2,4,3,1,0:T(8,128)S(1)}) fusion(pred[8,8]{1,0:T(8,128)(4,1)S(1)} %constant_dynamic-slice_fusion, bf16[8,8,4,128,128]{4,3,2,1,0:T(8,128)(2,1)} %bitcast.305, bf16[8,128,4,128,1]{3,2,1,0,4:T(4,128)(2,1)S(1)} %bitcast.307), kind=kOutput, calls=%fused_computation.16 | convolution fusion | flops 1086320640 | bytes 26230848 | tf_op jit(solution)/shard_map/bihd,bmhjd->hbimj/dot_general | solution.py:105
  148.1 6.7 %exponential_select_fusion = f32[4,8,128,8,128]{2,4,3,1,0:T(8,128)} fusion(f32[4,8,128,8,128]{2,4,3,1,0:T(8,128)S(1)} %get-tuple-element.18, f32[4,8,128]{2,1,0:T(8,128)S(1)} %get-tuple-element.17, pred[8,8]{1,0:T(8,128)(4,1)S(1)} %constant_dynamic-slice_fusion), kind=kLoop, calls=%fused_computation.15 | loop fusion | flops 12582912 | bytes 33570880 | tf_op jit(solution)/shard_map/jit(_where)/select_n | solution.py:110
  154.8 7.7 %reduce_sum.101 = f32[4,8,128]{2,1,0:T(8,128)S(1)} reduce(f32[4,8,128,8,128]{2,4,3,1,0:T(8,128)} %exponential_select_fusion, f32[]{:T(128)} %constant.55.clone.1), dimensions={3,4}, to_apply=%region_8.9 | reduce | flops 4190208 | bytes 16793604 | tf_op jit(solution)/shard_map/reduce_sum | solution.py:114
  162.6 8.3 %multiply_reduce_fusion.3 = f32[4,8,8,128]{3,2,1,0:T(8,128)S(1)} fusion(f32[4,8,128,8,128]{2,4,3,1,0:T(8,128)} %exponential_select_fusion, f32[4,8,128]{2,1,0:T(8,128)S(1)} %broadcast_divide_fusion.2), kind=kLoop, calls=%fused_computation.14 | loop fusion | flops 8355840 | bytes 16924672 | tf_op jit(solution)/shard_map/reduce_sum | solution.py:115
  171.9 4.6 %all-to-all-start = ((f32[8,8,4,128]{3,1,2,0:T(8,128)}), f32[8,8,4,128]{3,1,2,0:T(8,128)S(1)}, u32[]{:S(2)}, u32[]{:S(2)}) async-start(f32[8,8,4,128]{3,1,2,0:T(8,128)} %convolution_bitcast_fusion.2), calls=%async_computation | async-start | bytes 262144 | tf_op jit(solution)/shard_map/all_to_all | solution.py:119
  176.5 2.7 fusion.17
  179.2 2.7 fusion.19
  183.9 3.8 %all-to-all-start.1 = ((f32[8,8,4,128]{3,1,2,0:T(8,128)}), f32[8,8,4,128]{3,1,2,0:T(8,128)S(1)}, u32[]{:S(2)}, u32[]{:S(2)}) async-start(f32[8,8,4,128]{3,1,2,0:T(8,128)} %broadcast_in_dim.119), calls=%async_computation.1 | async-start | bytes 262144 | tf_op jit(solution)/shard_map/all_to_all | solution.py:124
  187.7 2.5 fusion.21
  190.2 4.2 %all-to-all-done.1 = f32[8,8,4,128]{3,1,2,0:T(8,128)S(1)} async-done(((f32[8,8,4,128]{3,1,2,0:T(8,128)}), f32[8,8,4,128]{3,1,2,0:T(8,128)S(1)}, u32[]{:S(2)}, u32[]{:S(2)}) %all-to-all-start.1) | async-done | bytes 131104 | tf_op jit(solution)/shard_map/all_to_all | solution.py:124
  194.7 7.6 %multiply_reduce_fusion.2 = f32[4,8,128]{2,1,0:T(8,128)S(1)} fusion(f32[4,8,128,8,128]{2,4,3,1,0:T(8,128)} %exponential_select_fusion, f32[4,8,8,128]{3,2,1,0:T(8,128)S(1)} %divide_bitcast_fusion.1), kind=kLoop, calls=%fused_computation.13 | loop fusion | flops 8384512 | bytes 16924672 | tf_op jit(solution)/shard_map/reduce_sum | solution.py:114
  202.3 8.2 %multiply_reduce_fusion.1 = f32[4,8,8,128]{3,2,1,0:T(8,128)S(1)} fusion(f32[4,8,128,8,128]{2,4,3,1,0:T(8,128)} %exponential_select_fusion, f32[4,8,128]{2,1,0:T(8,128)S(1)} %broadcast_divide_fusion.1), kind=kLoop, calls=%fused_computation.12 | loop fusion | flops 8355840 | bytes 16924672 | tf_op jit(solution)/shard_map/reduce_sum | solution.py:115
  211.6 3.4 %all-to-all-start.2 = ((f32[8,8,4,128]{3,1,2,0:T(8,128)}), f32[8,8,4,128]{3,1,2,0:T(8,128)S(1)}, u32[]{:S(2)}, u32[]{:S(2)}) async-start(f32[8,8,4,128]{3,1,2,0:T(8,128)} %copy.168), calls=%async_computation.2 | async-start | bytes 262144 | tf_op jit(solution)/shard_map/all_to_all | solution.py:119
  215.0 2.6 fusion.23
  217.6 4.1 %all-to-all-done.2 = f32[8,8,4,128]{3,1,2,0:T(8,128)S(1)} async-done(((f32[8,8,4,128]{3,1,2,0:T(8,128)}), f32[8,8,4,128]{3,1,2,0:T(8,128)S(1)}, u32[]{:S(2)}, u32[]{:S(2)}) %all-to-all-start.2) | async-done | bytes 131104 | tf_op jit(solution)/shard_map/all_to_all | solution.py:119
  222.3 3.4 %all-to-all-start.3 = ((f32[8,8,4,128]{3,1,2,0:T(8,128)}), f32[8,8,4,128]{3,1,2,0:T(8,128)S(1)}, u32[]{:S(2)}, u32[]{:S(2)}) async-start(f32[8,8,4,128]{3,1,2,0:T(8,128)} %broadcast_in_dim.120), calls=%async_computation.3 | async-start | bytes 262144 | tf_op jit(solution)/shard_map/all_to_all | solution.py:124
  225.7 2.6 fusion.25
  228.3 4.1 %all-to-all-done.3 = f32[8,8,4,128]{3,1,2,0:T(8,128)S(1)} async-done(((f32[8,8,4,128]{3,1,2,0:T(8,128)}), f32[8,8,4,128]{3,1,2,0:T(8,128)S(1)}, u32[]{:S(2)}, u32[]{:S(2)}) %all-to-all-start.3) | async-done | bytes 131104 | tf_op jit(solution)/shard_map/all_to_all | solution.py:124
  232.7 7.6 %multiply_reduce_fusion = f32[4,8,128]{2,1,0:T(8,128)S(1)} fusion(f32[4,8,128,8,128]{2,4,3,1,0:T(8,128)} %exponential_select_fusion, f32[4,8,8,128]{3,2,1,0:T(8,128)S(1)} %divide_bitcast_fusion), kind=kLoop, calls=%fused_computation.11 | loop fusion | flops 8384512 | bytes 16924672 | tf_op jit(solution)/shard_map/reduce_sum | solution.py:114
  240.3 8.2 %multiply_reduce_fusion.4 = f32[4,8,8,128]{3,2,1,0:T(8,128)S(1)} fusion(f32[4,8,128,8,128]{2,4,3,1,0:T(8,128)} %exponential_select_fusion, f32[4,8,128]{2,1,0:T(8,128)S(1)} %broadcast_divide_fusion), kind=kLoop, calls=%fused_computation.17 | loop fusion | flops 8355840 | bytes 16924672 | tf_op jit(solution)/shard_map/reduce_sum | solution.py:115
  249.6 3.4 %all-to-all-start.4 = ((f32[8,8,4,128]{3,1,2,0:T(8,128)}), f32[8,8,4,128]{3,1,2,0:T(8,128)S(1)}, u32[]{:S(2)}, u32[]{:S(2)}) async-start(f32[8,8,4,128]{3,1,2,0:T(8,128)} %copy.170), calls=%async_computation.4 | async-start | bytes 262144 | tf_op jit(solution)/shard_map/all_to_all | solution.py:119
  253.0 2.5 fusion.27
  255.5 4.1 %all-to-all-done.4 = f32[8,8,4,128]{3,1,2,0:T(8,128)S(1)} async-done(((f32[8,8,4,128]{3,1,2,0:T(8,128)}), f32[8,8,4,128]{3,1,2,0:T(8,128)S(1)}, u32[]{:S(2)}, u32[]{:S(2)}) %all-to-all-start.4) | async-done | bytes 131104 | tf_op jit(solution)/shard_map/all_to_all | solution.py:119
  260.3 3.6 %all-to-all-start.5 = ((f32[8,8,4,128]{3,1,2,0:T(8,128)}), f32[8,8,4,128]{3,1,2,0:T(8,128)S(1)}, u32[]{:S(2)}, u32[]{:S(2)}) async-start(f32[8,8,4,128]{3,1,2,0:T(8,128)} %broadcast_in_dim.121), calls=%async_computation.5 | async-start | bytes 262144 | tf_op jit(solution)/shard_map/all_to_all | solution.py:124
  264.0 2.6 fusion.29
  266.5 7.7 %gather_fusion.8 = bf16[64,4,128,128]{3,2,1,0:T(8,128)(2,1)} fusion(bf16[32,4,128,128]{3,2,1,0:T(8,128)(2,1)} %fusion.29, s32[1024]{0:T(1024)S(1)} %pad_clamp_fusion), kind=kCustom, calls=%fused_computation.8 | custom fusion | bytes 16777472 | tf_op jit(solution)/shard_map/jit(_take)/gather | solution.py:101
  274.5 11.8 %fusion.9 = bf16[8,128,4,128]{1,3,2,0:T(8,128)(2,1)S(1)} fusion(bf16[8,8,4,128,128]{4,3,2,1,0:T(8,128)(2,1)} %bitcast.304, f32[4,8,128,8,128]{2,4,3,1,0:T(8,128)} %exponential_select_fusion, f32[4,8,8,128]{3,2,1,0:T(8,128)S(1)} %fusion.49, f32[4,8,128]{2,1,0:T(8,128)S(1)} %broadcast_divide_fusion), kind=kOutput, calls=%fused_computation.28 | convolution fusion | flops 1086849024 | bytes 26361856 | tf_op jit(solution)/shard_map/hbimj,bmhjd->bihd/dot_general | solution.py:132
  290.3 24.0 %collective-permute-done.14 = bf16[1024,512]{1,0:T(8,128)(2,1)} collective-permute-done((bf16[1024,512]{1,0:T(8,128)(2,1)}, bf16[1024,512]{1,0:T(8,128)(2,1)}, u32[]{:S(2)}, u32[]{:S(2)}) %collective-permute-start.14) | collective-permute-done | bytes 1048608 | tf_op jit(solution)/shard_map/ppermute | solution.py:147
  314.3 3.0 add_convert_fusion
  (130 shorter events, 44.5 us)
Async XLA Ops:
  0.0 56.2 %copy-start = (bf16[1024,512]{1,0:T(8,128)(2,1)S(1)}, bf16[1024,512]{1,0:T(8,128)(2,1)}, u32[]{:S(2)}) copy-start(bf16[1024,512]{1,0:T(8,128)(2,1)} %param.9) | copy-start | bytes 3145732
  2.5 14.8 %copy-start.2 = (s32[64,8]{0,1:T(8,128)S(1)}, s32[64,8]{0,1:T(8,128)}, u32[]{:S(2)}) copy-start(s32[64,8]{0,1:T(8,128)} %param.12) | copy-start | bytes 6148
  5.7 24.9 %collective-permute-start = (bf16[4,64,1024]{2,1,0:T(8,128)(2,1)}, bf16[4,64,1024]{2,1,0:T(8,128)(2,1)}, u32[]{:S(2)}, u32[]{:S(2)}) collective-permute-start(bf16[4,64,1024]{2,1,0:T(8,128)(2,1)} %gather_fusion.1), channel_id=1, source_target_pairs={{0,1},{1,0},{4,5},{5,4},{8,9},{9,8},{12,13},{13,12},{2,3},{3,2},{6... | collective-permute-start | bytes 1572872 | tf_op jit(solution)/shard_map/ppermute | solution.py:83
  7.6 34.9 %collective-permute-start.2 = (bf16[4,64,1024]{2,1,0:T(8,128)(2,1)}, bf16[4,64,1024]{2,1,0:T(8,128)(2,1)}, u32[]{:S(2)}, u32[]{:S(2)}) collective-permute-start(bf16[4,64,1024]{2,1,0:T(8,128)(2,1)} %gather_fusion.2), channel_id=1, source_target_pairs={{0,4},{1,5},{4,0},{5,1},{8,12},{9,13},{12,8},{13,9},{2,6},{3,7},{6... | collective-permute-start | bytes 1572872 | tf_op jit(solution)/shard_map/ppermute | solution.py:83
  11.6 41.8 %collective-permute-start.4 = (bf16[4,64,1024]{2,1,0:T(8,128)(2,1)}, bf16[4,64,1024]{2,1,0:T(8,128)(2,1)}, u32[]{:S(2)}, u32[]{:S(2)}) collective-permute-start(bf16[4,64,1024]{2,1,0:T(8,128)(2,1)} %gather_fusion.3), channel_id=1, source_target_pairs={{0,5},{1,4},{4,1},{5,0},{8,13},{9,12},{12,9},{13,8},{2,7},{3,6},{6... | collective-permute-start | bytes 1572872 | tf_op jit(solution)/shard_map/ppermute | solution.py:83
  13.1 41.7 %collective-permute-start.6 = (bf16[4,64,1024]{2,1,0:T(8,128)(2,1)}, bf16[4,64,1024]{2,1,0:T(8,128)(2,1)}, u32[]{:S(2)}, u32[]{:S(2)}) collective-permute-start(bf16[4,64,1024]{2,1,0:T(8,128)(2,1)} %gather_fusion.4), channel_id=1, source_target_pairs={{0,8},{1,9},{4,12},{5,13},{8,0},{9,1},{12,4},{13,5},{2,10},{3,11},... | collective-permute-start | bytes 1572872 | tf_op jit(solution)/shard_map/ppermute | solution.py:83
  17.3 66.9 %collective-permute-start.8 = (bf16[4,64,1024]{2,1,0:T(8,128)(2,1)}, bf16[4,64,1024]{2,1,0:T(8,128)(2,1)}, u32[]{:S(2)}, u32[]{:S(2)}) collective-permute-start(bf16[4,64,1024]{2,1,0:T(8,128)(2,1)} %gather_fusion.5), channel_id=1, source_target_pairs={{0,9},{1,8},{4,13},{5,12},{8,1},{9,0},{12,5},{13,4},{2,11},{3,10},... | collective-permute-start | bytes 1572872 | tf_op jit(solution)/shard_map/ppermute | solution.py:83
  30.6 27.2 %collective-permute-start.1 = (bf16[4,64,1024]{2,1,0:T(8,128)(2,1)}, bf16[4,64,1024]{2,1,0:T(8,128)(2,1)S(1)}, u32[]{:S(2)}, u32[]{:S(2)}) collective-permute-start(bf16[4,64,1024]{2,1,0:T(8,128)(2,1)} %collective-permute-done), channel_id=1, source_target_pairs={{0,2},{2,0},{1,3},{3,1},{4,6},{6,4},{5,7},{7,5},{8,10},{10,8},{9,1... | collective-permute-start | bytes 1572872 | tf_op jit(solution)/shard_map/ppermute | solution.py:85
  42.5 43.1 %collective-permute-start.10 = (bf16[4,64,1024]{2,1,0:T(8,128)(2,1)}, bf16[4,64,1024]{2,1,0:T(8,128)(2,1)S(1)}, u32[]{:S(2)}, u32[]{:S(2)}) collective-permute-start(bf16[4,64,1024]{2,1,0:T(8,128)(2,1)} %gather_fusion.6), channel_id=1, source_target_pairs={{0,12},{1,13},{4,8},{5,9},{8,4},{9,5},{12,0},{13,1},{2,14},{3,15},... | collective-permute-start | bytes 1572872 | tf_op jit(solution)/shard_map/ppermute | solution.py:83
  53.4 32.8 %collective-permute-start.12 = (bf16[4,64,1024]{2,1,0:T(8,128)(2,1)}, bf16[4,64,1024]{2,1,0:T(8,128)(2,1)S(1)}, u32[]{:S(2)}, u32[]{:S(2)}) collective-permute-start(bf16[4,64,1024]{2,1,0:T(8,128)(2,1)} %gather_fusion.7), channel_id=1, source_target_pairs={{0,13},{1,12},{4,9},{5,8},{8,5},{9,4},{12,1},{13,0},{2,15},{3,14},... | collective-permute-start | bytes 1572872 | tf_op jit(solution)/shard_map/ppermute | solution.py:83
  54.8 32.9 %collective-permute-start.3 = (bf16[4,64,1024]{2,1,0:T(8,128)(2,1)}, bf16[4,64,1024]{2,1,0:T(8,128)(2,1)S(1)}, u32[]{:S(2)}, u32[]{:S(2)}) collective-permute-start(bf16[4,64,1024]{2,1,0:T(8,128)(2,1)} %collective-permute-done.2), channel_id=1, source_target_pairs={{0,2},{2,0},{1,3},{3,1},{4,6},{6,4},{5,7},{7,5},{8,10},{10,8},{9,1... | collective-permute-start | bytes 1572872 | tf_op jit(solution)/shard_map/ppermute | solution.py:85
  57.8 29.9 %copy-start.15 = (bf16[4,64,1024]{2,1,0:T(8,128)(2,1)}, bf16[4,64,1024]{2,1,0:T(8,128)(2,1)S(1)}, u32[]{:S(2)}) copy-start(bf16[4,64,1024]{2,1,0:T(8,128)(2,1)S(1)} %collective-permute-done.1) | copy-start | bytes 1572868
  57.8 33.1 %collective-permute-start.5 = (bf16[4,64,1024]{2,1,0:T(8,128)(2,1)}, bf16[4,64,1024]{2,1,0:T(8,128)(2,1)S(1)}, u32[]{:S(2)}, u32[]{:S(2)}) collective-permute-start(bf16[4,64,1024]{2,1,0:T(8,128)(2,1)} %collective-permute-done.4), channel_id=1, source_target_pairs={{0,2},{2,0},{1,3},{3,1},{4,6},{6,4},{5,7},{7,5},{8,10},{10,8},{9,1... | collective-permute-start | bytes 1572872 | tf_op jit(solution)/shard_map/ppermute | solution.py:85
  84.2 15.0 %collective-permute-start.7 = (bf16[4,64,1024]{2,1,0:T(8,128)(2,1)}, bf16[4,64,1024]{2,1,0:T(8,128)(2,1)S(1)}, u32[]{:S(2)}, u32[]{:S(2)}) collective-permute-start(bf16[4,64,1024]{2,1,0:T(8,128)(2,1)} %collective-permute-done.6), channel_id=1, source_target_pairs={{0,2},{2,0},{1,3},{3,1},{4,6},{6,4},{5,7},{7,5},{8,10},{10,8},{9,1... | collective-permute-start | bytes 1572872 | tf_op jit(solution)/shard_map/ppermute | solution.py:85
  85.6 36.0 %copy-start.7 = (bf16[4,64,1024]{2,1,0:T(8,128)(2,1)}, bf16[4,64,1024]{2,1,0:T(8,128)(2,1)S(1)}, u32[]{:S(2)}) copy-start(bf16[4,64,1024]{2,1,0:T(8,128)(2,1)S(1)} %collective-permute-done.10) | copy-start | bytes 1572868
  85.6 24.8 %collective-permute-start.9 = (bf16[4,64,1024]{2,1,0:T(8,128)(2,1)}, bf16[4,64,1024]{2,1,0:T(8,128)(2,1)S(1)}, u32[]{:S(2)}, u32[]{:S(2)}) collective-permute-start(bf16[4,64,1024]{2,1,0:T(8,128)(2,1)} %collective-permute-done.8), channel_id=1, source_target_pairs={{0,2},{2,0},{1,3},{3,1},{4,6},{6,4},{5,7},{7,5},{8,10},{10,8},{9,1... | collective-permute-start | bytes 1572872 | tf_op jit(solution)/shard_map/ppermute | solution.py:85
  86.2 46.7 %copy-start.5 = (bf16[4,64,1024]{2,1,0:T(8,128)(2,1)}, bf16[4,64,1024]{2,1,0:T(8,128)(2,1)S(1)}, u32[]{:S(2)}) copy-start(bf16[4,64,1024]{2,1,0:T(8,128)(2,1)S(1)} %collective-permute-done.12) | copy-start | bytes 1572868
  86.2 35.4 %collective-permute-start.11 = (bf16[4,64,1024]{2,1,0:T(8,128)(2,1)S(1)}, bf16[4,64,1024]{2,1,0:T(8,128)(2,1)S(1)}, u32[]{:S(2)}, u32[]{:S(2)}) collective-permute-start(bf16[4,64,1024]{2,1,0:T(8,128)(2,1)S(1)} %collective-permute-done.10), channel_id=1, source_target_pairs={{0,2},{2,0},{1,3},{3,1},{4,6},{6,4},{5,7},{7,5},{8,10},{10,8},{9,1... | collective-permute-start | bytes 1572872 | tf_op jit(solution)/shard_map/ppermute | solution.py:85
  87.7 5.9 %copy-start.19 = (bf16[4,64,1024]{2,1,0:T(8,128)(2,1)}, bf16[4,64,1024]{2,1,0:T(8,128)(2,1)S(1)}, u32[]{:S(2)}) copy-start(bf16[4,64,1024]{2,1,0:T(8,128)(2,1)S(1)} %collective-permute-done.3) | copy-start | bytes 1572868
  87.7 45.2 %collective-permute-start.13 = (bf16[4,64,1024]{2,1,0:T(8,128)(2,1)S(1)}, bf16[4,64,1024]{2,1,0:T(8,128)(2,1)S(1)}, u32[]{:S(2)}, u32[]{:S(2)}) collective-permute-start(bf16[4,64,1024]{2,1,0:T(8,128)(2,1)S(1)} %collective-permute-done.12), channel_id=1, source_target_pairs={{0,2},{2,0},{1,3},{3,1},{4,6},{6,4},{5,7},{7,5},{8,10},{10,8},{9,1... | collective-permute-start | bytes 1572872 | tf_op jit(solution)/shard_map/ppermute | solution.py:85
  90.9 11.1 %copy-start.17 = (bf16[4,64,1024]{2,1,0:T(8,128)(2,1)}, bf16[4,64,1024]{2,1,0:T(8,128)(2,1)S(1)}, u32[]{:S(2)}) copy-start(bf16[4,64,1024]{2,1,0:T(8,128)(2,1)S(1)} %collective-permute-done.5) | copy-start | bytes 1572868
  99.2 14.0 %copy-start.13 = (bf16[4,64,1024]{2,1,0:T(8,128)(2,1)}, bf16[4,64,1024]{2,1,0:T(8,128)(2,1)S(1)}, u32[]{:S(2)}) copy-start(bf16[4,64,1024]{2,1,0:T(8,128)(2,1)S(1)} %collective-permute-done.7) | copy-start | bytes 1572868
  110.4 12.7 %copy-start.11 = (bf16[4,64,1024]{2,1,0:T(8,128)(2,1)}, bf16[4,64,1024]{2,1,0:T(8,128)(2,1)S(1)}, u32[]{:S(2)}) copy-start(bf16[4,64,1024]{2,1,0:T(8,128)(2,1)S(1)} %collective-permute-done.9) | copy-start | bytes 1572868
  121.7 11.2 %copy-start.10 = (bf16[4,64,1024]{2,1,0:T(8,128)(2,1)}, bf16[4,64,1024]{2,1,0:T(8,128)(2,1)S(1)}, u32[]{:S(2)}) copy-start(bf16[4,64,1024]{2,1,0:T(8,128)(2,1)S(1)} %collective-permute-done.11) | copy-start | bytes 1572868
  132.9 0.8 copy-start.9
  162.5 14.0 %copy-start.3 = (bf16[1024,512]{1,0:T(8,128)(2,1)S(1)}, bf16[1024,512]{1,0:T(8,128)(2,1)}, u32[]{:S(2)}) copy-start(bf16[1024,512]{1,0:T(8,128)(2,1)} %param.10) | copy-start | bytes 3145732
  162.5 14.0 %copy-start.16 = (bf16[4,64,1024]{2,1,0:T(8,128)(2,1)S(1)}, bf16[4,64,1024]{2,1,0:T(8,128)(2,1)}, u32[]{:S(2)}) copy-start(bf16[4,64,1024]{2,1,0:T(8,128)(2,1)} %copy-done.15) | copy-start | bytes 1572868
  171.9 11.3 %all-to-all-start = ((f32[8,8,4,128]{3,1,2,0:T(8,128)}), f32[8,8,4,128]{3,1,2,0:T(8,128)S(1)}, u32[]{:S(2)}, u32[]{:S(2)}) async-start(f32[8,8,4,128]{3,1,2,0:T(8,128)} %convolution_bitcast_fusion.2), calls=%async_computation | async-start | bytes 262144 | tf_op jit(solution)/shard_map/all_to_all | solution.py:119
  176.5 11.2 %copy-start.18 = (bf16[4,64,1024]{2,1,0:T(8,128)(2,1)S(1)}, bf16[4,64,1024]{2,1,0:T(8,128)(2,1)}, u32[]{:S(2)}) copy-start(bf16[4,64,1024]{2,1,0:T(8,128)(2,1)} %copy-done.17) | copy-start | bytes 1572868
  183.9 10.5 %all-to-all-start.1 = ((f32[8,8,4,128]{3,1,2,0:T(8,128)}), f32[8,8,4,128]{3,1,2,0:T(8,128)S(1)}, u32[]{:S(2)}, u32[]{:S(2)}) async-start(f32[8,8,4,128]{3,1,2,0:T(8,128)} %broadcast_in_dim.119), calls=%async_computation.1 | async-start | bytes 262144 | tf_op jit(solution)/shard_map/all_to_all | solution.py:124
  202.3 12.7 %copy-start.14 = (bf16[4,64,1024]{2,1,0:T(8,128)(2,1)S(1)}, bf16[4,64,1024]{2,1,0:T(8,128)(2,1)}, u32[]{:S(2)}) copy-start(bf16[4,64,1024]{2,1,0:T(8,128)(2,1)} %copy-done.13) | copy-start | bytes 1572868
  210.6 15.1 %copy-start.12 = (bf16[4,64,1024]{2,1,0:T(8,128)(2,1)S(1)}, bf16[4,64,1024]{2,1,0:T(8,128)(2,1)}, u32[]{:S(2)}) copy-start(bf16[4,64,1024]{2,1,0:T(8,128)(2,1)} %copy-done.11) | copy-start | bytes 1572868
  211.6 10.1 %all-to-all-start.2 = ((f32[8,8,4,128]{3,1,2,0:T(8,128)}), f32[8,8,4,128]{3,1,2,0:T(8,128)S(1)}, u32[]{:S(2)}, u32[]{:S(2)}) async-start(f32[8,8,4,128]{3,1,2,0:T(8,128)} %copy.168), calls=%async_computation.2 | async-start | bytes 262144 | tf_op jit(solution)/shard_map/all_to_all | solution.py:119
  222.3 10.1 %all-to-all-start.3 = ((f32[8,8,4,128]{3,1,2,0:T(8,128)}), f32[8,8,4,128]{3,1,2,0:T(8,128)S(1)}, u32[]{:S(2)}, u32[]{:S(2)}) async-start(f32[8,8,4,128]{3,1,2,0:T(8,128)} %broadcast_in_dim.120), calls=%async_computation.3 | async-start | bytes 262144 | tf_op jit(solution)/shard_map/all_to_all | solution.py:124
  240.3 12.7 %copy-start.8 = (bf16[4,64,1024]{2,1,0:T(8,128)(2,1)S(1)}, bf16[4,64,1024]{2,1,0:T(8,128)(2,1)}, u32[]{:S(2)}) copy-start(bf16[4,64,1024]{2,1,0:T(8,128)(2,1)} %copy-done.7) | copy-start | bytes 1572868
  248.6 15.4 %copy-start.6 = (bf16[4,64,1024]{2,1,0:T(8,128)(2,1)S(1)}, bf16[4,64,1024]{2,1,0:T(8,128)(2,1)}, u32[]{:S(2)}) copy-start(bf16[4,64,1024]{2,1,0:T(8,128)(2,1)} %copy-done.5) | copy-start | bytes 1572868
  249.6 10.1 %all-to-all-start.4 = ((f32[8,8,4,128]{3,1,2,0:T(8,128)}), f32[8,8,4,128]{3,1,2,0:T(8,128)S(1)}, u32[]{:S(2)}, u32[]{:S(2)}) async-start(f32[8,8,4,128]{3,1,2,0:T(8,128)} %copy.170), calls=%async_computation.4 | async-start | bytes 262144 | tf_op jit(solution)/shard_map/all_to_all | solution.py:119
  260.3 13.9 %all-to-all-start.5 = ((f32[8,8,4,128]{3,1,2,0:T(8,128)}), f32[8,8,4,128]{3,1,2,0:T(8,128)S(1)}, u32[]{:S(2)}, u32[]{:S(2)}) async-start(f32[8,8,4,128]{3,1,2,0:T(8,128)} %broadcast_in_dim.121), calls=%async_computation.5 | async-start | bytes 262144 | tf_op jit(solution)/shard_map/all_to_all | solution.py:124
  274.5 12.5 %copy-start.4 = (bf16[512,1024]{1,0:T(8,128)(2,1)S(1)}, bf16[512,1024]{1,0:T(8,128)(2,1)}, u32[]{:S(2)}) copy-start(bf16[512,1024]{1,0:T(8,128)(2,1)} %param.11) | copy-start | bytes 3145732
  287.1 30.2 %copy-start.1 = (bf16[1024,512]{1,0:T(8,128)(2,1)S(1)}, bf16[1024,512]{1,0:T(8,128)(2,1)}, u32[]{:S(2)}) copy-start(bf16[1024,512]{1,0:T(8,128)(2,1)} %param.9) | copy-start | bytes 3145732
  288.8 25.5 %collective-permute-start.14 = (bf16[1024,512]{1,0:T(8,128)(2,1)}, bf16[1024,512]{1,0:T(8,128)(2,1)}, u32[]{:S(2)}, u32[]{:S(2)}) collective-permute-start(bf16[1024,512]{1,0:T(8,128)(2,1)} %convolution_convert_fusion.1), channel_id=1, source_target_pairs={{0,2},{2,0},{1,3},{3,1},{4,6},{6,4},{5,7},{7,5},{8,10},{10,8},{9,1... | collective-permute-start | bytes 3145736 | tf_op jit(solution)/shard_map/ppermute | solution.py:147

commit v8 on v5

--- a/solution.py
+++ b/solution.py
@@ -1,6 +1,7 @@
 import jax
 import jax.numpy as jnp
 from jax import lax
+from jax.experimental import pallas as pl
 from jax.sharding import PartitionSpec as P
 
 HS = 128
@@ -9,6 +10,36 @@
 
 
 COLUMN_FLOOR = 0.1
+
+
+def round_kernel(score_ref, max_ref, valid_ref, column_ref, row_out, column_out):
+    exps = jnp.where(valid_ref[0] > 0, jnp.exp(score_ref[0, 0] - max_ref[0, 0]), 0.0)
+    column = column_ref[0, 0]
+    row = 1.0 / jnp.sum(exps * column, axis=1, keepdims=True)
+    row_out[0, 0] = row
+    column_out[0, 0] = column * jnp.sum(exps * row, axis=0, keepdims=True)
+
+
+def balance_round(scores, row_max, valid, column):
+    heads, blocks, rows, width = scores.shape
+    return pl.pallas_call(
+        round_kernel,
+        grid=(heads, blocks),
+        in_specs=[
+            pl.BlockSpec((1, 1, rows, width), lambda h, b: (h, b, 0, 0)),
+            pl.BlockSpec((1, 1, rows, 1), lambda h, b: (h, b, 0, 0)),
+            pl.BlockSpec((1, 1, width), lambda h, b: (b, 0, 0)),
+            pl.BlockSpec((1, 1, 1, width), lambda h, b: (h, b, 0, 0)),
+        ],
+        out_specs=[
+            pl.BlockSpec((1, 1, rows, 1), lambda h, b: (h, b, 0, 0)),
+            pl.BlockSpec((1, 1, 1, width), lambda h, b: (h, b, 0, 0)),
+        ],
+        out_shape=[
+            jax.ShapeDtypeStruct((heads, blocks, rows, 1), jnp.float32),
+            jax.ShapeDtypeStruct((heads, blocks, 1, width), jnp.float32),
+        ],
+    )(scores, row_max, valid, column)
 
 
 def body(activations, w_query, w_key, w_value, w_out, tile_lists, query_block_counts):
@@ -110,9 +141,21 @@
     weights = jnp.where(valid_mask, jnp.exp(scores - row_max), 0.0)
     column_scale = jnp.ones(weights.shape[:2] + weights.shape[3:], jnp.float32)
     onehot = matches.astype(jnp.float32)
+    slot_width = maximum_tiles * TILE
+    flat_scores = scores.reshape(heads_here, local_blocks, TILE, slot_width)
+    flat_max = row_max.reshape(heads_here, local_blocks, TILE, 1)
+    flat_valid = jnp.repeat(my_valid.astype(jnp.float32), TILE, axis=1).reshape(
+        local_blocks, 1, slot_width
+    )
     for round_number in range(BALANCING_ROUNDS):
-        row_scale = 1.0 / jnp.sum(weights * column_scale[:, :, None], axis=(3, 4))
-        partial_cols = column_scale * jnp.sum(weights * row_scale[:, :, :, None, None], axis=2)
+        row_out, column_out = balance_round(
+            flat_scores,
+            flat_max,
+            flat_valid,
+            column_scale.reshape(heads_here, local_blocks, 1, slot_width),
+        )
+        row_scale = row_out.reshape(heads_here, local_blocks, TILE)
+        partial_cols = column_out.reshape(heads_here, local_blocks, maximum_tiles, TILE)
         column_complete = jnp.einsum(
             "bmt,hbmj->thj", onehot, partial_cols, precision=lax.Precision.HIGHEST
         ).reshape(seq_devices, local_blocks, heads_here, TILE)

time: 309 us -> 366 us (1.18)
  Pallas kernels: 0 us -> 71.8 us
  other arithmetic: 44.9 us -> 4.86 us
  local copies, waits for them, and re-layouts: 38.7 us -> 54.9 us
  matrix products: 69 us -> 75.9 us
    pallas_call x0 -> x3, Pallas kernels: none -> 71.8 us  [balance_round(): pl.pallas_call(round_kernel, grid=(heads, blocks), in_specs=[pl.BlockSpec...]
    reduce_sum x6 -> x0, other arithmetic: 40.5 us -> none  [the longest x3 21.7 us: body(): jnp.sum(weights * row_scale[:, :, :, None, None], axis=2)]
    reshape x2, local copies, waits for them, and re-layouts: 1.33 us -> 17 us  [the longest x1 16.3 us: body(): flat_scores = scores.reshape(heads_here, local_blocks, TILE, slot_width)]
    dot_general x3, matrix products: 1.7 us -> 6.07 us  [body(): jnp.einsum('bmt,hbmj->thj', onehot, partial_cols, precision=lax.Precision...]
    dot_general x1, matrix products: 5.13 us -> 9.33 us  [body(): jnp.einsum('bihd,bmhjd->hbimj', query_blocks, key_slots, preferred_elemen...]
  transfers between devices with their start and end apart: 21 -> 21, of which waited for: 13 -> 13; matrix products, arithmetic and copies ran while one was open for 21% -> 17% of each run, Pallas kernels for 0% -> 0%
where the time goes in v8:
time: 366 us; the launch traced here: 362 us
  waiting for transfers between devices  115 us (31%)
  matrix products  75.9 us (21%)
  Pallas kernels  71.8 us (20%)
  local copies, waits for them, and re-layouts  54.9 us (15%)
  starting transfers between devices  40.1 us (11%)
  other arithmetic  4.86 us (1%)
    pallas_call x3, Pallas kernels, balance_round(): pl.pallas_call(round_kernel, grid=(heads, blocks), in_specs=[pl.BlockSpec...  71.8 us
    ppermute x7, waiting for transfers between devices, body(): got = lax.ppermute(piece, ('seq', 'sub'), perm=pairs)  40 us
    ppermute x7, waiting for transfers between devices, body(): partner = lax.ppermute(got, 'head', perm=[(0, 1), (1, 0)])  32.3 us
    ppermute x1, waiting for transfers between devices, body(): lax.ppermute(other_part.astype(jnp.bfloat16), 'head', perm=[(0, 1), (1, 0)])  24.2 us
    dot_general x8, matrix products, body(): jnp.einsum('cjf,fhd->chjd', full, value_weights, preferred_element_type=j...  19.7 us
    dot_general x8, matrix products, body(): jnp.einsum('cjf,fhd->chjd', full, key_weights, preferred_element_type=jnp...  18 us
    reshape x1, local copies, waits for them, and re-layouts, body(): flat_scores = scores.reshape(heads_here, local_blocks, TILE, slot_width)  16.3 us
    dot_general x1, matrix products, body(): jnp.einsum('hbimj,bmhjd->bihd', probabilities, value_slots, preferred_ele...  12 us
  transfers between devices with their start and end apart: 21, of which 13 were waited for; matrix products, arithmetic and copies ran while one was open for 17% of the time, Pallas kernels for 0%

profile of v8, /device:TPU:0, one launch (start us, length us, event | category | flops | bytes accessed | tf_op | source)
XLA Modules:
  0.0 362.5 jit_solution(1591742100736249120)
XLA Ops:
  2.5 1.8 constant_dynamic-slice_fusion.11
  7.6 2.6 collective-permute-start.2
  13.0 2.8 collective-permute-start.6
  18.3 4.1 %convolution_convert_fusion = bf16[1024,512]{1,0:T(8,128)(2,1)} fusion(bf16[1024,1024]{1,0:T(8,128)(2,1)} %param.7, bf16[1024,512]{1,0:T(8,128)(2,1)} %param.8), kind=kOutput, calls=%fused_computation.20 | convolution fusion | flops 1074266112 | bytes 4194304 | tf_op jit(solution)/shard_map/dot_general | solution.py:57
  28.2 2.2 gather_fusion
  33.6 9.0 %collective-permute-done.2 = bf16[4,64,1024]{2,1,0:T(8,128)(2,1)} collective-permute-done((bf16[4,64,1024]{2,1,0:T(8,128)(2,1)}, bf16[4,64,1024]{2,1,0:T(8,128)(2,1)}, u32[]{:S(2)}, u32[]{:S(2)}) %collective-permute-start.2) | collective-permute-done | bytes 524320 | tf_op jit(solution)/shard_map/ppermute | solution.py:114
  44.3 9.1 %collective-permute-done.4 = bf16[4,64,1024]{2,1,0:T(8,128)(2,1)} collective-permute-done((bf16[4,64,1024]{2,1,0:T(8,128)(2,1)}, bf16[4,64,1024]{2,1,0:T(8,128)(2,1)}, u32[]{:S(2)}, u32[]{:S(2)}) %collective-permute-start.4) | collective-permute-done | bytes 524320 | tf_op jit(solution)/shard_map/ppermute | solution.py:114
  56.3 2.7 fusion.14
  59.6 2.6 fusion.32
  62.2 21.9 %collective-permute-done.8 = bf16[4,64,1024]{2,1,0:T(8,128)(2,1)} collective-permute-done((bf16[4,64,1024]{2,1,0:T(8,128)(2,1)}, bf16[4,64,1024]{2,1,0:T(8,128)(2,1)}, u32[]{:S(2)}, u32[]{:S(2)}) %collective-permute-start.8) | collective-permute-done | bytes 524320 | tf_op jit(solution)/shard_map/ppermute | solution.py:114
  88.2 2.5 fusion.34
  90.8 2.7 fusion.36
  93.5 5.6 %collective-permute-done.7 = bf16[4,64,1024]{2,1,0:T(8,128)(2,1)S(1)} collective-permute-done((bf16[4,64,1024]{2,1,0:T(8,128)(2,1)}, bf16[4,64,1024]{2,1,0:T(8,128)(2,1)S(1)}, u32[]{:S(2)}, u32[]{:S(2)}) %collective-permute-start.7) | collective-permute-done | bytes 524320 | tf_op jit(solution)/shard_map/ppermute | solution.py:116
  99.1 2.8 fusion.38
  101.9 8.5 %collective-permute-done.9 = bf16[4,64,1024]{2,1,0:T(8,128)(2,1)S(1)} collective-permute-done((bf16[4,64,1024]{2,1,0:T(8,128)(2,1)}, bf16[4,64,1024]{2,1,0:T(8,128)(2,1)S(1)}, u32[]{:S(2)}, u32[]{:S(2)}) %collective-permute-start.9) | collective-permute-done | bytes 524320 | tf_op jit(solution)/shard_map/ppermute | solution.py:116
  110.3 2.8 fusion.40
  113.1 8.5 %collective-permute-done.11 = bf16[4,64,1024]{2,1,0:T(8,128)(2,1)S(1)} collective-permute-done((bf16[4,64,1024]{2,1,0:T(8,128)(2,1)S(1)}, bf16[4,64,1024]{2,1,0:T(8,128)(2,1)S(1)}, u32[]{:S(2)}, u32[]{:S(2)}) %collective-permute-start.11) | collective-permute-done | bytes 524320 | tf_op jit(solution)/shard_map/ppermute | solution.py:116
  123.1 9.7 %collective-permute-done.13 = bf16[4,64,1024]{2,1,0:T(8,128)(2,1)S(1)} collective-permute-done((bf16[4,64,1024]{2,1,0:T(8,128)(2,1)S(1)}, bf16[4,64,1024]{2,1,0:T(8,128)(2,1)S(1)}, u32[]{:S(2)}, u32[]{:S(2)}) %collective-permute-start.13) | collective-permute-done | bytes 524320 | tf_op jit(solution)/shard_map/ppermute | solution.py:116
  135.1 7.7 %gather_fusion.9 = bf16[64,4,128,128]{3,2,1,0:T(8,128)(2,1)} fusion(bf16[32,4,128,128]{3,2,1,0:T(8,128)(2,1)} %fusion.44, s32[1024]{0:T(1024)S(1)} %pad_clamp_fusion), kind=kCustom, calls=%fused_computation.9 | custom fusion | bytes 16777472 | tf_op jit(solution)/shard_map/jit(_take)/gather | solution.py:129
  142.8 9.3 %select_reduce_fusion = (f32[4,8,128]{2,1,0:T(8,128)S(1)}, f32[4,8,128,8,128]{2,4,3,1,0:T(8,128)}) fusion(pred[8,8]{1,0:T(8,128)(4,1)S(1)} %get-tuple-element.22, bf16[8,8,4,128,128]{4,3,2,1,0:T(8,128)(2,1)} %bitcast.320, bf16[8,128,4,128,1]{3,2,1,0,4:T(4,128)(2,1)S(1)} %bitcast.322), kind=kOutput, calls=%fused_computation.11 | convolution fusion | flops 1086320640 | bytes 26230848 | tf_op jit(solution)/shard_map/bihd,bmhjd->hbimj/dot_general | solution.py:136
  152.2 1.9 copy.180.max_ref
  154.1 16.3 %copy.208.score_ref = f32[4,8,128,1024]{3,2,1,0:T(8,128)} copy(f32[4,8,128,1024]{2,3,1,0:T(8,128)} %bitcast.318) | data formatting | bytes 33554432 | tf_op jit(solution)/shard_map/reshape | solution.py:145
  171.8 24.0 %shard_map.73 = (f32[4,8,128,1]{3,2,1,0:T(8,128)}, f32[4,8,1,1024]{3,2,1,0:T(1,128)}) custom-call(f32[4,8,128,1024]{3,2,1,0:T(8,128)} %copy.208.score_ref, f32[4,8,128,1]{3,2,1,0:T(8,128)} %copy.180.max_ref, f32[8,1,1024]{2,1,0:T(1,128)} %bitcast.325, f32[4,8,1,1024]{3,2,1,0:T(1,128)} %reshape.155.column_ref), custom_call_target="tpu_custom_call" | custom-call | tf_op jit(solution)/shard_map/pallas_call | solution.py:25
  195.8 2.0 convolution_bitcast_fusion.2
  197.8 4.8 %all-to-all-start = ((f32[8,8,4,128]{3,1,2,0:T(8,128)}), f32[8,8,4,128]{3,1,2,0:T(8,128)S(1)}, u32[]{:S(2)}, u32[]{:S(2)}) async-start(f32[8,8,4,128]{3,1,2,0:T(8,128)} %convolution_bitcast_fusion.2), calls=%async_computation | async-start | bytes 262144 | tf_op jit(solution)/shard_map/all_to_all | solution.py:162
  202.7 2.6 fusion.16
  205.3 2.5 fusion.18
  210.1 3.6 all-to-all-start.1
  213.6 2.6 fusion.20
  216.2 4.2 %all-to-all-done.1 = f32[8,8,4,128]{3,1,2,0:T(8,128)S(1)} async-done(((f32[8,8,4,128]{3,1,2,0:T(8,128)}), f32[8,8,4,128]{3,1,2,0:T(8,128)S(1)}, u32[]{:S(2)}, u32[]{:S(2)}) %all-to-all-start.1) | async-done | bytes 131104 | tf_op jit(solution)/shard_map/all_to_all | solution.py:167
  221.3 23.9 %shard_map.74 = (f32[4,8,128,1]{3,2,1,0:T(8,128)}, f32[4,8,1,1024]{3,2,1,0:T(1,128)}) custom-call(f32[4,8,128,1024]{3,2,1,0:T(8,128)} %copy.208.score_ref, f32[4,8,128,1]{3,2,1,0:T(8,128)} %copy.180.max_ref, f32[8,1,1024]{2,1,0:T(1,128)} %bitcast.326, f32[4,8,1,1024]{3,2,1,0:T(1,128)} %bitcast.329), custom_call_target="tpu_custom_call" | custom-call | tf_op jit(solution)/shard_map/pallas_call | solution.py:25
  245.2 2.0 convolution_bitcast_fusion.1
  247.2 3.4 all-to-all-start.2
  250.6 2.6 fusion.22
  253.2 4.1 %all-to-all-done.2 = f32[8,8,4,128]{3,1,2,0:T(8,128)S(1)} async-done(((f32[8,8,4,128]{3,1,2,0:T(8,128)}), f32[8,8,4,128]{3,1,2,0:T(8,128)S(1)}, u32[]{:S(2)}, u32[]{:S(2)}) %all-to-all-start.2) | async-done | bytes 131104 | tf_op jit(solution)/shard_map/all_to_all | solution.py:162
  258.0 3.4 all-to-all-start.3
  261.4 2.6 fusion.24
  263.9 4.1 %all-to-all-done.3 = f32[8,8,4,128]{3,1,2,0:T(8,128)S(1)} async-done(((f32[8,8,4,128]{3,1,2,0:T(8,128)}), f32[8,8,4,128]{3,1,2,0:T(8,128)S(1)}, u32[]{:S(2)}, u32[]{:S(2)}) %all-to-all-start.3) | async-done | bytes 131104 | tf_op jit(solution)/shard_map/all_to_all | solution.py:167
  268.9 23.9 %shard_map.75 = (f32[4,8,128,1]{3,2,1,0:T(8,128)}, f32[4,8,1,1024]{3,2,1,0:T(1,128)}) custom-call(f32[4,8,128,1024]{3,2,1,0:T(8,128)} %copy.208.score_ref, f32[4,8,128,1]{3,2,1,0:T(8,128)} %copy.180.max_ref, f32[8,1,1024]{2,1,0:T(1,128)} %bitcast.327, f32[4,8,1,1024]{3,2,1,0:T(1,128)} %bitcast.328), custom_call_target="tpu_custom_call" | custom-call | tf_op jit(solution)/shard_map/pallas_call | solution.py:25
  292.9 2.0 convolution_bitcast_fusion
  294.9 3.4 all-to-all-start.4
  298.3 2.5 fusion.26
  300.9 4.1 %all-to-all-done.4 = f32[8,8,4,128]{3,1,2,0:T(8,128)S(1)} async-done(((f32[8,8,4,128]{3,1,2,0:T(8,128)}), f32[8,8,4,128]{3,1,2,0:T(8,128)S(1)}, u32[]{:S(2)}, u32[]{:S(2)}) %all-to-all-start.4) | async-done | bytes 131104 | tf_op jit(solution)/shard_map/all_to_all | solution.py:162
  305.7 3.4 all-to-all-start.5
  310.6 7.8 %gather_fusion.8 = bf16[64,4,128,128]{3,2,1,0:T(8,128)(2,1)} fusion(bf16[32,4,128,128]{3,2,1,0:T(8,128)(2,1)} %fusion.28, s32[1024]{0:T(1024)S(1)} %pad_clamp_fusion), kind=kCustom, calls=%fused_computation.8 | custom fusion | bytes 16777472 | tf_op jit(solution)/shard_map/jit(_take)/gather | solution.py:132
  319.3 12.0 %fusion.8 = bf16[8,128,4,128]{1,3,2,0:T(8,128)(2,1)S(1)} fusion(bf16[8,8,4,128,128]{4,3,2,1,0:T(8,128)(2,1)} %bitcast.319, f32[4,8,128,8,128]{2,4,3,1,0:T(8,128)} %get-tuple-element.28, f32[4,8,8,128]{3,2,1,0:T(8,128)S(1)} %fusion.48, f32[4,8,128]{2,1,0:T(8,128)S(1)} %reduce.8, f32[4,8,128]{2,1,0:T(8,128)S(1)} %get-tuple-element.27, ...), kind=kOutput, calls=%fused_computation.22 | convolution fusion | flops 1095237632 | bytes 26378304 | tf_op jit(solution)/shard_map/hbimj,bmhjd->bihd/dot_general | solution.py:175
  335.3 24.2 %collective-permute-done.14 = bf16[1024,512]{1,0:T(8,128)(2,1)} collective-permute-done((bf16[1024,512]{1,0:T(8,128)(2,1)}, bf16[1024,512]{1,0:T(8,128)(2,1)}, u32[]{:S(2)}, u32[]{:S(2)}) %collective-permute-start.14) | collective-permute-done | bytes 1048608 | tf_op jit(solution)/shard_map/ppermute | solution.py:190
  359.5 3.0 add_convert_fusion
  (130 shorter events, 46.3 us)
Async XLA Ops:
  0.0 32.0 %copy-start = (bf16[1024,512]{1,0:T(8,128)(2,1)S(1)}, bf16[1024,512]{1,0:T(8,128)(2,1)}, u32[]{:S(2)}) copy-start(bf16[1024,512]{1,0:T(8,128)(2,1)} %param.9) | copy-start | bytes 3145732
  2.5 14.7 %copy-start.3 = (s32[64,8]{0,1:T(8,128)S(1)}, s32[64,8]{0,1:T(8,128)}, u32[]{:S(2)}) copy-start(s32[64,8]{0,1:T(8,128)} %param.12) | copy-start | bytes 6148
  5.7 24.8 %collective-permute-start = (bf16[4,64,1024]{2,1,0:T(8,128)(2,1)}, bf16[4,64,1024]{2,1,0:T(8,128)(2,1)}, u32[]{:S(2)}, u32[]{:S(2)}) collective-permute-start(bf16[4,64,1024]{2,1,0:T(8,128)(2,1)} %gather_fusion.1), channel_id=1, source_target_pairs={{0,1},{1,0},{4,5},{5,4},{8,9},{9,8},{12,13},{13,12},{2,3},{3,2},{6... | collective-permute-start | bytes 1572872 | tf_op jit(solution)/shard_map/ppermute | solution.py:114
  7.6 35.0 %collective-permute-start.2 = (bf16[4,64,1024]{2,1,0:T(8,128)(2,1)}, bf16[4,64,1024]{2,1,0:T(8,128)(2,1)}, u32[]{:S(2)}, u32[]{:S(2)}) collective-permute-start(bf16[4,64,1024]{2,1,0:T(8,128)(2,1)} %gather_fusion.2), channel_id=1, source_target_pairs={{0,4},{1,5},{4,0},{5,1},{8,12},{9,13},{12,8},{13,9},{2,6},{3,7},{6... | collective-permute-start | bytes 1572872 | tf_op jit(solution)/shard_map/ppermute | solution.py:114
  11.5 41.9 %collective-permute-start.4 = (bf16[4,64,1024]{2,1,0:T(8,128)(2,1)}, bf16[4,64,1024]{2,1,0:T(8,128)(2,1)}, u32[]{:S(2)}, u32[]{:S(2)}) collective-permute-start(bf16[4,64,1024]{2,1,0:T(8,128)(2,1)} %gather_fusion.3), channel_id=1, source_target_pairs={{0,5},{1,4},{4,1},{5,0},{8,13},{9,12},{12,9},{13,8},{2,7},{3,6},{6... | collective-permute-start | bytes 1572872 | tf_op jit(solution)/shard_map/ppermute | solution.py:114
  13.0 41.8 %collective-permute-start.6 = (bf16[4,64,1024]{2,1,0:T(8,128)(2,1)}, bf16[4,64,1024]{2,1,0:T(8,128)(2,1)}, u32[]{:S(2)}, u32[]{:S(2)}) collective-permute-start(bf16[4,64,1024]{2,1,0:T(8,128)(2,1)} %gather_fusion.4), channel_id=1, source_target_pairs={{0,8},{1,9},{4,12},{5,13},{8,0},{9,1},{12,4},{13,5},{2,10},{3,11},... | collective-permute-start | bytes 1572872 | tf_op jit(solution)/shard_map/ppermute | solution.py:114
  17.2 66.9 %collective-permute-start.8 = (bf16[4,64,1024]{2,1,0:T(8,128)(2,1)}, bf16[4,64,1024]{2,1,0:T(8,128)(2,1)}, u32[]{:S(2)}, u32[]{:S(2)}) collective-permute-start(bf16[4,64,1024]{2,1,0:T(8,128)(2,1)} %gather_fusion.5), channel_id=1, source_target_pairs={{0,9},{1,8},{4,13},{5,12},{8,1},{9,0},{12,5},{13,4},{2,11},{3,10},... | collective-permute-start | bytes 1572872 | tf_op jit(solution)/shard_map/ppermute | solution.py:114
  30.5 28.6 %collective-permute-start.1 = (bf16[4,64,1024]{2,1,0:T(8,128)(2,1)}, bf16[4,64,1024]{2,1,0:T(8,128)(2,1)S(1)}, u32[]{:S(2)}, u32[]{:S(2)}) collective-permute-start(bf16[4,64,1024]{2,1,0:T(8,128)(2,1)} %collective-permute-done), channel_id=1, source_target_pairs={{0,2},{2,0},{1,3},{3,1},{4,6},{6,4},{5,7},{7,5},{8,10},{10,8},{9,1... | collective-permute-start | bytes 1572872 | tf_op jit(solution)/shard_map/ppermute | solution.py:116
  42.6 43.0 %collective-permute-start.10 = (bf16[4,64,1024]{2,1,0:T(8,128)(2,1)}, bf16[4,64,1024]{2,1,0:T(8,128)(2,1)S(1)}, u32[]{:S(2)}, u32[]{:S(2)}) collective-permute-start(bf16[4,64,1024]{2,1,0:T(8,128)(2,1)} %gather_fusion.6), channel_id=1, source_target_pairs={{0,12},{1,13},{4,8},{5,9},{8,4},{9,5},{12,0},{13,1},{2,14},{3,15},... | collective-permute-start | bytes 1572872 | tf_op jit(solution)/shard_map/ppermute | solution.py:114
  53.4 32.7 %collective-permute-start.12 = (bf16[4,64,1024]{2,1,0:T(8,128)(2,1)}, bf16[4,64,1024]{2,1,0:T(8,128)(2,1)S(1)}, u32[]{:S(2)}, u32[]{:S(2)}) collective-permute-start(bf16[4,64,1024]{2,1,0:T(8,128)(2,1)} %gather_fusion.7), channel_id=1, source_target_pairs={{0,13},{1,12},{4,9},{5,8},{8,5},{9,4},{12,1},{13,0},{2,15},{3,14},... | collective-permute-start | bytes 1572872 | tf_op jit(solution)/shard_map/ppermute | solution.py:114
  54.8 32.8 %collective-permute-start.3 = (bf16[4,64,1024]{2,1,0:T(8,128)(2,1)}, bf16[4,64,1024]{2,1,0:T(8,128)(2,1)S(1)}, u32[]{:S(2)}, u32[]{:S(2)}) collective-permute-start(bf16[4,64,1024]{2,1,0:T(8,128)(2,1)} %collective-permute-done.2), channel_id=1, source_target_pairs={{0,2},{2,0},{1,3},{3,1},{4,6},{6,4},{5,7},{7,5},{8,10},{10,8},{9,1... | collective-permute-start | bytes 1572872 | tf_op jit(solution)/shard_map/ppermute | solution.py:116
  59.0 28.6 %copy-start.17 = (bf16[4,64,1024]{2,1,0:T(8,128)(2,1)}, bf16[4,64,1024]{2,1,0:T(8,128)(2,1)S(1)}, u32[]{:S(2)}) copy-start(bf16[4,64,1024]{2,1,0:T(8,128)(2,1)S(1)} %collective-permute-done.1) | copy-start | bytes 1572868
  59.0 31.8 %collective-permute-start.5 = (bf16[4,64,1024]{2,1,0:T(8,128)(2,1)}, bf16[4,64,1024]{2,1,0:T(8,128)(2,1)S(1)}, u32[]{:S(2)}, u32[]{:S(2)}) collective-permute-start(bf16[4,64,1024]{2,1,0:T(8,128)(2,1)} %collective-permute-done.4), channel_id=1, source_target_pairs={{0,2},{2,0},{1,3},{3,1},{4,6},{6,4},{5,7},{7,5},{8,10},{10,8},{9,1... | collective-permute-start | bytes 1572872 | tf_op jit(solution)/shard_map/ppermute | solution.py:116
  84.1 15.0 %collective-permute-start.7 = (bf16[4,64,1024]{2,1,0:T(8,128)(2,1)}, bf16[4,64,1024]{2,1,0:T(8,128)(2,1)S(1)}, u32[]{:S(2)}, u32[]{:S(2)}) collective-permute-start(bf16[4,64,1024]{2,1,0:T(8,128)(2,1)} %collective-permute-done.6), channel_id=1, source_target_pairs={{0,2},{2,0},{1,3},{3,1},{4,6},{6,4},{5,7},{7,5},{8,10},{10,8},{9,1... | collective-permute-start | bytes 1572872 | tf_op jit(solution)/shard_map/ppermute | solution.py:116
  85.5 36.0 %copy-start.8 = (bf16[4,64,1024]{2,1,0:T(8,128)(2,1)}, bf16[4,64,1024]{2,1,0:T(8,128)(2,1)S(1)}, u32[]{:S(2)}) copy-start(bf16[4,64,1024]{2,1,0:T(8,128)(2,1)S(1)} %collective-permute-done.10) | copy-start | bytes 1572868
  85.5 24.8 %collective-permute-start.9 = (bf16[4,64,1024]{2,1,0:T(8,128)(2,1)}, bf16[4,64,1024]{2,1,0:T(8,128)(2,1)S(1)}, u32[]{:S(2)}, u32[]{:S(2)}) collective-permute-start(bf16[4,64,1024]{2,1,0:T(8,128)(2,1)} %collective-permute-done.8), channel_id=1, source_target_pairs={{0,2},{2,0},{1,3},{3,1},{4,6},{6,4},{5,7},{7,5},{8,10},{10,8},{9,1... | collective-permute-start | bytes 1572872 | tf_op jit(solution)/shard_map/ppermute | solution.py:116
  86.1 46.7 %copy-start.6 = (bf16[4,64,1024]{2,1,0:T(8,128)(2,1)}, bf16[4,64,1024]{2,1,0:T(8,128)(2,1)S(1)}, u32[]{:S(2)}) copy-start(bf16[4,64,1024]{2,1,0:T(8,128)(2,1)S(1)} %collective-permute-done.12) | copy-start | bytes 1572868
  86.1 35.4 %collective-permute-start.11 = (bf16[4,64,1024]{2,1,0:T(8,128)(2,1)S(1)}, bf16[4,64,1024]{2,1,0:T(8,128)(2,1)S(1)}, u32[]{:S(2)}, u32[]{:S(2)}) collective-permute-start(bf16[4,64,1024]{2,1,0:T(8,128)(2,1)S(1)} %collective-permute-done.10), channel_id=1, source_target_pairs={{0,2},{2,0},{1,3},{3,1},{4,6},{6,4},{5,7},{7,5},{8,10},{10,8},{9,1... | collective-permute-start | bytes 1572872 | tf_op jit(solution)/shard_map/ppermute | solution.py:116
  87.6 5.9 %copy-start.21 = (bf16[4,64,1024]{2,1,0:T(8,128)(2,1)}, bf16[4,64,1024]{2,1,0:T(8,128)(2,1)S(1)}, u32[]{:S(2)}) copy-start(bf16[4,64,1024]{2,1,0:T(8,128)(2,1)S(1)} %collective-permute-done.3) | copy-start | bytes 1572868
  87.6 45.2 %collective-permute-start.13 = (bf16[4,64,1024]{2,1,0:T(8,128)(2,1)S(1)}, bf16[4,64,1024]{2,1,0:T(8,128)(2,1)S(1)}, u32[]{:S(2)}, u32[]{:S(2)}) collective-permute-start(bf16[4,64,1024]{2,1,0:T(8,128)(2,1)S(1)} %collective-permute-done.12), channel_id=1, source_target_pairs={{0,2},{2,0},{1,3},{3,1},{4,6},{6,4},{5,7},{7,5},{8,10},{10,8},{9,1... | collective-permute-start | bytes 1572872 | tf_op jit(solution)/shard_map/ppermute | solution.py:116
  90.8 11.1 %copy-start.19 = (bf16[4,64,1024]{2,1,0:T(8,128)(2,1)}, bf16[4,64,1024]{2,1,0:T(8,128)(2,1)S(1)}, u32[]{:S(2)}) copy-start(bf16[4,64,1024]{2,1,0:T(8,128)(2,1)S(1)} %collective-permute-done.5) | copy-start | bytes 1572868
  99.1 14.0 %copy-start.15 = (bf16[4,64,1024]{2,1,0:T(8,128)(2,1)}, bf16[4,64,1024]{2,1,0:T(8,128)(2,1)S(1)}, u32[]{:S(2)}) copy-start(bf16[4,64,1024]{2,1,0:T(8,128)(2,1)S(1)} %collective-permute-done.7) | copy-start | bytes 1572868
  110.3 12.7 %copy-start.13 = (bf16[4,64,1024]{2,1,0:T(8,128)(2,1)}, bf16[4,64,1024]{2,1,0:T(8,128)(2,1)S(1)}, u32[]{:S(2)}) copy-start(bf16[4,64,1024]{2,1,0:T(8,128)(2,1)S(1)} %collective-permute-done.9) | copy-start | bytes 1572868
  121.6 11.2 %copy-start.12 = (bf16[4,64,1024]{2,1,0:T(8,128)(2,1)}, bf16[4,64,1024]{2,1,0:T(8,128)(2,1)S(1)}, u32[]{:S(2)}) copy-start(bf16[4,64,1024]{2,1,0:T(8,128)(2,1)S(1)} %collective-permute-done.11) | copy-start | bytes 1572868
  132.8 0.8 copy-start.10
  171.8 30.8 %copy-start.4 = (bf16[1024,512]{1,0:T(8,128)(2,1)S(1)}, bf16[1024,512]{1,0:T(8,128)(2,1)}, u32[]{:S(2)}) copy-start(bf16[1024,512]{1,0:T(8,128)(2,1)} %param.10) | copy-start | bytes 3145732
  171.8 30.8 %copy-start.18 = (bf16[4,64,1024]{2,1,0:T(8,128)(2,1)S(1)}, bf16[4,64,1024]{2,1,0:T(8,128)(2,1)}, u32[]{:S(2)}) copy-start(bf16[4,64,1024]{2,1,0:T(8,128)(2,1)} %copy-done.17) | copy-start | bytes 1572868
  195.8 9.4 %copy-start.22 = (bf16[4,64,1024]{2,1,0:T(8,128)(2,1)S(1)}, bf16[4,64,1024]{2,1,0:T(8,128)(2,1)}, u32[]{:S(2)}) copy-start(bf16[4,64,1024]{2,1,0:T(8,128)(2,1)} %copy-done.21) | copy-start | bytes 1572868
  197.8 11.5 %all-to-all-start = ((f32[8,8,4,128]{3,1,2,0:T(8,128)}), f32[8,8,4,128]{3,1,2,0:T(8,128)S(1)}, u32[]{:S(2)}, u32[]{:S(2)}) async-start(f32[8,8,4,128]{3,1,2,0:T(8,128)} %convolution_bitcast_fusion.2), calls=%async_computation | async-start | bytes 262144 | tf_op jit(solution)/shard_map/all_to_all | solution.py:162
  202.6 11.0 %copy-start.20 = (bf16[4,64,1024]{2,1,0:T(8,128)(2,1)S(1)}, bf16[4,64,1024]{2,1,0:T(8,128)(2,1)}, u32[]{:S(2)}) copy-start(bf16[4,64,1024]{2,1,0:T(8,128)(2,1)} %copy-done.19) | copy-start | bytes 1572868
  210.1 10.3 %all-to-all-start.1 = ((f32[8,8,4,128]{3,1,2,0:T(8,128)}), f32[8,8,4,128]{3,1,2,0:T(8,128)S(1)}, u32[]{:S(2)}, u32[]{:S(2)}) async-start(f32[8,8,4,128]{3,1,2,0:T(8,128)} %broadcast_in_dim.117), calls=%async_computation.1 | async-start | bytes 262144 | tf_op jit(solution)/shard_map/all_to_all | solution.py:167
  221.3 29.3 %copy-start.16 = (bf16[4,64,1024]{2,1,0:T(8,128)(2,1)S(1)}, bf16[4,64,1024]{2,1,0:T(8,128)(2,1)}, u32[]{:S(2)}) copy-start(bf16[4,64,1024]{2,1,0:T(8,128)(2,1)} %copy-done.15) | copy-start | bytes 1572868
  245.2 16.1 %copy-start.14 = (bf16[4,64,1024]{2,1,0:T(8,128)(2,1)S(1)}, bf16[4,64,1024]{2,1,0:T(8,128)(2,1)}, u32[]{:S(2)}) copy-start(bf16[4,64,1024]{2,1,0:T(8,128)(2,1)} %copy-done.13) | copy-start | bytes 1572868
  247.2 10.1 %all-to-all-start.2 = ((f32[8,8,4,128]{3,1,2,0:T(8,128)}), f32[8,8,4,128]{3,1,2,0:T(8,128)S(1)}, u32[]{:S(2)}, u32[]{:S(2)}) async-start(f32[8,8,4,128]{3,1,2,0:T(8,128)} %convolution_bitcast_fusion.1), calls=%async_computation.2 | async-start | bytes 262144 | tf_op jit(solution)/shard_map/all_to_all | solution.py:162
  258.0 10.1 %all-to-all-start.3 = ((f32[8,8,4,128]{3,1,2,0:T(8,128)}), f32[8,8,4,128]{3,1,2,0:T(8,128)S(1)}, u32[]{:S(2)}, u32[]{:S(2)}) async-start(f32[8,8,4,128]{3,1,2,0:T(8,128)} %broadcast_in_dim.118), calls=%async_computation.3 | async-start | bytes 262144 | tf_op jit(solution)/shard_map/all_to_all | solution.py:167
  268.9 29.4 %copy-start.9 = (bf16[4,64,1024]{2,1,0:T(8,128)(2,1)S(1)}, bf16[4,64,1024]{2,1,0:T(8,128)(2,1)}, u32[]{:S(2)}) copy-start(bf16[4,64,1024]{2,1,0:T(8,128)(2,1)} %copy-done.8) | copy-start | bytes 1572868
  292.9 16.2 %copy-start.7 = (bf16[4,64,1024]{2,1,0:T(8,128)(2,1)S(1)}, bf16[4,64,1024]{2,1,0:T(8,128)(2,1)}, u32[]{:S(2)}) copy-start(bf16[4,64,1024]{2,1,0:T(8,128)(2,1)} %copy-done.6) | copy-start | bytes 1572868
  292.9 16.2 %copy-start.11 = (bf16[4,64,1024]{2,1,0:T(8,128)(2,1)S(1)}, bf16[4,64,1024]{2,1,0:T(8,128)(2,1)}, u32[]{:S(2)}) copy-start(bf16[4,64,1024]{2,1,0:T(8,128)(2,1)} %copy-done.10) | copy-start | bytes 1572868
  294.9 10.1 %all-to-all-start.4 = ((f32[8,8,4,128]{3,1,2,0:T(8,128)}), f32[8,8,4,128]{3,1,2,0:T(8,128)S(1)}, u32[]{:S(2)}, u32[]{:S(2)}) async-start(f32[8,8,4,128]{3,1,2,0:T(8,128)} %convolution_bitcast_fusion), calls=%async_computation.4 | async-start | bytes 262144 | tf_op jit(solution)/shard_map/all_to_all | solution.py:162
  305.7 13.4 %all-to-all-start.5 = ((f32[8,8,4,128]{3,1,2,0:T(8,128)}), f32[8,8,4,128]{3,1,2,0:T(8,128)S(1)}, u32[]{:S(2)}, u32[]{:S(2)}) async-start(f32[8,8,4,128]{3,1,2,0:T(8,128)} %broadcast_in_dim.119), calls=%async_computation.5 | async-start | bytes 262144 | tf_op jit(solution)/shard_map/all_to_all | solution.py:167
  310.6 7.8 %copy-start.2 = (f32[4,8,128,1]{3,2,1,0:T(8,128)S(1)}, f32[4,8,128,1]{3,2,1,0:T(8,128)}, u32[]{:S(2)}) copy-start(f32[4,8,128,1]{3,2,1,0:T(8,128)} %get-tuple-element.11) | copy-start | bytes 49156
  319.3 12.7 %copy-start.5 = (bf16[512,1024]{1,0:T(8,128)(2,1)S(1)}, bf16[512,1024]{1,0:T(8,128)(2,1)}, u32[]{:S(2)}) copy-start(bf16[512,1024]{1,0:T(8,128)(2,1)} %param.11) | copy-start | bytes 3145732
  332.0 30.4 %copy-start.1 = (bf16[1024,512]{1,0:T(8,128)(2,1)S(1)}, bf16[1024,512]{1,0:T(8,128)(2,1)}, u32[]{:S(2)}) copy-start(bf16[1024,512]{1,0:T(8,128)(2,1)} %param.9) | copy-start | bytes 3145732
  333.8 25.7 %collective-permute-start.14 = (bf16[1024,512]{1,0:T(8,128)(2,1)}, bf16[1024,512]{1,0:T(8,128)(2,1)}, u32[]{:S(2)}, u32[]{:S(2)}) collective-permute-start(bf16[1024,512]{1,0:T(8,128)(2,1)} %convolution_convert_fusion.1), channel_id=1, source_target_pairs={{0,2},{2,0},{1,3},{3,1},{4,6},{6,4},{5,7},{7,5},{8,10},{10,8},{9,1... | collective-permute-start | bytes 3145736 | tf_op jit(solution)/shard_map/ppermute | solution.py:190
